TPU v7x, 128 devices: a whole 4x4x4 slice. The times are simulated.
128 devices in a mesh: kv: 16 (over y, x), seq: 8 (over z, core).
Axes of the slice: x: 4, y: 4, z: 4, core: 2. Of those that a mesh axis runs over, the one named last changes fastest.
Arguments:
- prefill_keys: bfloat16 [262144, 1024], P(('kv', 'seq')), may hold values from -50 to 50
- queries: bfloat16 [1024, 8192], P('seq'), may hold values from -6 to 6
- outlier_spans: int32 [512], P(('kv', 'seq')), may hold values from 0 to 255
- start_basis: float32 [160, 1024], replicated, may hold values from -6 to 6
Outputs:
- basis: float32 [160, 1024], replicated
- coefficients: bfloat16 [160, 262144], P(None, ('kv', 'seq'))
- landmark_scores: bfloat16 [8, 1024, 32768], P(None, 'seq', 'kv')
- outlier_scores: bfloat16 [8, 1024, 4096], P(None, 'seq', 'kv')
Inputs may be any that keep to these rules, and one draw needn't show every extreme that they name: `outlier_spans`: entries index spans of 8 rows among the rows held by the same device.
All inputs are finite; a program needn't handle non-finite values.
Results may differ from a plain program's by a relative error of at most 0.0037.
Values may be sent and summed in bfloat16 or wider, within the bound.
No kernel may reach another device: no remote copies, remote signals or barrier semaphores. Data moves between devices by JAX's collectives and lax.ppermute only.
A program may use at most 128 MiB of HBM per device.

v0:
```python
import math

import jax
import jax.numpy as jnp
from jax import lax
from jax.sharding import PartitionSpec as P

KVH = 8
HEAD = 128
GROUP = 8
ITERS = 8
SPAN = 8


def moment_of(product):
    return jnp.dot(
        product, product.T, precision=lax.Precision.HIGHEST, preferred_element_type=jnp.float32
    )


def solve_lower(moment, product):
    return jax.scipy.linalg.solve_triangular(jnp.linalg.cholesky(moment), product, lower=True)


def apply_gram(subspace, gram_rows):
    return lax.dot_general(
        subspace,
        gram_rows,
        (((1,), (1,)), ((), ())),
        precision=lax.Precision.HIGHEST,
        preferred_element_type=jnp.float32,
    )


def local(prefill_keys, queries, outlier_spans, start_basis):
    rows_dev = prefill_keys.shape[0]
    width = prefill_keys.shape[1]
    inverse_tokens = 1.0 / (rows_dev * lax.axis_size("kv") * lax.axis_size("seq"))
    scale_factor = 1.0 / math.sqrt(HEAD)
    spanned = prefill_keys.reshape(rows_dev // SPAN, SPAN, width)
    landmarks = jnp.mean(spanned, axis=1, dtype=jnp.float32).astype(jnp.bfloat16)
    picked = jnp.take(spanned, outlier_spans, axis=0).reshape(-1, width)
    query_count = queries.shape[0]
    query_heads = jnp.transpose(queries.reshape(query_count, KVH, GROUP, HEAD), (1, 0, 2, 3))

    def score_rows(shard_rows):
        count_rows = shard_rows.shape[0]
        key_heads = jnp.swapaxes(shard_rows.reshape(count_rows, KVH, HEAD), 0, 1)

        def one_head(pairing):
            query_group, key_group = pairing
            scores = jnp.einsum(
                "qgd,cd->qgc", query_group, key_group, preferred_element_type=jnp.float32
            )
            return jnp.max(scores, axis=1)

        return (lax.map(one_head, (query_heads, key_heads)) * scale_factor).astype(jnp.bfloat16)

    landmark_scores = score_rows(lax.all_gather(landmarks, "seq", axis=0, tiled=True))
    outlier_scores = score_rows(lax.all_gather(picked, "seq", axis=0, tiled=True))
    subspace = start_basis
    gram_block = lax.psum_scatter(
        lax.dot_general(
            prefill_keys, prefill_keys, (((0,), (0,)), ((), ())), preferred_element_type=jnp.float32
        )
        * inverse_tokens,
        "kv",
        scatter_dimension=0,
        tiled=True,
    )
    gram_rows = lax.psum(gram_block, "seq")
    for iteration in range(ITERS):
        product = apply_gram(subspace, gram_rows)
        moment = lax.psum(moment_of(product), "kv")
        basis_piece = solve_lower(moment, product)
        subspace = lax.all_gather(basis_piece, "kv", axis=1, tiled=True)
    rounded = subspace.astype(jnp.bfloat16)
    coefficients = lax.dot_general(
        rounded, prefill_keys, (((1,), (1,)), ((), ())), preferred_element_type=jnp.float32
    ).astype(jnp.bfloat16)
    return (subspace, coefficients, landmark_scores, outlier_scores)


def solution(mesh):
    placed = (P(("kv", "seq"), None), P("seq", None), P(("kv", "seq")), P())
    return jax.shard_map(
        local,
        mesh=mesh,
        in_specs=placed,
        out_specs=(P(), P(None, ("kv", "seq")), P(None, "seq", "kv"), P(None, "seq", "kv")),
        check_vma=False,
    )
```

profile of v0, /device:TPU:1, one launch (start us, length us, event | category | flops | bytes accessed | tf_op | source)
XLA Modules:
  0.0 1427.7 jit_solution(11385063445946750643)
XLA Ops:
  7.2 10.1 convolution_multiply_fusion
  17.4 79.2 %reduce-scatter.2.cloned.1.call-done = f32[64,1024]{1,0:T(8,128)} async-done(((f32[1024,1024]{1,0:T(8,128)}), f32[64,1024]{1,0:T(8,128)}) %reduce-scatter.2.cloned.1.call-update) | async-done | bytes 262160 | tf_op jit(solution)/shard_map/reduce_scatter | solution.py:62
  96.6 61.4 %all-reduce.13.cloned.1.call-done = f32[64,1024]{1,0:T(8,128)} async-done(((f32[64,1024]{1,0:T(8,128)}), f32[64,1024]{1,0:T(8,128)}) %all-reduce.13.cloned.1.call-update) | async-done | bytes 262160 | tf_op jit(solution)/shard_map/psum | solution.py:71
  161.4 82.8 %all-reduce.15.cloned.1.call-done = f32[160,160]{0,1:T(8,128)} async-done(((f32[160,160]{0,1:T(8,128)}), f32[160,160]{0,1:T(8,128)}) %all-reduce.15.cloned.1.call-update) | async-done | bytes 102416 | tf_op jit(solution)/shard_map/psum | solution.py:74
  246.2 11.7 cholesky.412
  258.0 9.8 custom-call.25
  273.8 19.7 %custom-call.26 = f32[2,128,128]{1,2,0:T(8,128)S(1)} custom-call(f32[2,128,128]{2,1,0:T(8,128)S(1)} %pad_maximum_fusion), custom_call_target="InvertDiagBlocksLowerTriangular" | custom-call | tf_op jit(solution)/shard_map/jit(_solve_triangular)/triangular_solve | solution.py:22
  294.1 18.3 %all_gather.30 = f32[160,1024]{0,1:T(8,128)S(1)} all-gather(f32[160,64]{0,1:T(8,128)S(1)} %pad_maximum_fusion.8), channel_id=1, replica_groups=mesh['kv'=16,'seq'=8] {'kv'}, dimensions={1}, use_global_device_ids=true | all-gather | bytes 696320 | tf_op jit(solution)/shard_map/all_gather | solution.py:76
  314.4 87.4 %all-reduce.17.cloned.1.call-done = f32[160,160]{0,1:T(8,128)} async-done(((f32[160,160]{0,1:T(8,128)}), f32[160,160]{0,1:T(8,128)}) %all-reduce.17.cloned.1.call-update) | async-done | bytes 102416 | tf_op jit(solution)/shard_map/psum | solution.py:74
  403.7 11.7 cholesky.450
  415.5 9.8 custom-call.27
  431.3 19.7 %custom-call.28 = f32[2,128,128]{1,2,0:T(8,128)S(1)} custom-call(f32[2,128,128]{2,1,0:T(8,128)S(1)} %pad_maximum_fusion.1), custom_call_target="InvertDiagBlocksLowerTriangular" | custom-call | tf_op jit(solution)/shard_map/jit(_solve_triangular)/triangular_solve | solution.py:22
  451.5 18.3 %all_gather.31 = f32[160,1024]{0,1:T(8,128)S(1)} all-gather(f32[160,64]{0,1:T(8,128)S(1)} %pad_maximum_fusion.9), channel_id=1, replica_groups=mesh['kv'=16,'seq'=8] {'kv'}, dimensions={1}, use_global_device_ids=true | all-gather | bytes 696320 | tf_op jit(solution)/shard_map/all_gather | solution.py:76
  472.0 87.1 %all-reduce.19.cloned.1.call-done = f32[160,160]{0,1:T(8,128)} async-done(((f32[160,160]{0,1:T(8,128)}), f32[160,160]{0,1:T(8,128)}) %all-reduce.19.cloned.1.call-update) | async-done | bytes 102416 | tf_op jit(solution)/shard_map/psum | solution.py:74
  561.2 11.7 cholesky.488
  572.9 9.8 custom-call.29
  588.8 19.7 %custom-call.30 = f32[2,128,128]{1,2,0:T(8,128)S(1)} custom-call(f32[2,128,128]{2,1,0:T(8,128)S(1)} %pad_maximum_fusion.2), custom_call_target="InvertDiagBlocksLowerTriangular" | custom-call | tf_op jit(solution)/shard_map/jit(_solve_triangular)/triangular_solve | solution.py:22
  609.0 18.3 %all_gather.32 = f32[160,1024]{0,1:T(8,128)S(1)} all-gather(f32[160,64]{0,1:T(8,128)S(1)} %pad_maximum_fusion.10), channel_id=1, replica_groups=mesh['kv'=16,'seq'=8] {'kv'}, dimensions={1}, use_global_device_ids=true | all-gather | bytes 696320 | tf_op jit(solution)/shard_map/all_gather | solution.py:76
  634.7 81.9 %all-reduce.21.cloned.1.call-done = f32[160,160]{0,1:T(8,128)} async-done(((f32[160,160]{0,1:T(8,128)}), f32[160,160]{0,1:T(8,128)}) %all-reduce.21.cloned.1.call-update) | async-done | bytes 102416 | tf_op jit(solution)/shard_map/psum | solution.py:74
  718.6 11.7 cholesky.526
  730.4 9.8 custom-call.31
  746.2 19.7 %custom-call.32 = f32[2,128,128]{1,2,0:T(8,128)S(1)} custom-call(f32[2,128,128]{2,1,0:T(8,128)S(1)} %pad_maximum_fusion.3), custom_call_target="InvertDiagBlocksLowerTriangular" | custom-call | tf_op jit(solution)/shard_map/jit(_solve_triangular)/triangular_solve | solution.py:22
  766.5 18.3 %all_gather.33 = f32[160,1024]{0,1:T(8,128)S(1)} all-gather(f32[160,64]{0,1:T(8,128)S(1)} %pad_maximum_fusion.11), channel_id=1, replica_groups=mesh['kv'=16,'seq'=8] {'kv'}, dimensions={1}, use_global_device_ids=true | all-gather | bytes 696320 | tf_op jit(solution)/shard_map/all_gather | solution.py:76
  796.4 20.8 %all_gather.39 = bf16[256,1024]{1,0:T(8,128)(2,1)S(1)} all-gather(bf16[32,1024]{1,0:T(8,128)(2,1)S(1)} %bitcast_select_fusion), channel_id=1, replica_groups=mesh['kv'=16,'seq'=8] {'seq'}, dimensions={0}, use_global_device_ids=true | all-gather | bytes 589824 | tf_op jit(solution)/shard_map/all_gather | solution.py:60
  817.5 15.8 %while.30 = (s32[]{:T(128)}, f32[8,128,256]{2,1,0:T(8,128)}, bf16[8,128,8,128]{3,1,2,0:T(8,128)(2,1)}, bf16[8,256,128]{1,2,0:T(8,128)(2,1)S(1)}, s32[]{:T(128)}) while((s32[]{:T(128)}, f32[8,128,256]{2,1,0:T(8,128)}, bf16[8,128,8,128]{3,1,2,0:T(8,128)(2,1)}, bf16[8,256,128]{1,2,0:T(8,128)(2,1)S(1)}, s32[]{:T(128)}) %tuple.133), condition=%wide.region_20.23_spmd, body=%wide.region_18.22_spmd.sunk | while | flops 67338240 | bytes 722493 | solution.py:57
  833.2 40.9 %all-reduce.23.cloned.1.call-done = f32[160,160]{0,1:T(8,128)} async-done(((f32[160,160]{0,1:T(8,128)}), f32[160,160]{0,1:T(8,128)}) %all-reduce.23.cloned.1.call-update) | async-done | bytes 102416 | tf_op jit(solution)/shard_map/psum | solution.py:74
  876.1 11.7 cholesky.564
  887.9 9.8 custom-call.33
  903.7 19.7 %custom-call.34 = f32[2,128,128]{1,2,0:T(8,128)S(1)} custom-call(f32[2,128,128]{2,1,0:T(8,128)S(1)} %pad_maximum_fusion.4), custom_call_target="InvertDiagBlocksLowerTriangular" | custom-call | tf_op jit(solution)/shard_map/jit(_solve_triangular)/triangular_solve | solution.py:22
  923.9 18.3 %all_gather.34 = f32[160,1024]{0,1:T(8,128)S(1)} all-gather(f32[160,64]{0,1:T(8,128)S(1)} %pad_maximum_fusion.12), channel_id=1, replica_groups=mesh['kv'=16,'seq'=8] {'kv'}, dimensions={1}, use_global_device_ids=true | all-gather | bytes 696320 | tf_op jit(solution)/shard_map/all_gather | solution.py:76
  945.0 6.6 copy.121
  951.5 80.0 %all-reduce.25.cloned.1.call-done = f32[160,160]{0,1:T(8,128)} async-done(((f32[160,160]{0,1:T(8,128)}), f32[160,160]{0,1:T(8,128)}) %all-reduce.25.cloned.1.call-update) | async-done | bytes 102416 | tf_op jit(solution)/shard_map/psum | solution.py:74
  1033.6 11.7 cholesky.602
  1045.3 9.8 custom-call.35
  1061.2 19.7 %custom-call.36 = f32[2,128,128]{1,2,0:T(8,128)S(1)} custom-call(f32[2,128,128]{2,1,0:T(8,128)S(1)} %pad_maximum_fusion.5), custom_call_target="InvertDiagBlocksLowerTriangular" | custom-call | tf_op jit(solution)/shard_map/jit(_solve_triangular)/triangular_solve | solution.py:22
  1081.4 18.3 %all_gather.35 = f32[160,1024]{0,1:T(8,128)S(1)} all-gather(f32[160,64]{0,1:T(8,128)S(1)} %pad_maximum_fusion.13), channel_id=1, replica_groups=mesh['kv'=16,'seq'=8] {'kv'}, dimensions={1}, use_global_device_ids=true | all-gather | bytes 696320 | tf_op jit(solution)/shard_map/all_gather | solution.py:76
  1101.5 28.5 %while.29 = (s32[]{:T(128)}, f32[8,128,2048]{2,1,0:T(8,128)}, bf16[8,128,8,128]{3,1,2,0:T(8,128)(2,1)}, bf16[8,2048,128]{1,2,0:T(8,128)(2,1)}, s32[]{:T(128)}) while((s32[]{:T(128)}, f32[8,128,2048]{2,1,0:T(8,128)}, bf16[8,128,8,128]{3,1,2,0:T(8,128)(2,1)}, bf16[8,2048,128]{1,2,0:T(8,128)(2,1)}, s32[]{:T(128)}) %tuple.132), condition=%wide.region_17.20_spmd, body=%wide.region_15.19_spmd.sunk | while | flops 538705920 | bytes 3933757 | solution.py:57
  1130.0 59.0 %all-reduce.27.cloned.1.call-done = f32[160,160]{0,1:T(8,128)} async-done(((f32[160,160]{0,1:T(8,128)}), f32[160,160]{0,1:T(8,128)}) %all-reduce.27.cloned.1.call-update) | async-done | bytes 102416 | tf_op jit(solution)/shard_map/psum | solution.py:74
  1191.0 11.7 cholesky.640
  1202.8 9.8 custom-call.37
  1218.6 19.7 %custom-call.38 = f32[2,128,128]{1,2,0:T(8,128)S(1)} custom-call(f32[2,128,128]{2,1,0:T(8,128)S(1)} %pad_maximum_fusion.6), custom_call_target="InvertDiagBlocksLowerTriangular" | custom-call | tf_op jit(solution)/shard_map/jit(_solve_triangular)/triangular_solve | solution.py:22
  1238.9 18.5 %all_gather.36 = f32[160,1024]{0,1:T(8,128)S(1)} all-gather(f32[160,64]{0,1:T(8,128)S(1)} %pad_maximum_fusion.14), channel_id=1, replica_groups=mesh['kv'=16,'seq'=8] {'kv'}, dimensions={1}, use_global_device_ids=true | all-gather | bytes 696320 | tf_op jit(solution)/shard_map/all_gather | solution.py:76
  1259.2 6.6 multiply_convert_fusion
  1265.7 81.0 %all-reduce.29.cloned.1.call-done = f32[160,160]{0,1:T(8,128)} async-done(((f32[160,160]{0,1:T(8,128)}), f32[160,160]{0,1:T(8,128)}) %all-reduce.29.cloned.1.call-update) | async-done | bytes 102416 | tf_op jit(solution)/shard_map/psum | solution.py:74
  1348.7 11.7 cholesky.678
  1360.5 9.8 custom-call.39
  1376.4 19.7 %custom-call.40 = f32[2,128,128]{1,2,0:T(8,128)S(1)} custom-call(f32[2,128,128]{2,1,0:T(8,128)S(1)} %pad_maximum_fusion.7), custom_call_target="InvertDiagBlocksLowerTriangular" | custom-call | tf_op jit(solution)/shard_map/jit(_solve_triangular)/triangular_solve | solution.py:22
  1396.6 18.4 %all_gather.37 = f32[160,1024]{0,1:T(8,128)S(1)} all-gather(f32[160,64]{0,1:T(8,128)S(1)} %pad_maximum_fusion.15), channel_id=1, replica_groups=mesh['kv'=16,'seq'=8] {'kv'}, dimensions={1}, use_global_device_ids=true | all-gather | bytes 696320 | tf_op jit(solution)/shard_map/all_gather | solution.py:76
  (259 shorter events, 140.0 us)
Async XLA Ops:
  7.2 150.9 %copy-start = (f32[160,1024]{1,0:T(8,128)S(1)}, f32[160,1024]{1,0:T(8,128)}, u32[]{:S(2)}) copy-start(f32[160,1024]{1,0:T(8,128)} %param.14) | copy-start | bytes 1966084
  7.2 89.4 %reduce-scatter.2.cloned.1.call-start = ((), (), s32[]{:S(2)}) async-start(), calls=%async_computation.1 | async-start | bytes 4456448 | tf_op jit(solution)/shard_map/reduce_scatter | solution.py:62
  17.3 140.7 %all-reduce.13.cloned.1.call-start = ((), (), s32[]{:S(2)}) async-start(), calls=%async_computation.2 | async-start | bytes 524288 | tf_op jit(solution)/shard_map/psum | solution.py:71
  96.6 147.7 %all-reduce.15.cloned.1.call-start = ((), (), s32[]{:S(2)}) async-start(), calls=%async_computation.3 | async-start | bytes 327680 | tf_op jit(solution)/shard_map/psum | solution.py:74
  158.0 154.3 %copy-start.2 = (f32[64,1024]{1,0:T(8,128)S(1)}, f32[64,1024]{1,0:T(8,128)}, u32[]{:S(2)}) copy-start(f32[64,1024]{1,0:T(8,128)} %all-reduce.13.cloned.1.call-done) | copy-start | bytes 786436
  160.9 240.8 %all-reduce.17.cloned.1.call-start = ((), (), s32[]{:S(2)}) async-start(), calls=%async_computation.4 | async-start | bytes 327680 | tf_op jit(solution)/shard_map/psum | solution.py:74
  314.1 245.1 %all-reduce.19.cloned.1.call-start = ((), (), s32[]{:S(2)}) async-start(), calls=%async_computation.5 | async-start | bytes 327680 | tf_op jit(solution)/shard_map/psum | solution.py:74
  471.6 245.1 %all-reduce.21.cloned.1.call-start = ((), (), s32[]{:S(2)}) async-start(), calls=%async_computation.6 | async-start | bytes 327680 | tf_op jit(solution)/shard_map/psum | solution.py:74
  629.1 245.1 %all-reduce.23.cloned.1.call-start = ((), (), s32[]{:S(2)}) async-start(), calls=%async_computation.7 | async-start | bytes 327680 | tf_op jit(solution)/shard_map/psum | solution.py:74
  786.5 158.4 %all-gather.2.cloned.1.call-start = ((), (), s32[]{:S(2)}) async-start(), calls=%async_computation.11 | async-start | bytes 4718592 | tf_op jit(solution)/shard_map/all_gather | solution.py:59
  787.5 244.1 %all-reduce.25.cloned.1.call-start = ((), (), s32[]{:S(2)}) async-start(), calls=%async_computation.8 | async-start | bytes 327680 | tf_op jit(solution)/shard_map/psum | solution.py:74
  787.5 5.9 copy-start.4
  833.2 110.8 %copy-start.3 = (f32[8,128,256]{2,1,0:T(8,128)S(1)}, f32[8,128,256]{2,1,0:T(8,128)}, u32[]{:S(2)}) copy-start(f32[8,128,256]{2,1,0:T(8,128)} %get-tuple-element.51) | copy-start | bytes 3145732
  944.0 245.1 %all-reduce.27.cloned.1.call-start = ((), (), s32[]{:S(2)}) async-start(), calls=%async_computation.9 | async-start | bytes 327680 | tf_op jit(solution)/shard_map/psum | solution.py:74
  1101.5 245.3 %all-reduce.29.cloned.1.call-start = ((), (), s32[]{:S(2)}) async-start(), calls=%async_computation.10 | async-start | bytes 327680 | tf_op jit(solution)/shard_map/psum | solution.py:74
  1396.6 24.1 %copy-start.1 = (f32[160,1024]{1,0:T(8,128)S(1)}, f32[160,1024]{1,0:T(8,128)}, u32[]{:S(2)}) copy-start(f32[160,1024]{1,0:T(8,128)} %param.14) | copy-start | bytes 1966084
Sparse Core Ops, SparseCore 0:
  17.5 79.0 reduce-scatter.1
  99.0 59.0 all-reduce.12
  161.8 82.3 all-reduce.14
  314.2 87.4 all-reduce.16
  471.7 87.4 all-reduce.18
  629.2 87.4 all-reduce.20
  786.6 87.4 all-reduce.22
  876.4 33.6 all-gather.1
  944.1 87.4 all-reduce.24
  1101.6 87.4 all-reduce.26
  1259.3 87.4 all-reduce.28
where the time goes:
time: 1440 us; the launch traced here: 1430 us
  waiting for transfers between devices  741 us (51%)
  other arithmetic  386 us (27%)
  blocking collectives  167 us (12%)
  matrix products  65.8 us (5%)
  local copies, waits for them, and re-layouts  39.1 us (3%)
  between operations  25.9 us (2%)
    psum x8, waiting for transfers between devices, local(): moment = lax.psum(moment_of(product), 'kv')  600 us
    another operation x56, other arithmetic, solve_lower(): jnp.linalg.cholesky(moment)  206 us
    another operation x42, other arithmetic, solve_lower(): jax.scipy.linalg.solve_triangular(jnp.linalg.cholesky(moment), product, l...  158 us
    all_gather x8, blocking collectives, local(): subspace = lax.all_gather(basis_piece, 'kv', axis=1, tiled=True)  147 us
    reduce_scatter x1, waiting for transfers between devices, local(): lax.psum_scatter(lax.dot_general(prefill_keys, prefill_keys, (((0,), (0,)...  79.2 us
    psum x1, waiting for transfers between devices, local(): gram_rows = lax.psum(gram_block, 'seq')  61.4 us
    dot_general x16, matrix products, one_head(): jnp.einsum('qgd,cd->qgc', query_group, key_group, preferred_element_type=...  29.6 us
  transfers between devices with their start and end apart: 11, of which 10 were waited for; matrix products, arithmetic and copies ran while one was open for 9% of the time, Pallas kernels for 0%

commit v1 on v0

--- a/solution.py
+++ b/solution.py
@@ -22,13 +22,9 @@
     return jax.scipy.linalg.solve_triangular(jnp.linalg.cholesky(moment), product, lower=True)
 
 
-def apply_gram(subspace, gram_rows):
-    return lax.dot_general(
-        subspace,
-        gram_rows,
-        (((1,), (1,)), ((), ())),
-        precision=lax.Precision.HIGHEST,
-        preferred_element_type=jnp.float32,
+def apply_gram(subspace, gram):
+    return jnp.dot(
+        subspace, gram, precision=lax.Precision.HIGHEST, preferred_element_type=jnp.float32
     )
 
 
@@ -58,22 +54,16 @@
 
     landmark_scores = score_rows(lax.all_gather(landmarks, "seq", axis=0, tiled=True))
     outlier_scores = score_rows(lax.all_gather(picked, "seq", axis=0, tiled=True))
-    subspace = start_basis
-    gram_block = lax.psum_scatter(
+    gram = lax.psum(
         lax.dot_general(
             prefill_keys, prefill_keys, (((0,), (0,)), ((), ())), preferred_element_type=jnp.float32
-        )
-        * inverse_tokens,
-        "kv",
-        scatter_dimension=0,
-        tiled=True,
-    )
-    gram_rows = lax.psum(gram_block, "seq")
+        ),
+        ("kv", "seq"),
+    ) * inverse_tokens
+    subspace = start_basis
     for iteration in range(ITERS):
-        product = apply_gram(subspace, gram_rows)
-        moment = lax.psum(moment_of(product), "kv")
-        basis_piece = solve_lower(moment, product)
-        subspace = lax.all_gather(basis_piece, "kv", axis=1, tiled=True)
+        product = apply_gram(subspace, gram)
+        subspace = solve_lower(moment_of(product), product)
     rounded = subspace.astype(jnp.bfloat16)
     coefficients = lax.dot_general(
         rounded, prefill_keys, (((1,), (1,)), ((), ())), preferred_element_type=jnp.float32

time: 1440 us -> 689 us (0.48)
  waiting for transfers between devices: 741 us -> 121 us
  blocking collectives: 167 us -> 16.7 us
  matrix products: 65.8 us -> 103 us
    psum x9 -> x1, waiting for transfers between devices: 662 us -> 121 us  [local(): lax.psum(lax.dot_general(prefill_keys, prefill_keys, (((0,), (0,)), ((),...]
    all_gather x8 -> x0, blocking collectives: 147 us -> none  [local(): subspace = lax.all_gather(basis_piece, 'kv', axis=1, tiled=True)]
    reduce_scatter x1 -> x0, waiting for transfers between devices: 79.2 us -> none  [local(): lax.psum_scatter(lax.dot_general(prefill_keys, prefill_keys, (((0,), (0,)...]
    dot_general x8, matrix products: 6.91 us -> 39.8 us  [apply_gram(): jnp.dot(subspace, gram, precision=lax.Precision.HIGHEST, preferred_elemen...]
    another operation x42 -> x35, other arithmetic: 158 us -> 161 us  [solve_lower(): jax.scipy.linalg.solve_triangular(jnp.linalg.cholesky(moment), product, l...]
  transfers between devices with their start and end apart: 11 -> 2, of which waited for: 10 -> 1; matrix products, arithmetic and copies ran while one was open for 9% -> 68% of each run, Pallas kernels for 0% -> 0%
where the time goes in v1:
time: 689 us; the launch traced here: 682 us
  other arithmetic  382 us (55%)
  waiting for transfers between devices  121 us (18%)
  matrix products  103 us (15%)
  local copies, waits for them, and re-layouts  30.4 us (4%)
  between operations  27.6 us (4%)
  blocking collectives  16.7 us (2%)
    another operation x56, other arithmetic, solve_lower(): jnp.linalg.cholesky(moment)  206 us
    another operation x35, other arithmetic, solve_lower(): jax.scipy.linalg.solve_triangular(jnp.linalg.cholesky(moment), product, l...  161 us
    psum x1, waiting for transfers between devices, local(): lax.psum(lax.dot_general(prefill_keys, prefill_keys, (((0,), (0,)), ((),...  121 us
    dot_general x8, matrix products, apply_gram(): jnp.dot(subspace, gram, precision=lax.Precision.HIGHEST, preferred_elemen...  39.8 us
    dot_general x16, matrix products, one_head(): jnp.einsum('qgd,cd->qgc', query_group, key_group, preferred_element_type=...  29.6 us
    all_gather x1, blocking collectives, local(): lax.all_gather(picked, 'seq', axis=0, tiled=True)  16.7 us
    dynamic_update_slice x16, local copies, waits for them, and re-layouts, score_rows(): lax.map(one_head, (query_heads, key_heads)) * scale_factor  13.9 us
  transfers between devices with their start and end apart: 2, of which 1 were waited for; matrix products, arithmetic and copies ran while one was open for 68% of the time, Pallas kernels for 0%

profile of v1, /device:TPU:1, one launch (start us, length us, event | category | flops | bytes accessed | tf_op | source)
XLA Modules:
  0.0 681.7 jit_solution(4986286330486133360)
XLA Ops:
  8.1 10.1 %fusion.157 = f32[1024,1024]{1,0:T(8,128)} fusion(bf16[2048,1024]{1,0:T(8,128)(2,1)} %param.11), kind=kOutput, calls=%fused_computation.300 | convolution fusion | flops 4294967296 | bytes 8388608 | tf_op jit(solution)/shard_map/dot_general | solution.py:58
  18.2 5.5 convert_reduce_fusion
  24.7 3.2 copy.51
  33.5 16.7 %all_gather.7 = bf16[256,1024]{1,0:T(8,128)(2,1)S(1)} all-gather(bf16[32,1024]{1,0:T(8,128)(2,1)S(1)} %bitcast_select_fusion), channel_id=1, replica_groups=mesh['kv'=16,'seq'=8] {'seq'}, dimensions={0}, use_global_device_ids=true | all-gather | bytes 589824 | tf_op jit(solution)/shard_map/all_gather | solution.py:56
  50.4 15.4 %while.30 = (s32[]{:T(128)}, f32[8,128,256]{2,1,0:T(8,128)}, bf16[8,128,8,128]{3,1,2,0:T(8,128)(2,1)}, bf16[8,256,128]{1,2,0:T(8,128)(2,1)S(1)}, s32[]{:T(128)}) while((s32[]{:T(128)}, f32[8,128,256]{2,1,0:T(8,128)}, bf16[8,128,8,128]{3,1,2,0:T(8,128)(2,1)}, bf16[8,256,128]{1,2,0:T(8,128)(2,1)S(1)}, s32[]{:T(128)}) %tuple.111), condition=%wide.region_11.14_spmd, body=%wide.region_9.13_spmd.sunk | while | flops 67338240 | bytes 722493 | solution.py:53
  68.0 121.4 %all-reduce.5.cloned.1.call-done = f32[1024,1024]{1,0:T(8,128)} async-done(((f32[1024,1024]{1,0:T(8,128)}), f32[1024,1024]{1,0:T(8,128)}) %all-reduce.5.cloned.1.call-update) | async-done | bytes 4194320 | tf_op jit(solution)/shard_map/psum | solution.py:57
  189.4 5.0 fusion.24
  195.2 11.7 %cholesky.412 = f32[128,128]{1,0:T(8,128)S(1)} custom-call(f32[128,128]{1,0:T(8,128)S(1)} %cholesky.712), custom_call_target="Cholesky" | custom-call | tf_op jit(solution)/shard_map/jit(cholesky)/cholesky | solution.py:22
  207.0 9.8 %custom-call.25 = f32[1,128,128]{1,2,0:T(8,128)S(1)} custom-call(f32[1,128,128]{2,1,0:T(8,128)S(1)} %get-tuple-element.169), custom_call_target="InvertDiagBlocksLowerTriangular" | custom-call | tf_op jit(solution)/shard_map/jit(cholesky)/cholesky | solution.py:22
  217.1 2.9 cholesky.432
  222.8 20.1 %custom-call.26 = f32[2,128,128]{1,2,0:T(8,128)S(1)} custom-call(f32[2,128,128]{2,1,0:T(8,128)S(1)} %pad_maximum_fusion.1), custom_call_target="InvertDiagBlocksLowerTriangular" | custom-call | tf_op jit(solution)/shard_map/jit(_solve_triangular)/triangular_solve | solution.py:22
  244.3 5.0 fusion.22
  250.2 11.7 %cholesky.450 = f32[128,128]{1,0:T(8,128)S(1)} custom-call(f32[128,128]{1,0:T(8,128)S(1)} %cholesky.715), custom_call_target="Cholesky" | custom-call | tf_op jit(solution)/shard_map/jit(cholesky)/cholesky | solution.py:22
  261.9 9.8 %custom-call.27 = f32[1,128,128]{1,2,0:T(8,128)S(1)} custom-call(f32[1,128,128]{2,1,0:T(8,128)S(1)} %get-tuple-element.167), custom_call_target="InvertDiagBlocksLowerTriangular" | custom-call | tf_op jit(solution)/shard_map/jit(cholesky)/cholesky | solution.py:22
  272.1 2.9 cholesky.470
  277.8 19.9 %custom-call.28 = f32[2,128,128]{1,2,0:T(8,128)S(1)} custom-call(f32[2,128,128]{2,1,0:T(8,128)S(1)} %pad_maximum_fusion.2), custom_call_target="InvertDiagBlocksLowerTriangular" | custom-call | tf_op jit(solution)/shard_map/jit(_solve_triangular)/triangular_solve | solution.py:22
  299.0 5.0 fusion.20
  304.8 11.7 %cholesky.488 = f32[128,128]{1,0:T(8,128)S(1)} custom-call(f32[128,128]{1,0:T(8,128)S(1)} %cholesky.718), custom_call_target="Cholesky" | custom-call | tf_op jit(solution)/shard_map/jit(cholesky)/cholesky | solution.py:22
  316.6 9.8 %custom-call.29 = f32[1,128,128]{1,2,0:T(8,128)S(1)} custom-call(f32[1,128,128]{2,1,0:T(8,128)S(1)} %get-tuple-element.165), custom_call_target="InvertDiagBlocksLowerTriangular" | custom-call | tf_op jit(solution)/shard_map/jit(cholesky)/cholesky | solution.py:22
  326.8 2.9 cholesky.508
  332.4 20.1 %custom-call.30 = f32[2,128,128]{1,2,0:T(8,128)S(1)} custom-call(f32[2,128,128]{2,1,0:T(8,128)S(1)} %pad_maximum_fusion.3), custom_call_target="InvertDiagBlocksLowerTriangular" | custom-call | tf_op jit(solution)/shard_map/jit(_solve_triangular)/triangular_solve | solution.py:22
  353.9 5.0 fusion.18
  359.7 11.7 %cholesky.526 = f32[128,128]{1,0:T(8,128)S(1)} custom-call(f32[128,128]{1,0:T(8,128)S(1)} %cholesky.721), custom_call_target="Cholesky" | custom-call | tf_op jit(solution)/shard_map/jit(cholesky)/cholesky | solution.py:22
  371.5 9.8 %custom-call.31 = f32[1,128,128]{1,2,0:T(8,128)S(1)} custom-call(f32[1,128,128]{2,1,0:T(8,128)S(1)} %get-tuple-element.163), custom_call_target="InvertDiagBlocksLowerTriangular" | custom-call | tf_op jit(solution)/shard_map/jit(cholesky)/cholesky | solution.py:22
  387.3 19.9 %custom-call.32 = f32[2,128,128]{1,2,0:T(8,128)S(1)} custom-call(f32[2,128,128]{2,1,0:T(8,128)S(1)} %pad_maximum_fusion.4), custom_call_target="InvertDiagBlocksLowerTriangular" | custom-call | tf_op jit(solution)/shard_map/jit(_solve_triangular)/triangular_solve | solution.py:22
  408.6 5.0 fusion.16
  414.4 11.7 %cholesky.564 = f32[128,128]{1,0:T(8,128)S(1)} custom-call(f32[128,128]{1,0:T(8,128)S(1)} %cholesky.724), custom_call_target="Cholesky" | custom-call | tf_op jit(solution)/shard_map/jit(cholesky)/cholesky | solution.py:22
  426.2 9.8 %custom-call.33 = f32[1,128,128]{1,2,0:T(8,128)S(1)} custom-call(f32[1,128,128]{2,1,0:T(8,128)S(1)} %get-tuple-element.161), custom_call_target="InvertDiagBlocksLowerTriangular" | custom-call | tf_op jit(solution)/shard_map/jit(cholesky)/cholesky | solution.py:22
  436.3 2.9 cholesky.584
  442.0 20.1 %custom-call.34 = f32[2,128,128]{1,2,0:T(8,128)S(1)} custom-call(f32[2,128,128]{2,1,0:T(8,128)S(1)} %pad_maximum_fusion.5), custom_call_target="InvertDiagBlocksLowerTriangular" | custom-call | tf_op jit(solution)/shard_map/jit(_solve_triangular)/triangular_solve | solution.py:22
  463.5 5.0 fusion.14
  469.3 11.7 %cholesky.602 = f32[128,128]{1,0:T(8,128)S(1)} custom-call(f32[128,128]{1,0:T(8,128)S(1)} %cholesky.727), custom_call_target="Cholesky" | custom-call | tf_op jit(solution)/shard_map/jit(cholesky)/cholesky | solution.py:22
  481.1 9.8 %custom-call.35 = f32[1,128,128]{1,2,0:T(8,128)S(1)} custom-call(f32[1,128,128]{2,1,0:T(8,128)S(1)} %get-tuple-element.159), custom_call_target="InvertDiagBlocksLowerTriangular" | custom-call | tf_op jit(solution)/shard_map/jit(cholesky)/cholesky | solution.py:22
  496.9 19.8 %custom-call.36 = f32[2,128,128]{1,2,0:T(8,128)S(1)} custom-call(f32[2,128,128]{2,1,0:T(8,128)S(1)} %pad_maximum_fusion.6), custom_call_target="InvertDiagBlocksLowerTriangular" | custom-call | tf_op jit(solution)/shard_map/jit(_solve_triangular)/triangular_solve | solution.py:22
  518.1 5.0 fusion.12
  524.0 11.7 %cholesky.640 = f32[128,128]{1,0:T(8,128)S(1)} custom-call(f32[128,128]{1,0:T(8,128)S(1)} %cholesky.730), custom_call_target="Cholesky" | custom-call | tf_op jit(solution)/shard_map/jit(cholesky)/cholesky | solution.py:22
  535.7 9.8 %custom-call.37 = f32[1,128,128]{1,2,0:T(8,128)S(1)} custom-call(f32[1,128,128]{2,1,0:T(8,128)S(1)} %get-tuple-element.157), custom_call_target="InvertDiagBlocksLowerTriangular" | custom-call | tf_op jit(solution)/shard_map/jit(cholesky)/cholesky | solution.py:22
  545.9 2.9 cholesky.660
  551.6 19.9 %custom-call.38 = f32[2,128,128]{1,2,0:T(8,128)S(1)} custom-call(f32[2,128,128]{2,1,0:T(8,128)S(1)} %pad_maximum_fusion.7), custom_call_target="InvertDiagBlocksLowerTriangular" | custom-call | tf_op jit(solution)/shard_map/jit(_solve_triangular)/triangular_solve | solution.py:22
  572.8 5.0 fusion.10
  578.6 11.7 %cholesky.678 = f32[128,128]{1,0:T(8,128)S(1)} custom-call(f32[128,128]{1,0:T(8,128)S(1)} %cholesky.733), custom_call_target="Cholesky" | custom-call | tf_op jit(solution)/shard_map/jit(cholesky)/cholesky | solution.py:22
  590.4 9.8 %custom-call.39 = f32[1,128,128]{1,2,0:T(8,128)S(1)} custom-call(f32[1,128,128]{2,1,0:T(8,128)S(1)} %get-tuple-element.155), custom_call_target="InvertDiagBlocksLowerTriangular" | custom-call | tf_op jit(solution)/shard_map/jit(cholesky)/cholesky | solution.py:22
  600.6 2.9 cholesky.698
  606.3 19.9 %custom-call.40 = f32[2,128,128]{1,2,0:T(8,128)S(1)} custom-call(f32[2,128,128]{2,1,0:T(8,128)S(1)} %pad_maximum_fusion.8), custom_call_target="InvertDiagBlocksLowerTriangular" | custom-call | tf_op jit(solution)/shard_map/jit(_solve_triangular)/triangular_solve | solution.py:22
  627.6 4.8 convolution_convert_fusion
  632.4 6.4 copy.52
  638.8 28.3 %while.29 = (s32[]{:T(128)}, f32[8,128,2048]{2,1,0:T(8,128)}, bf16[8,128,8,128]{3,1,2,0:T(8,128)(2,1)}, bf16[8,2048,128]{1,2,0:T(8,128)(2,1)}, s32[]{:T(128)}) while((s32[]{:T(128)}, f32[8,128,2048]{2,1,0:T(8,128)}, bf16[8,128,8,128]{3,1,2,0:T(8,128)(2,1)}, bf16[8,2048,128]{1,2,0:T(8,128)(2,1)}, s32[]{:T(128)}) %tuple.110), condition=%wide.region_8.11_spmd, body=%wide.region_6.10_spmd.sunk | while | flops 538705920 | bytes 3933757 | solution.py:53
  667.1 6.6 multiply_convert_fusion
  (214 shorter events, 90.1 us)
Async XLA Ops:
  8.0 181.4 %copy-start = (f32[160,1024]{1,0:T(8,128)S(1)}, f32[160,1024]{1,0:T(8,128)}, u32[]{:S(2)}) copy-start(f32[160,1024]{1,0:T(8,128)} %param.14) | copy-start | bytes 1966084
  8.0 181.4 %all-reduce.5.cloned.1.call-start = ((), (), s32[]{:S(2)}) async-start(), calls=%async_computation | async-start | bytes 8388608 | tf_op jit(solution)/shard_map/psum | solution.py:57
  18.2 6.5 copy-start.3
  18.2 614.2 %all-gather.2.cloned.1.call-start = ((), (), s32[]{:S(2)}) async-start(), calls=%async_computation.1 | async-start | bytes 4718592 | tf_op jit(solution)/shard_map/all_gather | solution.py:55
  627.6 11.2 %copy-start.2 = (f32[160,1024]{1,0:T(8,128)}, f32[160,1024]{1,0:T(8,128)S(1)}, u32[]{:S(2)}) copy-start(f32[160,1024]{1,0:T(8,128)S(1)} %pad_maximum_fusion) | copy-start | bytes 1966084
  667.1 6.6 copy-start.1
Sparse Core Ops, SparseCore 0:
  18.3 171.0 all-reduce.4
Sparse Core Ops, SparseCore 1:
  24.7 40.1 all-gather.1

commit v2 on v1

--- a/solution.py
+++ b/solution.py
@@ -3,7 +3,10 @@
 import jax
 import jax.numpy as jnp
 from jax import lax
+from jax.experimental import pallas as pl
 from jax.sharding import PartitionSpec as P
+
+HI = lax.Precision.HIGHEST
 
 KVH = 8
 HEAD = 128
@@ -18,8 +21,41 @@
     )
 
 
+def _mm(a, b):
+    return jnp.dot(a, b, precision=HI, preferred_element_type=jnp.float32)
+
+def _mm_nt(a, b):
+    return lax.dot_general(a, b, (((1,), (1,)), ((), ())), precision=HI,
+                           preferred_element_type=jnp.float32)
+
+def _eliminate(a):
+    n = a.shape[0]
+    rows = lax.broadcasted_iota(jnp.int32, (n, 1), 0)
+    eye = lax.broadcasted_iota(jnp.int32, (n, n), 0) == lax.broadcasted_iota(jnp.int32, (n, n), 1)
+    e = eye.astype(jnp.float32)
+    for j in range(n):
+        inv = 1.0 / a[j:j + 1, j:j + 1]
+        f = jnp.where(rows > j, a[:, j:j + 1] * inv, 0.0)
+        a = a - f * a[j:j + 1, :]
+        e = e - f * e[j:j + 1, :]
+    diag = jnp.where(eye, a, 0.0)
+    return e, jnp.sum(diag, axis=1, keepdims=True), jnp.sum(diag, axis=0, keepdims=True)
+
+def _cholqr_kernel(m_ref, p_ref, o_ref):
+    h = 128
+    e0, d0c, d0r = _eliminate(m_ref[0:h, 0:h])
+    c = _mm_nt(m_ref[h:, 0:h], e0) / d0r
+    s = m_ref[h:, h:] - _mm_nt(c * d0r, c)
+    e1, d1c, _ = _eliminate(s)
+    q0 = _mm(e0, p_ref[0:h, :])
+    q1 = _mm(e1, p_ref[h:, :] - _mm(c, q0))
+    o_ref[0:h, :] = q0 * lax.rsqrt(d0c)
+    o_ref[h:, :] = q1 * lax.rsqrt(d1c)
+
 def solve_lower(moment, product):
-    return jax.scipy.linalg.solve_triangular(jnp.linalg.cholesky(moment), product, lower=True)
+    return pl.pallas_call(
+        _cholqr_kernel, out_shape=jax.ShapeDtypeStruct(product.shape, jnp.float32)
+    )(moment, product)
 
 
 def apply_gram(subspace, gram):

time: 689 us -> 435 us (0.63)
  other arithmetic: 382 us -> 15.1 us
  Pallas kernels: 0 us -> 131 us
  between operations: 27.6 us -> 16.1 us
    another operation x91 -> x0, other arithmetic: 367 us -> none  [the longest x56 206 us: solve_lower(): jnp.linalg.cholesky(moment)]
    pallas_call x0 -> x8, Pallas kernels: none -> 131 us  [solve_lower(): pl.pallas_call(_cholqr_kernel, out_shape=jax.ShapeDtypeStruct(product.sha...]
    another operation x40 -> x0, matrix products: 13.2 us -> none  [the longest x24 10.7 us: solve_lower(): jax.scipy.linalg.solve_triangular(jnp.linalg.cholesky(moment), product, l...]
  transfers between devices with their start and end apart: 2 -> 2, of which waited for: 1 -> 1; matrix products, arithmetic and copies ran while one was open for 68% -> 21% of each run, Pallas kernels for 0% -> 31%
where the time goes in v2:
time: 435 us; the launch traced here: 427 us
  Pallas kernels  131 us (30%)
  waiting for transfers between devices  121 us (28%)
  matrix products  97 us (22%)
  local copies, waits for them, and re-layouts  29.4 us (7%)
  blocking collectives  16.5 us (4%)
  between operations  16.1 us (4%)
  other arithmetic  15.1 us (3%)
    pallas_call x8, Pallas kernels, solve_lower(): pl.pallas_call(_cholqr_kernel, out_shape=jax.ShapeDtypeStruct(product.sha...  131 us
    psum x1, waiting for transfers between devices, local(): lax.psum(lax.dot_general(prefill_keys, prefill_keys, (((0,), (0,)), ((),...  121 us
    dot_general x8, matrix products, apply_gram(): jnp.dot(subspace, gram, precision=lax.Precision.HIGHEST, preferred_elemen...  41.5 us
    dot_general x16, matrix products, one_head(): jnp.einsum('qgd,cd->qgc', query_group, key_group, preferred_element_type=...  29.7 us
    all_gather x1, blocking collectives, local(): lax.all_gather(picked, 'seq', axis=0, tiled=True)  16.5 us
    dynamic_update_slice x16, local copies, waits for them, and re-layouts, score_rows(): lax.map(one_head, (query_heads, key_heads)) * scale_factor  14 us
    dot_general x8, matrix products, moment_of(): jnp.dot(product, product.T, precision=lax.Precision.HIGHEST, preferred_el...  10.9 us
    dot_general x1, matrix products, local(): lax.dot_general(prefill_keys, prefill_keys, (((0,), (0,)), ((), ())), pre...  10.1 us
  transfers between devices with their start and end apart: 2, of which 1 were waited for; matrix products, arithmetic and copies ran while one was open for 21% of the time, Pallas kernels for 31%

profile of v2, /device:TPU:1, one launch (start us, length us, event | category | flops | bytes accessed | tf_op | source)
XLA Modules:
  0.0 426.7 jit_solution(335420880500580420)
XLA Ops:
  8.1 10.1 %fusion.43 = f32[1024,1024]{1,0:T(8,128)} fusion(bf16[2048,1024]{1,0:T(8,128)(2,1)} %param.8), kind=kOutput, calls=%fused_computation.57 | convolution fusion | flops 4294967296 | bytes 8388608 | tf_op jit(solution)/shard_map/dot_general | solution.py:94
  18.2 5.5 %convert_reduce_fusion = f32[256,1024]{1,0:T(8,128)S(1)} fusion(bf16[2048,1024]{1,0:T(8,128)(2,1)} %param.8), kind=kLoop, calls=%fused_computation.16 | loop fusion | flops 3932160 | bytes 5242880 | tf_op jit(solution)/shard_map/reduce_sum | solution.py:73
  24.7 3.2 copy.19
  27.9 2.6 copy.21
  30.7 2.7 gather_fusion
  33.5 16.5 %all_gather.7 = bf16[256,1024]{1,0:T(8,128)(2,1)S(1)} all-gather(bf16[32,1024]{1,0:T(8,128)(2,1)S(1)} %bitcast_select_fusion), channel_id=1, replica_groups=mesh['kv'=16,'seq'=8] {'seq'}, dimensions={0}, use_global_device_ids=true | all-gather | bytes 589824 | tf_op jit(solution)/shard_map/all_gather | solution.py:92
  50.2 15.9 %while.21 = (s32[]{:T(128)}, f32[8,128,256]{2,1,0:T(8,128)}, bf16[8,128,8,128]{3,1,2,0:T(8,128)(2,1)}, bf16[8,256,128]{1,2,0:T(8,128)(2,1)S(1)}, s32[]{:T(128)}) while((s32[]{:T(128)}, f32[8,128,256]{2,1,0:T(8,128)}, bf16[8,128,8,128]{3,1,2,0:T(8,128)(2,1)}, bf16[8,256,128]{1,2,0:T(8,128)(2,1)S(1)}, s32[]{:T(128)}) %tuple.53), condition=%wide.region_7.8_spmd, body=%wide.region_5.7_spmd.sunk | while | flops 67338240 | bytes 722493 | solution.py:89
  50.2 1.3 convolution_reduce_fusion.5
  59.8 1.3 convolution_reduce_fusion.5
  61.8 1.3 convolution_reduce_fusion.5
  66.1 2.1 multiply_convert_fusion.1
  68.3 120.7 %all-reduce.2.cloned.1.call-done = f32[1024,1024]{1,0:T(8,128)} async-done(((f32[1024,1024]{1,0:T(8,128)}), f32[1024,1024]{1,0:T(8,128)}) %all-reduce.2.cloned.1.call-update) | async-done | bytes 4194320 | tf_op jit(solution)/shard_map/psum | solution.py:93
  189.0 5.0 %fusion.24 = f32[1024,160]{0,1:T(8,128)S(1)} fusion(f32[160,1024]{1,0:T(8,128)S(1)} %copy-done, f32[1024,1024]{1,0:T(8,128)} %all-reduce.2.cloned.1.call-done), kind=kOutput, calls=%fused_computation.32 | convolution fusion | flops 2014314496 | bytes 5505024 | tf_op jit(solution)/shard_map/dot_general | solution.py:62
  194.0 1.4 fusion.44.m_ref
  195.4 16.3 %shard_map.75 = f32[160,1024]{1,0:T(8,128)} custom-call(f32[160,160]{1,0:T(8,128)} %fusion.44.m_ref, f32[160,1024]{1,0:T(8,128)} %bitcast.74), custom_call_target="tpu_custom_call" | custom-call | tf_op jit(solution)/shard_map/pallas_call | solution.py:56
  211.6 5.4 %fusion.22.p_ref = f32[160,1024]{1,0:T(8,128)S(1)} fusion(f32[160,1024]{1,0:T(8,128)} %shard_map.75, f32[1024,1024]{1,0:T(8,128)} %all-reduce.2.cloned.1.call-done), kind=kOutput, calls=%fused_computation.30 | convolution fusion | flops 2014314496 | bytes 5505024 | tf_op jit(solution)/shard_map/dot_general | solution.py:62
  217.0 1.4 fusion.45.m_ref
  218.4 16.3 %shard_map.76 = f32[160,1024]{1,0:T(8,128)} custom-call(f32[160,160]{1,0:T(8,128)} %fusion.45.m_ref, f32[160,1024]{1,0:T(8,128)} %copy-done.2), custom_call_target="tpu_custom_call" | custom-call | tf_op jit(solution)/shard_map/pallas_call | solution.py:56
  234.6 5.2 %fusion.20.p_ref = f32[160,1024]{1,0:T(8,128)S(1)} fusion(f32[160,1024]{1,0:T(8,128)} %shard_map.76, f32[1024,1024]{1,0:T(8,128)} %all-reduce.2.cloned.1.call-done), kind=kOutput, calls=%fused_computation.28 | convolution fusion | flops 2014314496 | bytes 5505024 | tf_op jit(solution)/shard_map/dot_general | solution.py:62
  239.8 1.4 fusion.46.m_ref
  241.2 16.5 %shard_map.77 = f32[160,1024]{1,0:T(8,128)} custom-call(f32[160,160]{1,0:T(8,128)} %fusion.46.m_ref, f32[160,1024]{1,0:T(8,128)} %copy-done.3), custom_call_target="tpu_custom_call" | custom-call | tf_op jit(solution)/shard_map/pallas_call | solution.py:56
  257.7 5.2 %fusion.18.p_ref = f32[160,1024]{1,0:T(8,128)S(1)} fusion(f32[160,1024]{1,0:T(8,128)} %shard_map.77, f32[1024,1024]{1,0:T(8,128)} %all-reduce.2.cloned.1.call-done), kind=kOutput, calls=%fused_computation.26 | convolution fusion | flops 2014314496 | bytes 5505024 | tf_op jit(solution)/shard_map/dot_general | solution.py:62
  262.9 1.4 fusion.47.m_ref
  264.2 16.7 %shard_map.78 = f32[160,1024]{1,0:T(8,128)} custom-call(f32[160,160]{1,0:T(8,128)} %fusion.47.m_ref, f32[160,1024]{1,0:T(8,128)} %copy-done.4), custom_call_target="tpu_custom_call" | custom-call | tf_op jit(solution)/shard_map/pallas_call | solution.py:56
  280.9 5.2 %fusion.16.p_ref = f32[160,1024]{1,0:T(8,128)S(1)} fusion(f32[160,1024]{1,0:T(8,128)} %shard_map.78, f32[1024,1024]{1,0:T(8,128)} %all-reduce.2.cloned.1.call-done), kind=kOutput, calls=%fused_computation.24 | convolution fusion | flops 2014314496 | bytes 5505024 | tf_op jit(solution)/shard_map/dot_general | solution.py:62
  286.1 1.4 fusion.48.m_ref
  287.4 16.3 %shard_map.79 = f32[160,1024]{1,0:T(8,128)} custom-call(f32[160,160]{1,0:T(8,128)} %fusion.48.m_ref, f32[160,1024]{1,0:T(8,128)} %copy-done.5), custom_call_target="tpu_custom_call" | custom-call | tf_op jit(solution)/shard_map/pallas_call | solution.py:56
  303.7 5.3 %fusion.14.p_ref = f32[160,1024]{1,0:T(8,128)S(1)} fusion(f32[160,1024]{1,0:T(8,128)} %shard_map.79, f32[1024,1024]{1,0:T(8,128)} %all-reduce.2.cloned.1.call-done), kind=kOutput, calls=%fused_computation.22 | convolution fusion | flops 2014314496 | bytes 5505024 | tf_op jit(solution)/shard_map/dot_general | solution.py:62
  309.1 1.4 fusion.49.m_ref
  310.4 16.3 %shard_map.80 = f32[160,1024]{1,0:T(8,128)} custom-call(f32[160,160]{1,0:T(8,128)} %fusion.49.m_ref, f32[160,1024]{1,0:T(8,128)} %copy-done.6), custom_call_target="tpu_custom_call" | custom-call | tf_op jit(solution)/shard_map/pallas_call | solution.py:56
  326.7 5.2 %fusion.12.p_ref = f32[160,1024]{1,0:T(8,128)S(1)} fusion(f32[160,1024]{1,0:T(8,128)} %shard_map.80, f32[1024,1024]{1,0:T(8,128)} %all-reduce.2.cloned.1.call-done), kind=kOutput, calls=%fused_computation.20 | convolution fusion | flops 2014314496 | bytes 5505024 | tf_op jit(solution)/shard_map/dot_general | solution.py:62
  331.9 1.4 fusion.50.m_ref
  333.3 16.5 %shard_map.81 = f32[160,1024]{1,0:T(8,128)} custom-call(f32[160,160]{1,0:T(8,128)} %fusion.50.m_ref, f32[160,1024]{1,0:T(8,128)} %copy-done.7), custom_call_target="tpu_custom_call" | custom-call | tf_op jit(solution)/shard_map/pallas_call | solution.py:56
  349.7 5.2 %fusion.10.p_ref = f32[160,1024]{1,0:T(8,128)S(1)} fusion(f32[160,1024]{1,0:T(8,128)} %shard_map.81, f32[1024,1024]{1,0:T(8,128)} %all-reduce.2.cloned.1.call-done), kind=kOutput, calls=%fused_computation.18 | convolution fusion | flops 2014314496 | bytes 5505024 | tf_op jit(solution)/shard_map/dot_general | solution.py:62
  354.9 1.4 fusion.51.m_ref
  356.3 16.5 %shard_map.82 = f32[160,1024]{1,0:T(8,128)} custom-call(f32[160,160]{1,0:T(8,128)} %fusion.51.m_ref, f32[160,1024]{1,0:T(8,128)} %copy-done.1), custom_call_target="tpu_custom_call" | custom-call | tf_op jit(solution)/shard_map/pallas_call | solution.py:56
  372.8 4.8 %convolution_convert_fusion = bf16[160,2048]{1,0:T(8,128)(2,1)} fusion(bf16[2048,1024]{1,0:T(8,128)(2,1)} %param.8, f32[160,1024]{1,0:T(8,128)} %shard_map.82), kind=kOutput, calls=%fused_computation.17 | convolution fusion | flops 671580160 | bytes 5505024 | tf_op jit(solution)/shard_map/dot_general | solution.py:104
  377.5 6.4 %copy.20 = bf16[2048,1024]{0,1:T(8,128)(2,1)} copy(bf16[2048,1024]{1,0:T(8,128)(2,1)} %all-gather.2.cloned.1.call-done) | data formatting | bytes 8388608 | tf_op jit(solution)/shard_map/all_gather | solution.py:91
  384.0 28.3 %while.20 = (s32[]{:T(128)}, f32[8,128,2048]{2,1,0:T(8,128)}, bf16[8,128,8,128]{3,1,2,0:T(8,128)(2,1)}, bf16[8,2048,128]{1,2,0:T(8,128)(2,1)}, s32[]{:T(128)}) while((s32[]{:T(128)}, f32[8,128,2048]{2,1,0:T(8,128)}, bf16[8,128,8,128]{3,1,2,0:T(8,128)(2,1)}, bf16[8,2048,128]{1,2,0:T(8,128)(2,1)}, s32[]{:T(128)}) %tuple.52), condition=%wide.region_4.5_spmd, body=%wide.region_2.4_spmd.sunk | while | flops 538705920 | bytes 3933757 | solution.py:89
  384.0 2.5 convolution_reduce_fusion.4
  387.5 2.5 convolution_reduce_fusion.4
  391.1 2.5 convolution_reduce_fusion.4
  394.6 2.5 convolution_reduce_fusion.4
  398.1 2.5 convolution_reduce_fusion.4
  401.6 2.5 convolution_reduce_fusion.4
  405.2 2.5 convolution_reduce_fusion.4
  408.7 2.5 convolution_reduce_fusion.4
  412.3 6.6 %multiply_convert_fusion = bf16[8,128,2048]{2,1,0:T(8,128)(2,1)} fusion(f32[8,128,2048]{2,1,0:T(8,128)} %get-tuple-element.48), kind=kLoop, calls=%fused_computation.15 | loop fusion | flops 4194304 | bytes 12582912 | tf_op jit(solution)/shard_map/convert_element_type | solution.py:89
  (56 shorter events, 21.7 us)
Async XLA Ops:
  8.0 181.0 %copy-start = (f32[160,1024]{1,0:T(8,128)S(1)}, f32[160,1024]{1,0:T(8,128)}, u32[]{:S(2)}) copy-start(f32[160,1024]{1,0:T(8,128)} %param.11) | copy-start | bytes 1966084
  8.0 181.0 %all-reduce.2.cloned.1.call-start = ((), (), s32[]{:S(2)}) async-start(), calls=%async_computation | async-start | bytes 8388608 | tf_op jit(solution)/shard_map/psum | solution.py:93
  18.2 6.4 %copy-start.9 = (s32[4]{0:T(128)S(1)}, s32[4]{0:T(128)}, u32[]{:S(2)}) copy-start(s32[4]{0:T(128)} %param.10) | copy-start | bytes 52
  18.2 359.4 %all-gather.2.cloned.1.call-start = ((), (), s32[]{:S(2)}) async-start(), calls=%async_computation.1 | async-start | bytes 4718592 | tf_op jit(solution)/shard_map/all_gather | solution.py:91
  194.0 1.4 copy-start.8
  217.0 1.4 copy-start.2
  239.8 1.4 copy-start.3
  262.8 1.4 copy-start.4
  286.1 1.4 copy-start.5
  309.1 1.4 copy-start.6
  331.9 1.4 copy-start.7
  354.9 1.4 copy-start.1
Sparse Core Ops, SparseCore 0:
  18.3 170.6 all-reduce.1
Sparse Core Ops, SparseCore 1:
  24.7 39.7 all-gather.1

commit v3 on v1

--- a/solution.py
+++ b/solution.py
@@ -3,7 +3,12 @@
 import jax
 import jax.numpy as jnp
 from jax import lax
+from jax.experimental import pallas as pl
+from jax.experimental.pallas import tpu as pltpu
 from jax.sharding import PartitionSpec as P
+
+HI = lax.Precision.HIGHEST
+HALF = 128
 
 KVH = 8
 HEAD = 128
@@ -12,20 +17,67 @@
 SPAN = 8
 
 
-def moment_of(product):
-    return jnp.dot(
-        product, product.T, precision=lax.Precision.HIGHEST, preferred_element_type=jnp.float32
+def _mm(a, b):
+    return jnp.dot(a, b, precision=HI, preferred_element_type=jnp.float32)
+
+
+def _mm_nt(a, b):
+    return lax.dot_general(
+        a, b, (((1,), (1,)), ((), ())), precision=HI, preferred_element_type=jnp.float32
     )
 
 
-def solve_lower(moment, product):
-    return jax.scipy.linalg.solve_triangular(jnp.linalg.cholesky(moment), product, lower=True)
+def _eliminate(a_ref, e_ref):
+    n = a_ref.shape[0]
+    eye = lax.broadcasted_iota(jnp.int32, (n, n), 0) == lax.broadcasted_iota(jnp.int32, (n, n), 1)
+    e_ref[...] = eye.astype(jnp.float32)
+    for j in range(n):
+        low = (j // 8) * 8
+        row_a = a_ref[j:j + 1, :]
+        inv = 1.0 / row_a[:, j:j + 1]
+        rows = lax.broadcasted_iota(jnp.int32, (n - low, 1), 0) + low
+        part = a_ref[low:, :]
+        f = jnp.where(rows > j, part[:, j:j + 1] * inv, 0.0)
+        a_ref[low:, :] = part - f * row_a
+        e_ref[low:, :] = e_ref[low:, :] - f * e_ref[j:j + 1, :]
+    diag = jnp.where(eye, a_ref[...], 0.0)
+    return jnp.sum(diag, axis=1, keepdims=True), jnp.sum(diag, axis=0, keepdims=True)
 
 
-def apply_gram(subspace, gram):
-    return jnp.dot(
-        subspace, gram, precision=lax.Precision.HIGHEST, preferred_element_type=jnp.float32
-    )
+def _iterate_kernel(g_ref, s_ref, o_ref, a0_ref, e0_ref, a1_ref, e1_ref):
+    o_ref[...] = s_ref[...]
+
+    def step(i, carry):
+        product = _mm(o_ref[...], g_ref[...])
+        moment = _mm_nt(product, product)
+        a0_ref[...] = moment[0:HALF, 0:HALF]
+        d0c, d0r = _eliminate(a0_ref, e0_ref)
+        e0 = e0_ref[...]
+        c = _mm_nt(moment[HALF:, 0:HALF], e0) / d0r
+        a1_ref[...] = moment[HALF:, HALF:] - _mm_nt(c * d0r, c)
+        d1c, _ = _eliminate(a1_ref, e1_ref)
+        q0 = _mm(e0, product[0:HALF, :])
+        q1 = _mm(e1_ref[...], product[HALF:, :] - _mm(c, q0))
+        o_ref[0:HALF, :] = q0 * lax.rsqrt(d0c)
+        o_ref[HALF:, :] = q1 * lax.rsqrt(d1c)
+        return carry
+
+    lax.fori_loop(0, ITERS, step, 0)
+
+
+def iterate(gram, start):
+    rank = start.shape[0]
+    rest = rank - HALF
+    return pl.pallas_call(
+        _iterate_kernel,
+        out_shape=jax.ShapeDtypeStruct(start.shape, jnp.float32),
+        scratch_shapes=[
+            pltpu.VMEM((HALF, HALF), jnp.float32),
+            pltpu.VMEM((HALF, HALF), jnp.float32),
+            pltpu.VMEM((rest, rest), jnp.float32),
+            pltpu.VMEM((rest, rest), jnp.float32),
+        ],
+    )(gram, start)
 
 
 def local(prefill_keys, queries, outlier_spans, start_basis):
@@ -60,10 +112,7 @@
         ),
         ("kv", "seq"),
     ) * inverse_tokens
-    subspace = start_basis
-    for iteration in range(ITERS):
-        product = apply_gram(subspace, gram)
-        subspace = solve_lower(moment_of(product), product)
+    subspace = iterate(gram, start_basis)
     rounded = subspace.astype(jnp.bfloat16)
     coefficients = lax.dot_general(
         rounded, prefill_keys, (((1,), (1,)), ((), ())), preferred_element_type=jnp.float32

time: 689 us -> 393 us (0.57)
  other arithmetic: 382 us -> 19 us
  Pallas kernels: 0 us -> 145 us
  matrix products: 103 us -> 44.5 us
  between operations: 27.6 us -> 15.5 us
    another operation x91 -> x0, other arithmetic: 367 us -> none  [the longest x56 206 us: solve_lower(): jnp.linalg.cholesky(moment)]
    pallas_call x0 -> x1, Pallas kernels: none -> 145 us  [iterate(): pl.pallas_call(_iterate_kernel, out_shape=jax.ShapeDtypeStruct(start.shap...]
    dot_general x16 -> x0, matrix products: 45.3 us -> none  [the longest x8 39.8 us: apply_gram(): jnp.dot(subspace, gram, precision=lax.Precision.HIGHEST, preferred_elemen...]
    another operation x40 -> x0, matrix products: 13.2 us -> none  [the longest x24 10.7 us: solve_lower(): jax.scipy.linalg.solve_triangular(jnp.linalg.cholesky(moment), product, l...]
  transfers between devices with their start and end apart: 2 -> 2, of which waited for: 1 -> 1; matrix products, arithmetic and copies ran while one was open for 68% -> 9% of each run, Pallas kernels for 0% -> 37%
where the time goes in v3:
time: 393 us; the launch traced here: 392 us
  Pallas kernels  145 us (37%)
  waiting for transfers between devices  127 us (32%)
  matrix products  44.5 us (11%)
  local copies, waits for them, and re-layouts  24.1 us (6%)
  other arithmetic  19 us (5%)
  blocking collectives  16.4 us (4%)
  between operations  15.5 us (4%)
    pallas_call x1, Pallas kernels, iterate(): pl.pallas_call(_iterate_kernel, out_shape=jax.ShapeDtypeStruct(start.shap...  145 us
    psum x1, waiting for transfers between devices, local(): lax.psum(lax.dot_general(prefill_keys, prefill_keys, (((0,), (0,)), ((),...  127 us
    dot_general x16, matrix products, one_head(): jnp.einsum('qgd,cd->qgc', query_group, key_group, preferred_element_type=...  29.7 us
    all_gather x1, blocking collectives, local(): lax.all_gather(picked, 'seq', axis=0, tiled=True)  16.4 us
    dot_general x1, matrix products, local(): lax.dot_general(prefill_keys, prefill_keys, (((0,), (0,)), ((), ())), pre...  10 us
    dynamic_update_slice x16, local copies, waits for them, and re-layouts, score_rows(): lax.map(one_head, (query_heads, key_heads)) * scale_factor  8.73 us
  transfers between devices with their start and end apart: 2, of which 1 were waited for; matrix products, arithmetic and copies ran while one was open for 9% of the time, Pallas kernels for 37%

profile of v3, /device:TPU:1, one launch (start us, length us, event | category | flops | bytes accessed | tf_op | source)
XLA Modules:
  0.0 392.2 jit_solution(1730364924481433816)
XLA Ops:
  8.0 0.0 all-reduce.2.cloned.1.call-start
  8.0 10.0 %fusion.11 = f32[1024,1024]{1,0:T(8,128)} fusion(bf16[2048,1024]{1,0:T(8,128)(2,1)} %param.8), kind=kOutput, calls=%fused_computation.26 | convolution fusion | flops 4294967296 | bytes 8388608 | tf_op jit(solution)/shard_map/dot_general | solution.py:110
  18.1 0.0 all-reduce.2.cloned.1.call-update
  18.1 0.0 all-gather.2.cloned.1.call-start
  18.2 5.5 %convert_reduce_fusion = f32[256,1024]{1,0:T(8,128)S(1)} fusion(bf16[2048,1024]{1,0:T(8,128)(2,1)} %param.8), kind=kLoop, calls=%fused_computation.16 | loop fusion | flops 3932160 | bytes 5242880 | tf_op jit(solution)/shard_map/reduce_sum | solution.py:89
  23.6 0.9 multiply_convert_fusion.2
  24.5 0.0 all-gather.2.cloned.1.call-update
  24.6 3.2 copy.19
  27.8 2.6 copy.21
  30.4 0.1 broadcast_in_dim.32
  30.5 0.1 broadcast_in_dim.33
  30.6 2.7 gather_fusion
  33.4 0.1 bitcast_select_fusion
  33.4 16.4 %all_gather.7 = bf16[256,1024]{1,0:T(8,128)(2,1)S(1)} all-gather(bf16[32,1024]{1,0:T(8,128)(2,1)S(1)} %bitcast_select_fusion), channel_id=1, replica_groups=mesh['kv'=16,'seq'=8] {'seq'}, dimensions={0}, use_global_device_ids=true | all-gather | bytes 589824 | tf_op jit(solution)/shard_map/all_gather | solution.py:108
  49.9 0.2 copy.23
  50.1 10.6 %while.21 = (s32[]{:T(128)}, f32[8,128,256]{2,1,0:T(8,128)S(1)}, bf16[8,128,8,128]{3,1,2,0:T(8,128)(2,1)}, bf16[8,256,128]{1,2,0:T(8,128)(2,1)S(1)}, s32[]{:T(128)}) while((s32[]{:T(128)}, f32[8,128,256]{2,1,0:T(8,128)S(1)}, bf16[8,128,8,128]{3,1,2,0:T(8,128)(2,1)}, bf16[8,256,128]{1,2,0:T(8,128)(2,1)S(1)}, s32[]{:T(128)}) %tuple.53), condition=%wide.region_7.8_spmd, body=%wide.region_5.7_spmd.sunk | while | flops 67338240 | bytes 721985 | solution.py:105
  50.3 1.3 convolution_reduce_fusion.5
  51.6 1.3 convolution_reduce_fusion.5
  52.9 1.3 convolution_reduce_fusion.5
  54.2 1.3 convolution_reduce_fusion.5
  55.5 1.3 convolution_reduce_fusion.5
  56.9 1.3 convolution_reduce_fusion.5
  58.2 1.2 convolution_reduce_fusion.5
  59.5 1.3 convolution_reduce_fusion.5
  60.7 0.9 multiply_convert_fusion.1
  61.7 127.3 %all-reduce.2.cloned.1.call-done = f32[1024,1024]{1,0:T(8,128)} async-done(((f32[1024,1024]{1,0:T(8,128)}), f32[1024,1024]{1,0:T(8,128)}) %all-reduce.2.cloned.1.call-update) | async-done | bytes 4194320 | tf_op jit(solution)/shard_map/psum | solution.py:109
  188.9 5.0 %broadcast_multiply_fusion.g_ref = f32[1024,1024]{1,0:T(8,128)} fusion(f32[1024,1024]{1,0:T(8,128)} %all-reduce.2.cloned.1.call-done), kind=kLoop, calls=%fused_computation.18 | loop fusion | flops 1048576 | bytes 8388608 | tf_op jit(solution)/shard_map/mul | solution.py:109
  194.0 144.8 %shard_map.75 = f32[160,1024]{1,0:T(8,128)} custom-call(f32[1024,1024]{1,0:T(8,128)} %broadcast_multiply_fusion.g_ref, f32[160,1024]{1,0:T(8,128)} %s_ref.1), custom_call_target="tpu_custom_call" | custom-call | tf_op jit(solution)/shard_map/pallas_call | solution.py:71
  338.7 4.8 %convolution_convert_fusion = bf16[160,2048]{1,0:T(8,128)(2,1)} fusion(bf16[2048,1024]{1,0:T(8,128)(2,1)} %param.8, f32[160,1024]{1,0:T(8,128)} %shard_map.75), kind=kOutput, calls=%fused_computation.17 | convolution fusion | flops 671580160 | bytes 5505024 | tf_op jit(solution)/shard_map/dot_general | solution.py:117
  343.5 6.4 %copy.20 = bf16[2048,1024]{0,1:T(8,128)(2,1)} copy(bf16[2048,1024]{1,0:T(8,128)(2,1)} %all-gather.2.cloned.1.call-done) | data formatting | bytes 8388608 | tf_op jit(solution)/shard_map/all_gather | solution.py:107
  349.9 28.3 %while.20 = (s32[]{:T(128)}, f32[8,128,2048]{2,1,0:T(8,128)}, bf16[8,128,8,128]{3,1,2,0:T(8,128)(2,1)}, bf16[8,2048,128]{1,2,0:T(8,128)(2,1)}, s32[]{:T(128)}) while((s32[]{:T(128)}, f32[8,128,2048]{2,1,0:T(8,128)}, bf16[8,128,8,128]{3,1,2,0:T(8,128)(2,1)}, bf16[8,2048,128]{1,2,0:T(8,128)(2,1)}, s32[]{:T(128)}) %tuple.52), condition=%wide.region_4.5_spmd, body=%wide.region_2.4_spmd.sunk | while | flops 538705920 | bytes 3933757 | solution.py:105
  349.9 2.5 convolution_reduce_fusion.4
  352.4 1.1 bitcast_dynamic-update-slice_fusion.4
  353.4 2.5 convolution_reduce_fusion.4
  355.9 1.1 bitcast_dynamic-update-slice_fusion.4
  357.0 2.5 convolution_reduce_fusion.4
  359.5 1.1 bitcast_dynamic-update-slice_fusion.4
  360.5 2.5 convolution_reduce_fusion.4
  363.0 1.1 bitcast_dynamic-update-slice_fusion.4
  364.1 2.5 convolution_reduce_fusion.4
  366.5 1.1 bitcast_dynamic-update-slice_fusion.4
  367.6 2.5 convolution_reduce_fusion.4
  370.0 1.1 bitcast_dynamic-update-slice_fusion.4
  371.1 2.5 convolution_reduce_fusion.4
  373.6 1.1 bitcast_dynamic-update-slice_fusion.4
  374.7 2.5 convolution_reduce_fusion.4
  377.1 1.1 bitcast_dynamic-update-slice_fusion.4
  378.2 6.6 %multiply_convert_fusion = bf16[8,128,2048]{2,1,0:T(8,128)(2,1)} fusion(f32[8,128,2048]{2,1,0:T(8,128)} %get-tuple-element.48), kind=kLoop, calls=%fused_computation.15 | loop fusion | flops 4194304 | bytes 12582912 | tf_op jit(solution)/shard_map/convert_element_type | solution.py:105
  (16 shorter events, 0.2 us)
Async XLA Ops:
  8.0 180.9 %all-reduce.2.cloned.1.call-start = ((), (), s32[]{:S(2)}) async-start(), calls=%async_computation | async-start | bytes 8388608 | tf_op jit(solution)/shard_map/psum | solution.py:109
  18.1 325.4 %all-gather.2.cloned.1.call-start = ((), (), s32[]{:S(2)}) async-start(), calls=%async_computation.1 | async-start | bytes 4718592 | tf_op jit(solution)/shard_map/all_gather | solution.py:107
  24.6 5.9 %copy-start = (s32[4]{0:T(128)S(1)}, s32[4]{0:T(128)}, u32[]{:S(2)}) copy-start(s32[4]{0:T(128)} %param.10) | copy-start | bytes 52
Sparse Core Ops, SparseCore 0:
  18.2 170.6 all-reduce.1
Sparse Core Ops, SparseCore 1:
  24.6 39.6 all-gather.1

commit v4 on v3

--- a/solution.py
+++ b/solution.py
@@ -80,6 +80,38 @@
     )(gram, start)
 
 
+def _swap(x, flip):
+    return lax.ppermute(x, "seq", [(i, i ^ flip) for i in range(lax.axis_size("seq"))])
+
+
+def _halve(x, bit, flip):
+    rows = x.shape[0] // 2
+    keep = lax.dynamic_slice_in_dim(x, bit * rows, rows)
+    send = lax.dynamic_slice_in_dim(x, (1 - bit) * rows, rows)
+    return keep + _swap(send, flip)
+
+
+def _double(x, bit, flip):
+    other = _swap(x, flip)
+    rows = x.shape[0]
+    out = jnp.zeros((2 * rows,) + x.shape[1:], x.dtype)
+    out = lax.dynamic_update_slice_in_dim(out, x, bit * rows, 0)
+    return lax.dynamic_update_slice_in_dim(out, other, (1 - bit) * rows, 0)
+
+
+def sum_gram(local_gram):
+    seq = lax.axis_index("seq")
+    kv_size = lax.axis_size("kv")
+    core, z_low, z_high = seq % 2, (seq // 2) % 2, (seq // 4) % 2
+    s = _halve(local_gram, core, 1)
+    s = lax.all_to_all(s.reshape((kv_size, -1) + s.shape[1:]), "kv", 0, 0, tiled=True)
+    s = jnp.sum(s, axis=0)
+    s = _halve(_halve(s, z_high, 4), z_low, 2)
+    s = _double(_double(s, z_low, 2), z_high, 4)
+    s = lax.all_gather(s, "kv", axis=0, tiled=True)
+    return _double(s, core, 1)
+
+
 def local(prefill_keys, queries, outlier_spans, start_basis):
     rows_dev = prefill_keys.shape[0]
     width = prefill_keys.shape[1]
@@ -106,12 +138,10 @@
 
     landmark_scores = score_rows(lax.all_gather(landmarks, "seq", axis=0, tiled=True))
     outlier_scores = score_rows(lax.all_gather(picked, "seq", axis=0, tiled=True))
-    gram = lax.psum(
-        lax.dot_general(
-            prefill_keys, prefill_keys, (((0,), (0,)), ((), ())), preferred_element_type=jnp.float32
-        ),
-        ("kv", "seq"),
+    local_gram = lax.dot_general(
+        prefill_keys, prefill_keys, (((0,), (0,)), ((), ())), preferred_element_type=jnp.float32
     ) * inverse_tokens
+    gram = sum_gram(local_gram)
     subspace = iterate(gram, start_basis)
     rounded = subspace.astype(jnp.bfloat16)
     coefficients = lax.dot_general(

time: 393 us -> 337 us (0.86)
  waiting for transfers between devices: 127 us -> 44.3 us
  starting transfers between devices: 0.08 us -> 20.3 us
  local copies, waits for them, and re-layouts: 24.1 us -> 33.8 us
    psum x1 -> x0, waiting for transfers between devices: 127 us -> none  [local(): lax.psum(lax.dot_general(prefill_keys, prefill_keys, (((0,), (0,)), ((),...]
    all_to_all x0 -> x1, waiting for transfers between devices: none -> 32 us  [sum_gram(): lax.all_to_all(s.reshape((kv_size, -1) + s.shape[1:]), 'kv', 0, 0, tiled=...]
    ppermute x0 -> x6, starting transfers between devices: none -> 13.4 us  [_swap(): lax.ppermute(x, 'seq', [(i, i ^ flip) for i in range(lax.axis_size('seq'))])]
    ppermute x0 -> x6, waiting for transfers between devices: none -> 10.7 us  [_swap(): lax.ppermute(x, 'seq', [(i, i ^ flip) for i in range(lax.axis_size('seq'))])]
    all_to_all x0 -> x1, starting transfers between devices: none -> 6.84 us  [sum_gram(): lax.all_to_all(s.reshape((kv_size, -1) + s.shape[1:]), 'kv', 0, 0, tiled=...]
    mul x1 -> x0, other arithmetic: 5.04 us -> none  [local(): lax.psum(lax.dot_general(prefill_keys, prefill_keys, (((0,), (0,)), ((),...]
  transfers between devices with their start and end apart: 2 -> 9, of which waited for: 1 -> 7; matrix products, arithmetic and copies ran while one was open for 9% -> 23% of each run, Pallas kernels for 37% -> 0%
where the time goes in v4:
time: 337 us; the launch traced here: 336 us
  Pallas kernels  145 us (43%)
  waiting for transfers between devices  44.3 us (13%)
  matrix products  42 us (12%)
  local copies, waits for them, and re-layouts  33.8 us (10%)
  starting transfers between devices  20.3 us (6%)
  blocking collectives  19.3 us (6%)
  other arithmetic  17.4 us (5%)
  between operations  14.2 us (4%)
    pallas_call x1, Pallas kernels, iterate(): pl.pallas_call(_iterate_kernel, out_shape=jax.ShapeDtypeStruct(start.shap...  145 us
    all_to_all x1, waiting for transfers between devices, sum_gram(): lax.all_to_all(s.reshape((kv_size, -1) + s.shape[1:]), 'kv', 0, 0, tiled=...  32 us
    dot_general x16, matrix products, one_head(): jnp.einsum('qgd,cd->qgc', query_group, key_group, preferred_element_type=...  29.6 us
    all_gather x1, blocking collectives, local(): lax.all_gather(picked, 'seq', axis=0, tiled=True)  19.3 us
    ppermute x6, starting transfers between devices, _swap(): lax.ppermute(x, 'seq', [(i, i ^ flip) for i in range(lax.axis_size('seq'))])  13.4 us
    ppermute x6, waiting for transfers between devices, _swap(): lax.ppermute(x, 'seq', [(i, i ^ flip) for i in range(lax.axis_size('seq'))])  10.7 us
    dynamic_update_slice x16, local copies, waits for them, and re-layouts, score_rows(): lax.map(one_head, (query_heads, key_heads)) * scale_factor  8.68 us
    dot_general x1, matrix products, local(): lax.dot_general(prefill_keys, prefill_keys, (((0,), (0,)), ((), ())), pre...  7.63 us
  transfers between devices with their start and end apart: 9, of which 7 were waited for; matrix products, arithmetic and copies ran while one was open for 23% of the time, Pallas kernels for 0%

profile of v4, /device:TPU:1, one launch (start us, length us, event | category | flops | bytes accessed | tf_op | source)
XLA Modules:
  0.0 336.4 jit_solution(12903711462460801892)
XLA Ops:
  7.2 5.5 %convert_reduce_fusion = f32[256,1024]{1,0:T(8,128)S(1)} fusion(bf16[2048,1024]{1,0:T(8,128)(2,1)} %param.8), kind=kLoop, calls=%fused_computation.16 | loop fusion | flops 3932160 | bytes 5242880 | tf_op jit(solution)/shard_map/reduce_sum | solution.py:121
  13.6 7.6 %convolution_multiply_fusion = f32[1024,1024]{1,0:T(8,128)S(1)} fusion(bf16[2048,1024]{1,0:T(8,128)(2,1)} %param.8), kind=kOutput, calls=%fused_computation.18 | convolution fusion | flops 4296015872 | bytes 8388608 | tf_op jit(solution)/shard_map/dot_general | solution.py:141
  21.2 2.0 copy-done
  23.3 1.6 constant_dynamic-slice_fusion.2
  24.8 1.4 collective-permute-start
  26.3 4.0 %collective-permute-done = f32[512,1024]{1,0:T(8,128)S(1)} collective-permute-done((f32[512,1024]{1,0:T(8,128)}, f32[512,1024]{1,0:T(8,128)S(1)}, u32[]{:S(2)}, u32[]{:S(2)}) %collective-permute-start) | collective-permute-done | bytes 2097184 | tf_op jit(solution)/shard_map/ppermute | solution.py:84
  30.3 3.3 dynamic-slice_add_fusion
  33.6 6.8 %all-to-all-start = ((f32[16,32,1024]{2,1,0:T(8,128)}), f32[16,32,1024]{2,1,0:T(8,128)S(1)}, u32[]{:S(2)}, u32[]{:S(2)}) async-start(f32[16,32,1024]{2,1,0:T(8,128)} %bitcast.8), calls=%async_computation | async-start | bytes 4194304 | tf_op jit(solution)/shard_map/all_to_all | solution.py:107
  40.5 32.0 %all-to-all-done = f32[16,32,1024]{2,1,0:T(8,128)S(1)} async-done(((f32[16,32,1024]{2,1,0:T(8,128)}), f32[16,32,1024]{2,1,0:T(8,128)S(1)}, u32[]{:S(2)}, u32[]{:S(2)}) %all-to-all-start) | async-done | bytes 2097184 | tf_op jit(solution)/shard_map/all_to_all | solution.py:107
  72.6 4.3 %collective-permute-start.1 = (f32[16,1024]{1,0:T(8,128)S(1)}, f32[16,1024]{1,0:T(8,128)S(1)}, u32[]{:S(2)}, u32[]{:S(2)}) collective-permute-start(f32[16,1024]{1,0:T(8,128)S(1)} %constant_dynamic-slice_fusion.1), channel_id=1, source_target_pairs={{0,4},{1,5},{2,6},{3,7},{4,0},{5,1},{6,2},{7,3},{8,12},{9,13},{10,... | collective-permute-start | bytes 196616 | tf_op jit(solution)/shard_map/ppermute | solution.py:84
  76.9 1.7 collective-permute-done.1
  78.6 1.5 collective-permute-start.2
  80.0 1.7 collective-permute-done.2
  81.8 1.1 collective-permute-start.3
  82.9 1.7 collective-permute-done.3
  84.6 3.6 %collective-permute-start.4 = (f32[16,1024]{1,0:T(8,128)S(1)}, f32[16,1024]{1,0:T(8,128)S(1)}, u32[]{:S(2)}, u32[]{:S(2)}) collective-permute-start(f32[16,1024]{1,0:T(8,128)S(1)} %constant_dynamic-update-slice_fusion.4), channel_id=1, source_target_pairs={{0,4},{1,5},{2,6},{3,7},{4,0},{5,1},{6,2},{7,3},{8,12},{9,13},{10,... | collective-permute-start | bytes 196616 | tf_op jit(solution)/shard_map/ppermute | solution.py:84
  88.3 1.6 collective-permute-done.4
  90.6 3.2 copy.19
  93.9 2.6 copy.21
  96.7 2.7 gather_fusion
  99.5 19.3 %all_gather.11 = bf16[256,1024]{1,0:T(8,128)(2,1)S(1)} all-gather(bf16[32,1024]{1,0:T(8,128)(2,1)S(1)} %bitcast_select_fusion), channel_id=1, replica_groups=mesh['kv'=16,'seq'=8] {'seq'}, dimensions={0}, use_global_device_ids=true | all-gather | bytes 589824 | tf_op jit(solution)/shard_map/all_gather | solution.py:140
  119.0 10.4 %while.21 = (s32[]{:T(128)}, f32[8,128,256]{2,1,0:T(8,128)S(1)}, bf16[8,128,8,128]{3,1,2,0:T(8,128)(2,1)}, bf16[8,256,128]{1,2,0:T(8,128)(2,1)S(1)}, s32[]{:T(128)}) while((s32[]{:T(128)}, f32[8,128,256]{2,1,0:T(8,128)S(1)}, bf16[8,128,8,128]{3,1,2,0:T(8,128)(2,1)}, bf16[8,256,128]{1,2,0:T(8,128)(2,1)S(1)}, s32[]{:T(128)}) %tuple.54), condition=%wide.region_7.8_spmd, body=%wide.region_5.7_spmd.sunk | while | flops 67338240 | bytes 721985 | solution.py:137
  119.0 1.2 convolution_reduce_fusion.5
  120.3 1.2 convolution_reduce_fusion.5
  121.6 1.2 convolution_reduce_fusion.5
  122.9 1.2 convolution_reduce_fusion.5
  124.2 1.3 convolution_reduce_fusion.5
  125.5 1.2 convolution_reduce_fusion.5
  126.8 1.2 convolution_reduce_fusion.5
  128.1 1.2 convolution_reduce_fusion.5
  130.3 6.4 %copy.20 = bf16[2048,1024]{0,1:T(8,128)(2,1)} copy(bf16[2048,1024]{1,0:T(8,128)(2,1)} %all-gather.5.cloned.1.call-done) | data formatting | bytes 8388608 | tf_op jit(solution)/shard_map/all_gather | solution.py:139
  136.7 1.6 all-gather.3.cloned.1.call-done
  138.3 1.5 collective-permute-start.5
  139.8 28.2 %while.20 = (s32[]{:T(128)}, f32[8,128,2048]{2,1,0:T(8,128)}, bf16[8,128,8,128]{3,1,2,0:T(8,128)(2,1)}, bf16[8,2048,128]{1,2,0:T(8,128)(2,1)}, s32[]{:T(128)}) while((s32[]{:T(128)}, f32[8,128,2048]{2,1,0:T(8,128)}, bf16[8,128,8,128]{3,1,2,0:T(8,128)(2,1)}, bf16[8,2048,128]{1,2,0:T(8,128)(2,1)}, s32[]{:T(128)}) %tuple.53), condition=%wide.region_4.5_spmd, body=%wide.region_2.4_spmd.sunk | while | flops 538705920 | bytes 3933757 | solution.py:137
  139.8 2.5 convolution_reduce_fusion.4
  143.3 2.5 convolution_reduce_fusion.4
  146.8 2.5 convolution_reduce_fusion.4
  150.4 2.5 convolution_reduce_fusion.4
  153.9 2.5 convolution_reduce_fusion.4
  157.4 2.5 convolution_reduce_fusion.4
  160.9 2.5 convolution_reduce_fusion.4
  164.5 2.5 convolution_reduce_fusion.4
  168.0 6.6 %multiply_convert_fusion = bf16[8,128,2048]{2,1,0:T(8,128)(2,1)} fusion(f32[8,128,2048]{2,1,0:T(8,128)} %get-tuple-element.48), kind=kLoop, calls=%fused_computation.15 | loop fusion | flops 4194304 | bytes 12582912 | tf_op jit(solution)/shard_map/convert_element_type | solution.py:137
  174.6 2.5 broadcast_in_dim.39
  177.1 1.5 constant_dynamic-update-slice_fusion.1
  178.5 1.5 constant_dynamic-update-slice_fusion.g_ref
  180.0 144.8 %shard_map.75 = f32[160,1024]{1,0:T(8,128)} custom-call(f32[1024,1024]{1,0:T(8,128)} %constant_dynamic-update-slice_fusion.g_ref, f32[160,1024]{1,0:T(8,128)} %s_ref.1), custom_call_target="tpu_custom_call" | custom-call | tf_op jit(solution)/shard_map/pallas_call | solution.py:71
  324.8 4.8 %convolution_convert_fusion = bf16[160,2048]{1,0:T(8,128)(2,1)} fusion(bf16[2048,1024]{1,0:T(8,128)(2,1)} %param.8, f32[160,1024]{1,0:T(8,128)} %shard_map.75), kind=kOutput, calls=%fused_computation.17 | convolution fusion | flops 671580160 | bytes 5505024 | tf_op jit(solution)/shard_map/dot_general | solution.py:147
  (50 shorter events, 11.9 us)
Async XLA Ops:
  7.2 123.1 %all-gather.5.cloned.1.call-start = ((), (), s32[]{:S(2)}) async-start(), calls=%async_computation.2 | async-start | bytes 4718592 | tf_op jit(solution)/shard_map/all_gather | solution.py:139
  21.2 2.0 copy-start
  24.8 5.4 %collective-permute-start = (f32[512,1024]{1,0:T(8,128)}, f32[512,1024]{1,0:T(8,128)S(1)}, u32[]{:S(2)}, u32[]{:S(2)}) collective-permute-start(f32[512,1024]{1,0:T(8,128)} %constant_dynamic-slice_fusion.2), channel_id=1, source_target_pairs={{0,1},{1,0},{2,3},{3,2},{4,5},{5,4},{6,7},{7,6},{8,9},{9,8},{10,11... | collective-permute-start | bytes 6291464 | tf_op jit(solution)/shard_map/ppermute | solution.py:84
  33.6 38.9 %all-to-all-start = ((f32[16,32,1024]{2,1,0:T(8,128)}), f32[16,32,1024]{2,1,0:T(8,128)S(1)}, u32[]{:S(2)}, u32[]{:S(2)}) async-start(f32[16,32,1024]{2,1,0:T(8,128)} %bitcast.8), calls=%async_computation | async-start | bytes 4194304 | tf_op jit(solution)/shard_map/all_to_all | solution.py:107
  40.4 97.8 %all-gather.3.cloned.1.call-start = ((), (), s32[]{:S(2)}) async-start(), calls=%async_computation.1 | async-start | bytes 2228224 | tf_op jit(solution)/shard_map/all_gather | solution.py:111
  72.6 5.9 %collective-permute-start.1 = (f32[16,1024]{1,0:T(8,128)S(1)}, f32[16,1024]{1,0:T(8,128)S(1)}, u32[]{:S(2)}, u32[]{:S(2)}) collective-permute-start(f32[16,1024]{1,0:T(8,128)S(1)} %constant_dynamic-slice_fusion.1), channel_id=1, source_target_pairs={{0,4},{1,5},{2,6},{3,7},{4,0},{5,1},{6,2},{7,3},{8,12},{9,13},{10,... | collective-permute-start | bytes 196616 | tf_op jit(solution)/shard_map/ppermute | solution.py:84
  78.6 3.2 collective-permute-start.2
  81.8 2.8 collective-permute-start.3
  84.6 5.3 %collective-permute-start.4 = (f32[16,1024]{1,0:T(8,128)S(1)}, f32[16,1024]{1,0:T(8,128)S(1)}, u32[]{:S(2)}, u32[]{:S(2)}) collective-permute-start(f32[16,1024]{1,0:T(8,128)S(1)} %constant_dynamic-update-slice_fusion.4), channel_id=1, source_target_pairs={{0,4},{1,5},{2,6},{3,7},{4,0},{5,1},{6,2},{7,3},{8,12},{9,13},{10,... | collective-permute-start | bytes 196616 | tf_op jit(solution)/shard_map/ppermute | solution.py:84
  89.9 0.7 copy-start.2
  90.6 5.9 %copy-start.3 = (s32[4]{0:T(128)S(1)}, s32[4]{0:T(128)}, u32[]{:S(2)}) copy-start(s32[4]{0:T(128)} %param.10) | copy-start | bytes 52
  138.3 40.3 %collective-permute-start.5 = (f32[512,1024]{1,0:T(8,128)}, f32[512,1024]{1,0:T(8,128)S(1)}, u32[]{:S(2)}, u32[]{:S(2)}) collective-permute-start(f32[512,1024]{1,0:T(8,128)} %all-gather.3.cloned.1.call-done), channel_id=1, source_target_pairs={{0,1},{1,0},{2,3},{3,2},{4,5},{5,4},{6,7},{7,6},{8,9},{9,8},{10,11... | collective-permute-start | bytes 6291464 | tf_op jit(solution)/shard_map/ppermute | solution.py:84
  174.6 2.5 copy-start.1
Sparse Core Ops, SparseCore 0:
  13.7 35.9 all-gather.4
  90.7 47.5 all-gather.2

commit v5 on v4

--- a/solution.py
+++ b/solution.py
@@ -80,8 +80,8 @@
     )(gram, start)
 
 
-def _swap(x, flip):
-    return lax.ppermute(x, "seq", [(i, i ^ flip) for i in range(lax.axis_size("seq"))])
+def _swap(x, flip, axis="seq"):
+    return lax.ppermute(x, axis, [(i, i ^ flip) for i in range(lax.axis_size(axis))])
 
 
 def _halve(x, bit, flip):
@@ -91,25 +91,31 @@
     return keep + _swap(send, flip)
 
 
-def _double(x, bit, flip):
-    other = _swap(x, flip)
+def _double(x, bit, flip, axis="seq"):
+    other = _swap(x, flip, axis)
     rows = x.shape[0]
     out = jnp.zeros((2 * rows,) + x.shape[1:], x.dtype)
     out = lax.dynamic_update_slice_in_dim(out, x, bit * rows, 0)
     return lax.dynamic_update_slice_in_dim(out, other, (1 - bit) * rows, 0)
 
 
-def sum_gram(local_gram):
+def sum_gram(local_gram, early, late):
     seq = lax.axis_index("seq")
+    kv = lax.axis_index("kv")
     kv_size = lax.axis_size("kv")
     core, z_low, z_high = seq % 2, (seq // 2) % 2, (seq // 4) % 2
     s = _halve(local_gram, core, 1)
     s = lax.all_to_all(s.reshape((kv_size, -1) + s.shape[1:]), "kv", 0, 0, tiled=True)
+    s, early = lax.optimization_barrier((s, early))
     s = jnp.sum(s, axis=0)
     s = _halve(_halve(s, z_high, 4), z_low, 2)
     s = _double(_double(s, z_low, 2), z_high, 4)
-    s = lax.all_gather(s, "kv", axis=0, tiled=True)
-    return _double(s, core, 1)
+    flip = 1
+    while flip < kv_size:
+        s = _double(s, (kv // flip) % 2, flip, "kv")
+        flip *= 2
+    s, late = lax.optimization_barrier((s, late))
+    return _double(s, core, 1), early, late
 
 
 def local(prefill_keys, queries, outlier_spans, start_basis):
@@ -141,7 +147,7 @@
     local_gram = lax.dot_general(
         prefill_keys, prefill_keys, (((0,), (0,)), ((), ())), preferred_element_type=jnp.float32
     ) * inverse_tokens
-    gram = sum_gram(local_gram)
+    gram, outlier_scores, landmark_scores = sum_gram(local_gram, outlier_scores, landmark_scores)
     subspace = iterate(gram, start_basis)
     rounded = subspace.astype(jnp.bfloat16)
     coefficients = lax.dot_general(

time: 337 us -> 368 us (1.092)
  waiting for transfers between devices: 44.3 us -> 71.5 us
  blocking collectives: 19.3 us -> 15.1 us
  starting transfers between devices: 20.3 us -> 24.5 us
    ppermute x6 -> x10, waiting for transfers between devices: 10.7 us -> 49.9 us  [_swap(): lax.ppermute(x, axis, [(i, i ^ flip) for i in range(lax.axis_size(axis))])]
    all_to_all x1, waiting for transfers between devices: 32 us -> 21.6 us  [sum_gram(): lax.all_to_all(s.reshape((kv_size, -1) + s.shape[1:]), 'kv', 0, 0, tiled=...]
    ppermute x6 -> x10, starting transfers between devices: 13.4 us -> 17.7 us  [_swap(): lax.ppermute(x, axis, [(i, i ^ flip) for i in range(lax.axis_size(axis))])]
    all_gather x1, blocking collectives: 19.3 us -> 15.1 us  [local(): lax.all_gather(picked, 'seq', axis=0, tiled=True)]
  transfers between devices with their start and end apart: 9 -> 12, of which waited for: 7 -> 9; matrix products, arithmetic and copies ran while one was open for 23% -> 10% of each run, Pallas kernels for 0% -> 0%
where the time goes in v5:
time: 368 us; the launch traced here: 367 us
  Pallas kernels  145 us (39%)
  waiting for transfers between devices  71.5 us (19%)
  matrix products  44.4 us (12%)
  local copies, waits for them, and re-layouts  35.7 us (10%)
  starting transfers between devices  24.5 us (7%)
  other arithmetic  16 us (4%)
  blocking collectives  15.1 us (4%)
  between operations  14.4 us (4%)
    pallas_call x1, Pallas kernels, iterate(): pl.pallas_call(_iterate_kernel, out_shape=jax.ShapeDtypeStruct(start.shap...  145 us
    ppermute x10, waiting for transfers between devices, _swap(): lax.ppermute(x, axis, [(i, i ^ flip) for i in range(lax.axis_size(axis))])  49.9 us
    dot_general x16, matrix products, one_head(): jnp.einsum('qgd,cd->qgc', query_group, key_group, preferred_element_type=...  29.6 us
    all_to_all x1, waiting for transfers between devices, sum_gram(): lax.all_to_all(s.reshape((kv_size, -1) + s.shape[1:]), 'kv', 0, 0, tiled=...  21.6 us
    ppermute x10, starting transfers between devices, _swap(): lax.ppermute(x, axis, [(i, i ^ flip) for i in range(lax.axis_size(axis))])  17.7 us
    all_gather x1, blocking collectives, local(): lax.all_gather(picked, 'seq', axis=0, tiled=True)  15.1 us
    dot_general x1, matrix products, local(): lax.dot_general(prefill_keys, prefill_keys, (((0,), (0,)), ((), ())), pre...  10 us
    dynamic_update_slice x16, local copies, waits for them, and re-layouts, score_rows(): lax.map(one_head, (query_heads, key_heads)) * scale_factor  8.7 us
  transfers between devices with their start and end apart: 12, of which 9 were waited for; matrix products, arithmetic and copies ran while one was open for 10% of the time, Pallas kernels for 0%

profile of v5, /device:TPU:1, one launch (start us, length us, event | category | flops | bytes accessed | tf_op | source)
XLA Modules:
  0.0 366.7 jit_solution(1751271226651780901)
XLA Ops:
  7.2 10.0 %convolution_multiply_fusion = f32[1024,1024]{1,0:T(8,128)} fusion(bf16[2048,1024]{1,0:T(8,128)(2,1)} %param.8), kind=kOutput, calls=%fused_computation.18 | convolution fusion | flops 4296015872 | bytes 8388608 | tf_op jit(solution)/shard_map/dot_general | solution.py:147
  17.3 3.3 constant_dynamic-slice_fusion.2
  20.6 1.4 collective-permute-start
  22.0 3.2 convert_reduce_fusion
  26.2 3.2 copy.19
  29.4 2.6 copy.21
  32.3 2.7 gather_fusion
  35.1 15.1 %all_gather.6 = bf16[256,1024]{1,0:T(8,128)(2,1)S(1)} all-gather(bf16[32,1024]{1,0:T(8,128)(2,1)S(1)} %bitcast_select_fusion), channel_id=1, replica_groups=mesh['kv'=16,'seq'=8] {'seq'}, dimensions={0}, use_global_device_ids=true | all-gather | bytes 589824 | tf_op jit(solution)/shard_map/all_gather | solution.py:146
  51.2 4.2 %dynamic-slice_add_fusion = f32[512,1024]{1,0:T(8,128)} fusion(f32[512,1024]{1,0:T(8,128)} %collective-permute-done, f32[1024,1024]{1,0:T(8,128)} %convolution_multiply_fusion, s32[]{:T(128)S(6)} %select_n.107), kind=kLoop, calls=%fused_computation.19 | loop fusion | flops 524288 | bytes 6291460 | tf_op jit(solution)/shard_map/add | solution.py:91
  55.4 6.8 %all-to-all-start = ((f32[16,32,1024]{2,1,0:T(8,128)}), f32[16,32,1024]{2,1,0:T(8,128)S(1)}, u32[]{:S(2)}, u32[]{:S(2)}) async-start(f32[16,32,1024]{2,1,0:T(8,128)} %bitcast.8), calls=%async_computation | async-start | bytes 4194304 | tf_op jit(solution)/shard_map/all_to_all | solution.py:108
  62.2 10.3 %while.20 = (s32[]{:T(128)}, f32[8,128,256]{2,1,0:T(8,128)S(1)}, bf16[8,128,8,128]{3,1,2,0:T(8,128)(2,1)}, bf16[8,256,128]{1,2,0:T(8,128)(2,1)}, s32[]{:T(128)}) while((s32[]{:T(128)}, f32[8,128,256]{2,1,0:T(8,128)S(1)}, bf16[8,128,8,128]{3,1,2,0:T(8,128)(2,1)}, bf16[8,256,128]{1,2,0:T(8,128)(2,1)}, s32[]{:T(128)}) %tuple.56), condition=%wide.region_2.3_spmd, body=%wide.region_0.2_spmd.sunk | while | flops 67338240 | bytes 721985 | solution.py:143
  62.2 1.3 convolution_reduce_fusion.4
  64.8 1.2 convolution_reduce_fusion.4
  66.1 1.2 convolution_reduce_fusion.4
  67.4 1.2 convolution_reduce_fusion.4
  68.7 1.2 convolution_reduce_fusion.4
  70.0 1.2 convolution_reduce_fusion.4
  73.5 21.6 %all-to-all-done = f32[16,32,1024]{2,1,0:T(8,128)S(1)} async-done(((f32[16,32,1024]{2,1,0:T(8,128)}), f32[16,32,1024]{2,1,0:T(8,128)S(1)}, u32[]{:S(2)}, u32[]{:S(2)}) %all-to-all-start) | async-done | bytes 2097184 | tf_op jit(solution)/shard_map/all_to_all | solution.py:108
  95.2 1.3 collective-permute-start.1
  96.5 3.4 collective-permute-done.1
  99.9 1.5 collective-permute-start.2
  101.4 1.3 collective-permute-done.2
  102.8 1.5 collective-permute-start.3
  104.3 1.9 collective-permute-done.3
  106.2 2.0 collective-permute-start.4
  108.3 2.6 collective-permute-done.4
  111.1 4.0 %collective-permute-done.5 = f32[32,1024]{1,0:T(8,128)S(1)} collective-permute-done((f32[32,1024]{1,0:T(8,128)S(1)}, f32[32,1024]{1,0:T(8,128)S(1)}, u32[]{:S(2)}, u32[]{:S(2)}) %collective-permute-start.5) | collective-permute-done | bytes 131104 | tf_op jit(solution)/shard_map/ppermute | solution.py:84
  115.3 7.9 %collective-permute-done.6 = f32[64,1024]{1,0:T(8,128)S(1)} collective-permute-done((f32[64,1024]{1,0:T(8,128)S(1)}, f32[64,1024]{1,0:T(8,128)S(1)}, u32[]{:S(2)}, u32[]{:S(2)}) %collective-permute-start.6) | collective-permute-done | bytes 262176 | tf_op jit(solution)/shard_map/ppermute | solution.py:84
  123.5 7.8 %collective-permute-done.7 = f32[128,1024]{1,0:T(8,128)S(1)} collective-permute-done((f32[128,1024]{1,0:T(8,128)S(1)}, f32[128,1024]{1,0:T(8,128)S(1)}, u32[]{:S(2)}, u32[]{:S(2)}) %collective-permute-start.7) | collective-permute-done | bytes 524320 | tf_op jit(solution)/shard_map/ppermute | solution.py:84
  132.1 20.9 %collective-permute-done.8 = f32[256,1024]{1,0:T(8,128)} collective-permute-done((f32[256,1024]{1,0:T(8,128)S(1)}, f32[256,1024]{1,0:T(8,128)}, u32[]{:S(2)}, u32[]{:S(2)}) %collective-permute-start.8) | collective-permute-done | bytes 1048608 | tf_op jit(solution)/shard_map/ppermute | solution.py:84
  153.0 1.3 constant_dynamic-update-slice_fusion.2
  154.4 6.4 %copy.23 = bf16[2048,1024]{0,1:T(8,128)(2,1)} copy(bf16[2048,1024]{1,0:T(8,128)(2,1)} %all-gather.2.cloned.1.call-done) | data formatting | bytes 8388608 | tf_op jit(solution)/shard_map/all_gather | solution.py:145
  160.8 28.3 %while.21 = (s32[]{:T(128)}, f32[8,128,2048]{2,1,0:T(8,128)}, bf16[8,128,8,128]{3,1,2,0:T(8,128)(2,1)}, bf16[8,2048,128]{1,2,0:T(8,128)(2,1)}, s32[]{:T(128)}) while((s32[]{:T(128)}, f32[8,128,2048]{2,1,0:T(8,128)}, bf16[8,128,8,128]{3,1,2,0:T(8,128)(2,1)}, bf16[8,2048,128]{1,2,0:T(8,128)(2,1)}, s32[]{:T(128)}) %tuple.55), condition=%wide.region_7.8_spmd, body=%wide.region_5.7_spmd.sunk | while | flops 538705920 | bytes 3933757 | solution.py:143
  160.8 2.5 convolution_reduce_fusion.5
  164.3 2.5 convolution_reduce_fusion.5
  167.9 2.5 convolution_reduce_fusion.5
  171.4 2.5 convolution_reduce_fusion.5
  174.9 2.5 convolution_reduce_fusion.5
  178.4 2.5 convolution_reduce_fusion.5
  182.0 2.5 convolution_reduce_fusion.5
  185.5 2.5 convolution_reduce_fusion.5
  189.1 6.6 %multiply_convert_fusion = bf16[8,128,2048]{2,1,0:T(8,128)(2,1)} fusion(f32[8,128,2048]{2,1,0:T(8,128)} %get-tuple-element.54), kind=kLoop, calls=%fused_computation.15 | loop fusion | flops 4194304 | bytes 12582912 | tf_op jit(solution)/shard_map/convert_element_type | solution.py:143
  195.6 9.3 %collective-permute-start.9 = (f32[512,1024]{1,0:T(8,128)S(1)}, f32[512,1024]{1,0:T(8,128)S(1)}, u32[]{:S(2)}, u32[]{:S(2)}) collective-permute-start(f32[512,1024]{1,0:T(8,128)S(1)} %constant_dynamic-update-slice_fusion.2), channel_id=1, source_target_pairs={{0,1},{1,0},{2,3},{3,2},{4,5},{5,4},{6,7},{7,6},{8,9},{9,8},{10,11... | collective-permute-start | bytes 6291464 | tf_op jit(solution)/shard_map/ppermute | solution.py:84
  204.9 2.5 broadcast_in_dim.51
  207.4 1.4 constant_dynamic-update-slice_fusion.1
  208.8 1.5 constant_dynamic-update-slice_fusion.g_ref
  210.3 144.8 %shard_map.75 = f32[160,1024]{1,0:T(8,128)} custom-call(f32[1024,1024]{1,0:T(8,128)} %constant_dynamic-update-slice_fusion.g_ref, f32[160,1024]{1,0:T(8,128)} %s_ref.1), custom_call_target="tpu_custom_call" | custom-call | tf_op jit(solution)/shard_map/pallas_call | solution.py:71
  355.1 4.8 %convolution_convert_fusion = bf16[160,2048]{1,0:T(8,128)(2,1)} fusion(bf16[2048,1024]{1,0:T(8,128)(2,1)} %param.8, f32[160,1024]{1,0:T(8,128)} %shard_map.75), kind=kOutput, calls=%fused_computation.17 | convolution fusion | flops 671580160 | bytes 5505024 | tf_op jit(solution)/shard_map/dot_general | solution.py:153
  (63 shorter events, 15.8 us)
Async XLA Ops:
  7.2 147.2 %all-gather.2.cloned.1.call-start = ((), (), s32[]{:S(2)}) async-start(), calls=%async_computation.1 | async-start | bytes 4718592 | tf_op jit(solution)/shard_map/all_gather | solution.py:145
  17.3 4.8 %copy-start = (bf16[2048,1024]{1,0:T(8,128)(2,1)S(1)}, bf16[2048,1024]{1,0:T(8,128)(2,1)}, u32[]{:S(2)}) copy-start(bf16[2048,1024]{1,0:T(8,128)(2,1)} %param.8) | copy-start | bytes 12582916
  20.6 30.6 %collective-permute-start = (f32[512,1024]{1,0:T(8,128)}, f32[512,1024]{1,0:T(8,128)}, u32[]{:S(2)}, u32[]{:S(2)}) collective-permute-start(f32[512,1024]{1,0:T(8,128)} %constant_dynamic-slice_fusion.2), channel_id=1, source_target_pairs={{0,1},{1,0},{2,3},{3,2},{4,5},{5,4},{6,7},{7,6},{8,9},{9,8},{10,11... | collective-permute-start | bytes 6291464 | tf_op jit(solution)/shard_map/ppermute | solution.py:84
  26.2 5.9 %copy-start.1 = (s32[4]{0:T(128)S(1)}, s32[4]{0:T(128)}, u32[]{:S(2)}) copy-start(s32[4]{0:T(128)} %param.10) | copy-start | bytes 52
  55.4 39.6 %all-to-all-start = ((f32[16,32,1024]{2,1,0:T(8,128)}), f32[16,32,1024]{2,1,0:T(8,128)S(1)}, u32[]{:S(2)}, u32[]{:S(2)}) async-start(f32[16,32,1024]{2,1,0:T(8,128)} %bitcast.8), calls=%async_computation | async-start | bytes 4194304 | tf_op jit(solution)/shard_map/all_to_all | solution.py:108
  95.2 4.7 %collective-permute-start.1 = (f32[16,1024]{1,0:T(8,128)S(1)}, f32[16,1024]{1,0:T(8,128)S(1)}, u32[]{:S(2)}, u32[]{:S(2)}) collective-permute-start(f32[16,1024]{1,0:T(8,128)S(1)} %constant_dynamic-slice_fusion.1), channel_id=1, source_target_pairs={{0,4},{1,5},{2,6},{3,7},{4,0},{5,1},{6,2},{7,3},{8,12},{9,13},{10,... | collective-permute-start | bytes 196616 | tf_op jit(solution)/shard_map/ppermute | solution.py:84
  99.9 2.8 collective-permute-start.2
  102.8 3.5 collective-permute-start.3
  106.2 4.6 %collective-permute-start.4 = (f32[16,1024]{1,0:T(8,128)S(1)}, f32[16,1024]{1,0:T(8,128)S(1)}, u32[]{:S(2)}, u32[]{:S(2)}) collective-permute-start(f32[16,1024]{1,0:T(8,128)S(1)} %constant_dynamic-update-slice_fusion.12), channel_id=1, source_target_pairs={{0,4},{1,5},{2,6},{3,7},{4,0},{5,1},{6,2},{7,3},{8,12},{9,13},{10,... | collective-permute-start | bytes 196616 | tf_op jit(solution)/shard_map/ppermute | solution.py:84
  110.9 4.2 %collective-permute-start.5 = (f32[32,1024]{1,0:T(8,128)S(1)}, f32[32,1024]{1,0:T(8,128)S(1)}, u32[]{:S(2)}, u32[]{:S(2)}) collective-permute-start(f32[32,1024]{1,0:T(8,128)S(1)} %constant_dynamic-update-slice_fusion.10), channel_id=1, source_target_pairs={{0,8},{8,0},{16,24},{24,16},{32,40},{40,32},{48,56},{56,48},{64,72... | collective-permute-start | bytes 393224 | tf_op jit(solution)/shard_map/ppermute | solution.py:84
  115.1 8.1 %collective-permute-start.6 = (f32[64,1024]{1,0:T(8,128)S(1)}, f32[64,1024]{1,0:T(8,128)S(1)}, u32[]{:S(2)}, u32[]{:S(2)}) collective-permute-start(f32[64,1024]{1,0:T(8,128)S(1)} %constant_dynamic-update-slice_fusion.8), channel_id=1, source_target_pairs={{0,16},{8,24},{16,0},{24,8},{32,48},{40,56},{48,32},{56,40},{64,80... | collective-permute-start | bytes 786440 | tf_op jit(solution)/shard_map/ppermute | solution.py:84
  123.2 8.1 %collective-permute-start.7 = (f32[128,1024]{1,0:T(8,128)S(1)}, f32[128,1024]{1,0:T(8,128)S(1)}, u32[]{:S(2)}, u32[]{:S(2)}) collective-permute-start(f32[128,1024]{1,0:T(8,128)S(1)} %constant_dynamic-update-slice_fusion.6), channel_id=1, source_target_pairs={{0,32},{8,40},{16,48},{24,56},{32,0},{40,8},{48,16},{56,24},{64,96... | collective-permute-start | bytes 1572872 | tf_op jit(solution)/shard_map/ppermute | solution.py:84
  131.4 21.7 %collective-permute-start.8 = (f32[256,1024]{1,0:T(8,128)S(1)}, f32[256,1024]{1,0:T(8,128)}, u32[]{:S(2)}, u32[]{:S(2)}) collective-permute-start(f32[256,1024]{1,0:T(8,128)S(1)} %constant_dynamic-update-slice_fusion.4), channel_id=1, source_target_pairs={{0,64},{8,72},{16,80},{24,88},{32,96},{40,104},{48,112},{56,120},{... | collective-permute-start | bytes 3145736 | tf_op jit(solution)/shard_map/ppermute | solution.py:84
  195.6 13.2 %collective-permute-start.9 = (f32[512,1024]{1,0:T(8,128)S(1)}, f32[512,1024]{1,0:T(8,128)S(1)}, u32[]{:S(2)}, u32[]{:S(2)}) collective-permute-start(f32[512,1024]{1,0:T(8,128)S(1)} %constant_dynamic-update-slice_fusion.2), channel_id=1, source_target_pairs={{0,1},{1,0},{2,3},{3,2},{4,5},{5,4},{6,7},{7,6},{8,9},{9,8},{10,11... | collective-permute-start | bytes 6291464 | tf_op jit(solution)/shard_map/ppermute | solution.py:84
Sparse Core Ops, SparseCore 0:
  26.3 36.0 all-gather.1

commit v6 on v5

--- a/solution.py
+++ b/solution.py
@@ -101,7 +101,6 @@
 
 def sum_gram(local_gram, early, late):
     seq = lax.axis_index("seq")
-    kv = lax.axis_index("kv")
     kv_size = lax.axis_size("kv")
     core, z_low, z_high = seq % 2, (seq // 2) % 2, (seq // 4) % 2
     s = _halve(local_gram, core, 1)
@@ -110,10 +109,7 @@
     s = jnp.sum(s, axis=0)
     s = _halve(_halve(s, z_high, 4), z_low, 2)
     s = _double(_double(s, z_low, 2), z_high, 4)
-    flip = 1
-    while flip < kv_size:
-        s = _double(s, (kv // flip) % 2, flip, "kv")
-        flip *= 2
+    s = lax.all_gather(s, "kv", axis=0, tiled=True)
     s, late = lax.optimization_barrier((s, late))
     return _double(s, core, 1), early, late
 
@@ -147,7 +143,7 @@
     local_gram = lax.dot_general(
         prefill_keys, prefill_keys, (((0,), (0,)), ((), ())), preferred_element_type=jnp.float32
     ) * inverse_tokens
-    gram, outlier_scores, landmark_scores = sum_gram(local_gram, outlier_scores, landmark_scores)
+    gram, landmark_scores, outlier_scores = sum_gram(local_gram, landmark_scores, outlier_scores)
     subspace = iterate(gram, start_basis)
     rounded = subspace.astype(jnp.bfloat16)
     coefficients = lax.dot_general(

time: 368 us -> 319 us (0.87)
  waiting for transfers between devices: 71.5 us -> 33.9 us
  starting transfers between devices: 24.5 us -> 13 us
    ppermute x10 -> x6, waiting for transfers between devices: 49.9 us -> 11.8 us  [_swap(): lax.ppermute(x, axis, [(i, i ^ flip) for i in range(lax.axis_size(axis))])]
    all_to_all x1, waiting for transfers between devices: 21.6 us -> 0.01 us  [sum_gram(): lax.all_to_all(s.reshape((kv_size, -1) + s.shape[1:]), 'kv', 0, 0, tiled=...]
    all_gather x0 -> x1, waiting for transfers between devices: none -> 15.6 us  [sum_gram(): s = lax.all_gather(s, 'kv', axis=0, tiled=True)]
    ppermute x10 -> x6, starting transfers between devices: 17.7 us -> 6.13 us  [_swap(): lax.ppermute(x, axis, [(i, i ^ flip) for i in range(lax.axis_size(axis))])]
    all_gather x1, waiting for transfers between devices: 0.02 us -> 6.47 us  [local(): lax.all_gather(landmarks, 'seq', axis=0, tiled=True)]
  transfers between devices with their start and end apart: 12 -> 9, of which waited for: 9 -> 7; matrix products, arithmetic and copies ran while one was open for 10% -> 25% of each run, Pallas kernels for 0% -> 0%
where the time goes in v6:
time: 319 us; the launch traced here: 318 us
  Pallas kernels  145 us (45%)
  matrix products  42 us (13%)
  waiting for transfers between devices  33.9 us (11%)
  local copies, waits for them, and re-layouts  33.8 us (11%)
  other arithmetic  18.2 us (6%)
  blocking collectives  18 us (6%)
  between operations  14.2 us (4%)
  starting transfers between devices  13 us (4%)
    pallas_call x1, Pallas kernels, iterate(): pl.pallas_call(_iterate_kernel, out_shape=jax.ShapeDtypeStruct(start.shap...  145 us
    dot_general x16, matrix products, one_head(): jnp.einsum('qgd,cd->qgc', query_group, key_group, preferred_element_type=...  29.6 us
    all_gather x1, blocking collectives, local(): lax.all_gather(picked, 'seq', axis=0, tiled=True)  18 us
    all_gather x1, waiting for transfers between devices, sum_gram(): s = lax.all_gather(s, 'kv', axis=0, tiled=True)  15.6 us
    ppermute x6, waiting for transfers between devices, _swap(): lax.ppermute(x, axis, [(i, i ^ flip) for i in range(lax.axis_size(axis))])  11.8 us
    dynamic_update_slice x16, local copies, waits for them, and re-layouts, score_rows(): lax.map(one_head, (query_heads, key_heads)) * scale_factor  8.68 us
    dot_general x1, matrix products, local(): lax.dot_general(prefill_keys, prefill_keys, (((0,), (0,)), ((), ())), pre...  7.63 us
    convert_element_type x2, other arithmetic, score_rows(): (lax.map(one_head, (query_heads, key_heads)) * scale_factor).astype(jnp.b...  7.49 us
  transfers between devices with their start and end apart: 9, of which 7 were waited for; matrix products, arithmetic and copies ran while one was open for 25% of the time, Pallas kernels for 0%

profile of v6, /device:TPU:1, one launch (start us, length us, event | category | flops | bytes accessed | tf_op | source)
XLA Modules:
  0.0 318.3 jit_solution(17187601431199723692)
XLA Ops:
  7.2 5.5 %convert_reduce_fusion = f32[256,1024]{1,0:T(8,128)S(1)} fusion(bf16[2048,1024]{1,0:T(8,128)(2,1)} %param.8), kind=kLoop, calls=%fused_computation.16 | loop fusion | flops 3932160 | bytes 5242880 | tf_op jit(solution)/shard_map/reduce_sum | solution.py:123
  13.6 7.6 %convolution_multiply_fusion = f32[1024,1024]{1,0:T(8,128)S(1)} fusion(bf16[2048,1024]{1,0:T(8,128)(2,1)} %param.8), kind=kOutput, calls=%fused_computation.18 | convolution fusion | flops 4296015872 | bytes 8388608 | tf_op jit(solution)/shard_map/dot_general | solution.py:143
  21.2 2.0 copy-done
  23.3 1.6 constant_dynamic-slice_fusion.2
  24.8 1.4 collective-permute-start
  26.2 3.3 %copy.19 = bf16[128,8192]{0,1:T(8,128)(2,1)S(1)} copy(bf16[128,8192]{1,0:T(8,128)(2,1)} %param.9) | data formatting | bytes 4194304 | tf_op args[1]
  29.5 2.7 copy.21
  32.2 4.2 %dynamic-slice_add_fusion = f32[512,1024]{1,0:T(8,128)} fusion(f32[512,1024]{1,0:T(8,128)} %collective-permute-done, f32[1024,1024]{1,0:T(8,128)} %copy-done, s32[]{:T(128)S(6)} %select_n.57), kind=kLoop, calls=%fused_computation.19 | loop fusion | flops 524288 | bytes 6291460 | tf_op jit(solution)/shard_map/add | solution.py:91
  36.3 6.8 %all-to-all-start = ((f32[16,32,1024]{2,1,0:T(8,128)}), f32[16,32,1024]{2,1,0:T(8,128)S(1)}, u32[]{:S(2)}, u32[]{:S(2)}) async-start(f32[16,32,1024]{2,1,0:T(8,128)} %bitcast.8), calls=%async_computation | async-start | bytes 4194304 | tf_op jit(solution)/shard_map/all_to_all | solution.py:107
  43.2 6.5 %all-gather.3.cloned.1.call-done = bf16[2048,1024]{1,0:T(8,128)(2,1)} async-done(((bf16[256,1024]{1,0:T(8,128)(2,1)}), bf16[2048,1024]{1,0:T(8,128)(2,1)}) %all-gather.3.cloned.1.call-update) | async-done | bytes 4194320 | tf_op jit(solution)/shard_map/all_gather | solution.py:141
  49.7 6.4 %copy.20 = bf16[2048,1024]{0,1:T(8,128)(2,1)} copy(bf16[2048,1024]{1,0:T(8,128)(2,1)} %all-gather.3.cloned.1.call-done) | data formatting | bytes 8388608 | tf_op jit(solution)/shard_map/all_gather | solution.py:141
  56.1 28.2 %while.20 = (s32[]{:T(128)}, f32[8,128,2048]{2,1,0:T(8,128)}, bf16[8,128,8,128]{3,1,2,0:T(8,128)(2,1)}, bf16[8,2048,128]{1,2,0:T(8,128)(2,1)}, s32[]{:T(128)}) while((s32[]{:T(128)}, f32[8,128,2048]{2,1,0:T(8,128)}, bf16[8,128,8,128]{3,1,2,0:T(8,128)(2,1)}, bf16[8,2048,128]{1,2,0:T(8,128)(2,1)}, s32[]{:T(128)}) %tuple.56), condition=%wide.region_3.4_spmd, body=%wide.region_1.0_spmd.sunk | while | flops 538705920 | bytes 3933757 | solution.py:139
  56.1 2.5 convolution_reduce_fusion.4
  59.6 2.5 convolution_reduce_fusion.4
  62.1 1.1 bitcast_dynamic-update-slice_fusion.4
  63.2 2.5 convolution_reduce_fusion.4
  66.7 2.5 convolution_reduce_fusion.4
  70.2 2.5 convolution_reduce_fusion.4
  73.7 2.5 convolution_reduce_fusion.4
  76.2 1.1 bitcast_dynamic-update-slice_fusion.4
  77.3 2.5 convolution_reduce_fusion.4
  80.8 2.5 convolution_reduce_fusion.4
  83.3 1.1 bitcast_dynamic-update-slice_fusion.4
  84.4 6.6 %multiply_convert_fusion = bf16[8,128,2048]{2,1,0:T(8,128)(2,1)} fusion(f32[8,128,2048]{2,1,0:T(8,128)} %get-tuple-element.52), kind=kLoop, calls=%fused_computation.15 | loop fusion | flops 4194304 | bytes 12582912 | tf_op jit(solution)/shard_map/convert_element_type | solution.py:139
  91.1 1.5 collective-permute-start.1
  92.6 3.2 %collective-permute-done.1 = f32[16,1024]{1,0:T(8,128)S(1)} collective-permute-done((f32[16,1024]{1,0:T(8,128)S(1)}, f32[16,1024]{1,0:T(8,128)S(1)}, u32[]{:S(2)}, u32[]{:S(2)}) %collective-permute-start.1) | collective-permute-done | bytes 65568 | tf_op jit(solution)/shard_map/ppermute | solution.py:84
  96.0 2.7 collective-permute-done.2
  98.9 2.7 collective-permute-done.3
  101.5 1.4 collective-permute-start.4
  103.0 3.2 %collective-permute-done.4 = f32[16,1024]{1,0:T(8,128)S(1)} collective-permute-done((f32[16,1024]{1,0:T(8,128)S(1)}, f32[16,1024]{1,0:T(8,128)S(1)}, u32[]{:S(2)}, u32[]{:S(2)}) %collective-permute-start.4) | collective-permute-done | bytes 65568 | tf_op jit(solution)/shard_map/ppermute | solution.py:84
  107.1 2.7 gather_fusion
  109.9 18.0 %all_gather.11 = bf16[256,1024]{1,0:T(8,128)(2,1)S(1)} all-gather(bf16[32,1024]{1,0:T(8,128)(2,1)S(1)} %bitcast_select_fusion), channel_id=1, replica_groups=mesh['kv'=16,'seq'=8] {'seq'}, dimensions={0}, use_global_device_ids=true | all-gather | bytes 589824 | tf_op jit(solution)/shard_map/all_gather | solution.py:142
  128.1 10.4 %while.21 = (s32[]{:T(128)}, f32[8,128,256]{2,1,0:T(8,128)S(1)}, bf16[8,128,8,128]{3,1,2,0:T(8,128)(2,1)}, bf16[8,256,128]{1,2,0:T(8,128)(2,1)S(1)}, s32[]{:T(128)}) while((s32[]{:T(128)}, f32[8,128,256]{2,1,0:T(8,128)S(1)}, bf16[8,128,8,128]{3,1,2,0:T(8,128)(2,1)}, bf16[8,256,128]{1,2,0:T(8,128)(2,1)S(1)}, s32[]{:T(128)}) %tuple.58), condition=%wide.region_7.8_spmd, body=%wide.region_5.7_spmd.sunk | while | flops 67338240 | bytes 721985 | solution.py:139
  128.1 1.2 convolution_reduce_fusion.5
  129.4 1.3 convolution_reduce_fusion.5
  130.7 1.2 convolution_reduce_fusion.5
  132.0 1.3 convolution_reduce_fusion.5
  133.3 1.3 convolution_reduce_fusion.5
  134.6 1.3 convolution_reduce_fusion.5
  135.9 1.3 convolution_reduce_fusion.5
  137.2 1.3 convolution_reduce_fusion.5
  139.4 15.6 %all-gather.5.cloned.1.call-done = f32[512,1024]{1,0:T(8,128)} async-done(((f32[32,1024]{1,0:T(8,128)}), f32[512,1024]{1,0:T(8,128)}) %all-gather.5.cloned.1.call-update) | async-done | bytes 2097168 | tf_op jit(solution)/shard_map/all_gather | solution.py:112
  155.0 1.5 collective-permute-start.5
  156.5 2.5 broadcast_in_dim.39
  158.9 1.5 constant_dynamic-update-slice_fusion.1
  160.5 1.5 constant_dynamic-update-slice_fusion.g_ref
  161.9 144.8 %shard_map.75 = f32[160,1024]{1,0:T(8,128)} custom-call(f32[1024,1024]{1,0:T(8,128)} %constant_dynamic-update-slice_fusion.g_ref, f32[160,1024]{1,0:T(8,128)} %s_ref.1), custom_call_target="tpu_custom_call" | custom-call | tf_op jit(solution)/shard_map/pallas_call | solution.py:71
  306.7 4.8 %convolution_convert_fusion = bf16[160,2048]{1,0:T(8,128)(2,1)} fusion(bf16[2048,1024]{1,0:T(8,128)(2,1)} %param.8, f32[160,1024]{1,0:T(8,128)} %shard_map.75), kind=kOutput, calls=%fused_computation.17 | convolution fusion | flops 671580160 | bytes 5505024 | tf_op jit(solution)/shard_map/dot_general | solution.py:149
  (50 shorter events, 9.0 us)
Async XLA Ops:
  7.2 42.5 %all-gather.3.cloned.1.call-start = ((), (), s32[]{:S(2)}) async-start(), calls=%async_computation.1 | async-start | bytes 4718592 | tf_op jit(solution)/shard_map/all_gather | solution.py:141
  21.2 2.0 copy-start
  24.8 7.4 %collective-permute-start = (f32[512,1024]{1,0:T(8,128)}, f32[512,1024]{1,0:T(8,128)}, u32[]{:S(2)}, u32[]{:S(2)}) collective-permute-start(f32[512,1024]{1,0:T(8,128)} %constant_dynamic-slice_fusion.2), channel_id=1, source_target_pairs={{0,1},{1,0},{2,3},{3,2},{4,5},{5,4},{6,7},{7,6},{8,9},{9,8},{10,11... | collective-permute-start | bytes 6291464 | tf_op jit(solution)/shard_map/ppermute | solution.py:84
  36.3 54.6 %all-to-all-start = ((f32[16,32,1024]{2,1,0:T(8,128)}), f32[16,32,1024]{2,1,0:T(8,128)S(1)}, u32[]{:S(2)}, u32[]{:S(2)}) async-start(f32[16,32,1024]{2,1,0:T(8,128)} %bitcast.8), calls=%async_computation | async-start | bytes 4194304 | tf_op jit(solution)/shard_map/all_to_all | solution.py:107
  43.2 111.8 %all-gather.5.cloned.1.call-start = ((), (), s32[]{:S(2)}) async-start(), calls=%async_computation.2 | async-start | bytes 2228224 | tf_op jit(solution)/shard_map/all_gather | solution.py:112
  84.4 22.5 %copy-start.3 = (s32[4]{0:T(128)S(1)}, s32[4]{0:T(128)}, u32[]{:S(2)}) copy-start(s32[4]{0:T(128)} %param.10) | copy-start | bytes 52
  91.1 4.7 %collective-permute-start.1 = (f32[16,1024]{1,0:T(8,128)S(1)}, f32[16,1024]{1,0:T(8,128)S(1)}, u32[]{:S(2)}, u32[]{:S(2)}) collective-permute-start(f32[16,1024]{1,0:T(8,128)S(1)} %constant_dynamic-slice_fusion.1), channel_id=1, source_target_pairs={{0,4},{1,5},{2,6},{3,7},{4,0},{5,1},{6,2},{7,3},{8,12},{9,13},{10,... | collective-permute-start | bytes 196616 | tf_op jit(solution)/shard_map/ppermute | solution.py:84
  95.8 2.8 collective-permute-start.2
  98.7 2.8 collective-permute-start.3
  101.5 4.6 %collective-permute-start.4 = (f32[16,1024]{1,0:T(8,128)S(1)}, f32[16,1024]{1,0:T(8,128)S(1)}, u32[]{:S(2)}, u32[]{:S(2)}) collective-permute-start(f32[16,1024]{1,0:T(8,128)S(1)} %constant_dynamic-update-slice_fusion.4), channel_id=1, source_target_pairs={{0,4},{1,5},{2,6},{3,7},{4,0},{5,1},{6,2},{7,3},{8,12},{9,13},{10,... | collective-permute-start | bytes 196616 | tf_op jit(solution)/shard_map/ppermute | solution.py:84
  106.2 0.7 copy-start.2
  155.0 4.0 %copy-start.1 = (f32[512,1024]{1,0:T(8,128)S(1)}, f32[512,1024]{1,0:T(8,128)}, u32[]{:S(2)}) copy-start(f32[512,1024]{1,0:T(8,128)} %all-gather.5.cloned.1.call-done) | copy-start | bytes 6291460
  155.0 5.5 %collective-permute-start.5 = (f32[512,1024]{1,0:T(8,128)}, f32[512,1024]{1,0:T(8,128)S(1)}, u32[]{:S(2)}, u32[]{:S(2)}) collective-permute-start(f32[512,1024]{1,0:T(8,128)} %all-gather.5.cloned.1.call-done), channel_id=1, source_target_pairs={{0,1},{1,0},{2,3},{3,2},{4,5},{5,4},{6,7},{7,6},{8,9},{9,8},{10,11... | collective-permute-start | bytes 6291464 | tf_op jit(solution)/shard_map/ppermute | solution.py:84
Sparse Core Ops, SparseCore 0:
  13.7 35.9 all-gather.2
  107.0 47.9 all-gather.4

commit v7 on v6

--- a/solution.py
+++ b/solution.py
@@ -134,9 +134,9 @@
             scores = jnp.einsum(
                 "qgd,cd->qgc", query_group, key_group, preferred_element_type=jnp.float32
             )
-            return jnp.max(scores, axis=1)
+            return (jnp.max(scores, axis=1) * scale_factor).astype(jnp.bfloat16)
 
-        return (lax.map(one_head, (query_heads, key_heads)) * scale_factor).astype(jnp.bfloat16)
+        return lax.map(one_head, (query_heads, key_heads))
 
     landmark_scores = score_rows(lax.all_gather(landmarks, "seq", axis=0, tiled=True))
     outlier_scores = score_rows(lax.all_gather(picked, "seq", axis=0, tiled=True))

time: 319 us -> 311 us (0.975)
  local copies, waits for them, and re-layouts: 33.8 us -> 25.2 us
  other arithmetic: 18.2 us -> 23.1 us
  waiting for transfers between devices: 33.9 us -> 30 us
    dynamic_update_slice x0 -> x16, other arithmetic: none -> 12.3 us  [score_rows(): return lax.map(one_head, (query_heads, key_heads))]
    dynamic_update_slice x16 -> x0, local copies, waits for them, and re-layouts: 8.68 us -> none  [score_rows(): lax.map(one_head, (query_heads, key_heads)) * scale_factor]
    convert_element_type x2 -> x0, other arithmetic: 7.49 us -> none  [score_rows(): (lax.map(one_head, (query_heads, key_heads)) * scale_factor).astype(jnp.b...]
    all_gather x1, waiting for transfers between devices: 15.6 us -> 11.8 us  [sum_gram(): s = lax.all_gather(s, 'kv', axis=0, tiled=True)]
  transfers between devices with their start and end apart: 9 -> 9, of which waited for: 7 -> 7; matrix products, arithmetic and copies ran while one was open for 25% -> 24% of each run, Pallas kernels for 0% -> 0%
where the time goes in v7:
time: 311 us; the launch traced here: 310 us
  Pallas kernels  145 us (47%)
  matrix products  42 us (14%)
  waiting for transfers between devices  30 us (10%)
  local copies, waits for them, and re-layouts  25.2 us (8%)
  other arithmetic  23.1 us (7%)
  blocking collectives  17.8 us (6%)
  between operations  14.2 us (5%)
  starting transfers between devices  13 us (4%)
    pallas_call x1, Pallas kernels, iterate(): pl.pallas_call(_iterate_kernel, out_shape=jax.ShapeDtypeStruct(start.shap...  145 us
    dot_general x16, matrix products, one_head(): jnp.einsum('qgd,cd->qgc', query_group, key_group, preferred_element_type=...  29.6 us
    all_gather x1, blocking collectives, local(): lax.all_gather(picked, 'seq', axis=0, tiled=True)  17.8 us
    dynamic_update_slice x16, other arithmetic, score_rows(): return lax.map(one_head, (query_heads, key_heads))  12.3 us
    ppermute x6, waiting for transfers between devices, _swap(): lax.ppermute(x, axis, [(i, i ^ flip) for i in range(lax.axis_size(axis))])  11.8 us
    all_gather x1, waiting for transfers between devices, sum_gram(): s = lax.all_gather(s, 'kv', axis=0, tiled=True)  11.8 us
    dot_general x1, matrix products, local(): lax.dot_general(prefill_keys, prefill_keys, (((0,), (0,)), ((), ())), pre...  7.7 us
    all_to_all x1, starting transfers between devices, sum_gram(): lax.all_to_all(s.reshape((kv_size, -1) + s.shape[1:]), 'kv', 0, 0, tiled=...  6.84 us
  transfers between devices with their start and end apart: 9, of which 7 were waited for; matrix products, arithmetic and copies ran while one was open for 24% of the time, Pallas kernels for 0%

profile of v7, /device:TPU:1, one launch (start us, length us, event | category | flops | bytes accessed | tf_op | source)
XLA Modules:
  0.0 310.4 jit_solution(5691077476853206774)
XLA Ops:
  7.2 5.5 %convert_reduce_fusion = f32[256,1024]{1,0:T(8,128)S(1)} fusion(bf16[2048,1024]{1,0:T(8,128)(2,1)} %param.8), kind=kLoop, calls=%fused_computation.19 | loop fusion | flops 3932160 | bytes 5242880 | tf_op jit(solution)/shard_map/reduce_sum | solution.py:123
  13.6 7.7 %convolution_multiply_fusion = f32[1024,1024]{1,0:T(8,128)S(1)} fusion(bf16[2048,1024]{1,0:T(8,128)(2,1)} %param.8), kind=kOutput, calls=%fused_computation.21 | convolution fusion | flops 4296015872 | bytes 8388608 | tf_op jit(solution)/shard_map/dot_general | solution.py:143
  21.3 2.0 copy-done
  23.3 1.6 constant_dynamic-slice_fusion.2
  24.9 1.4 collective-permute-start
  26.3 3.3 %copy.19 = bf16[128,8192]{0,1:T(8,128)(2,1)S(1)} copy(bf16[128,8192]{1,0:T(8,128)(2,1)} %param.9) | data formatting | bytes 4194304 | tf_op args[1]
  29.6 2.7 copy.21
  32.2 4.2 %dynamic-slice_add_fusion = f32[512,1024]{1,0:T(8,128)} fusion(f32[512,1024]{1,0:T(8,128)} %collective-permute-done, f32[1024,1024]{1,0:T(8,128)} %copy-done, s32[]{:T(128)S(6)} %select_n.57), kind=kLoop, calls=%fused_computation.22 | loop fusion | flops 524288 | bytes 6291460 | tf_op jit(solution)/shard_map/add | solution.py:91
  36.4 6.8 %all-to-all-start = ((f32[16,32,1024]{2,1,0:T(8,128)}), f32[16,32,1024]{2,1,0:T(8,128)S(1)}, u32[]{:S(2)}, u32[]{:S(2)}) async-start(f32[16,32,1024]{2,1,0:T(8,128)} %bitcast.8), calls=%async_computation | async-start | bytes 4194304 | tf_op jit(solution)/shard_map/all_to_all | solution.py:107
  43.3 6.4 %all-gather.3.cloned.1.call-done = bf16[2048,1024]{1,0:T(8,128)(2,1)} async-done(((bf16[256,1024]{1,0:T(8,128)(2,1)}), bf16[2048,1024]{1,0:T(8,128)(2,1)}) %all-gather.3.cloned.1.call-update) | async-done | bytes 4194320 | tf_op jit(solution)/shard_map/all_gather | solution.py:141
  49.7 6.5 %copy.20 = bf16[2048,1024]{0,1:T(8,128)(2,1)} copy(bf16[2048,1024]{1,0:T(8,128)(2,1)} %all-gather.3.cloned.1.call-done) | data formatting | bytes 8388608 | tf_op jit(solution)/shard_map/all_gather | solution.py:141
  56.2 26.8 %while.20 = (s32[]{:T(128)}, bf16[8,128,2048]{2,1,0:T(8,128)(2,1)}, bf16[8,128,8,128]{3,1,2,0:T(8,128)(2,1)}, bf16[8,2048,128]{1,2,0:T(8,128)(2,1)}, s32[]{:T(128)}) while((s32[]{:T(128)}, bf16[8,128,2048]{2,1,0:T(8,128)(2,1)}, bf16[8,128,8,128]{3,1,2,0:T(8,128)(2,1)}, bf16[8,2048,128]{1,2,0:T(8,128)(2,1)}, s32[]{:T(128)}) %tuple.56), condition=%wide.region_3.4_spmd, body=%wide.region_1.0_spmd.sunk | while | flops 539230208 | bytes 3409469 | solution.py:139
  56.2 2.5 convolution_reduce_fusion.4
  58.7 0.9 fusion.26
  59.6 2.5 convolution_reduce_fusion.4
  62.0 0.9 fusion.26
  62.9 2.5 convolution_reduce_fusion.4
  65.4 0.9 fusion.26
  66.3 2.5 convolution_reduce_fusion.4
  68.8 0.9 fusion.26
  69.6 2.5 convolution_reduce_fusion.4
  73.0 2.5 convolution_reduce_fusion.4
  76.4 2.5 convolution_reduce_fusion.4
  79.7 2.5 convolution_reduce_fusion.4
  83.2 1.5 collective-permute-start.1
  84.7 3.2 %collective-permute-done.1 = f32[16,1024]{1,0:T(8,128)S(1)} collective-permute-done((f32[16,1024]{1,0:T(8,128)S(1)}, f32[16,1024]{1,0:T(8,128)S(1)}, u32[]{:S(2)}, u32[]{:S(2)}) %collective-permute-start.1) | collective-permute-done | bytes 65568 | tf_op jit(solution)/shard_map/ppermute | solution.py:84
  88.1 2.7 collective-permute-done.2
  91.0 2.7 collective-permute-done.3
  93.7 1.4 collective-permute-start.4
  95.1 3.2 %collective-permute-done.4 = f32[16,1024]{1,0:T(8,128)S(1)} collective-permute-done((f32[16,1024]{1,0:T(8,128)S(1)}, f32[16,1024]{1,0:T(8,128)S(1)}, u32[]{:S(2)}, u32[]{:S(2)}) %collective-permute-start.4) | collective-permute-done | bytes 65568 | tf_op jit(solution)/shard_map/ppermute | solution.py:84
  99.2 2.7 gather_fusion
  102.0 17.8 %all_gather.11 = bf16[256,1024]{1,0:T(8,128)(2,1)S(1)} all-gather(bf16[32,1024]{1,0:T(8,128)(2,1)S(1)} %bitcast_select_fusion), channel_id=1, replica_groups=mesh['kv'=16,'seq'=8] {'seq'}, dimensions={0}, use_global_device_ids=true | all-gather | bytes 589824 | tf_op jit(solution)/shard_map/all_gather | solution.py:142
  120.1 15.2 %while.21 = (s32[]{:T(128)}, bf16[8,128,256]{2,1,0:T(8,128)(2,1)}, bf16[8,128,8,128]{3,1,2,0:T(8,128)(2,1)}, bf16[8,256,128]{1,2,0:T(8,128)(2,1)S(1)}, s32[]{:T(128)}) while((s32[]{:T(128)}, bf16[8,128,256]{2,1,0:T(8,128)(2,1)}, bf16[8,128,8,128]{3,1,2,0:T(8,128)(2,1)}, bf16[8,256,128]{1,2,0:T(8,128)(2,1)S(1)}, s32[]{:T(128)}) %tuple.58), condition=%wide.region_7.8_spmd, body=%wide.region_5.7_spmd.sunk | while | flops 67403776 | bytes 656957 | solution.py:139
  120.1 1.2 convolution_reduce_fusion.5
  122.0 1.3 convolution_reduce_fusion.5
  123.9 1.2 convolution_reduce_fusion.5
  125.8 1.2 convolution_reduce_fusion.5
  127.7 1.2 convolution_reduce_fusion.5
  129.6 1.2 convolution_reduce_fusion.5
  131.5 1.2 convolution_reduce_fusion.5
  133.4 1.2 convolution_reduce_fusion.5
  135.3 11.8 %all-gather.5.cloned.1.call-done = f32[512,1024]{1,0:T(8,128)} async-done(((f32[32,1024]{1,0:T(8,128)}), f32[512,1024]{1,0:T(8,128)}) %all-gather.5.cloned.1.call-update) | async-done | bytes 2097168 | tf_op jit(solution)/shard_map/all_gather | solution.py:112
  147.1 1.5 collective-permute-start.5
  148.6 2.5 broadcast_in_dim.35
  151.1 1.5 constant_dynamic-update-slice_fusion.1
  152.6 1.5 constant_dynamic-update-slice_fusion.g_ref
  154.1 144.8 %shard_map.75 = f32[160,1024]{1,0:T(8,128)} custom-call(f32[1024,1024]{1,0:T(8,128)} %constant_dynamic-update-slice_fusion.g_ref, f32[160,1024]{1,0:T(8,128)} %s_ref.1), custom_call_target="tpu_custom_call" | custom-call | tf_op jit(solution)/shard_map/pallas_call | solution.py:71
  298.8 4.8 %convolution_convert_fusion = bf16[160,2048]{1,0:T(8,128)(2,1)} fusion(bf16[2048,1024]{1,0:T(8,128)(2,1)} %param.8, f32[160,1024]{1,0:T(8,128)} %shard_map.75), kind=kOutput, calls=%fused_computation.20 | convolution fusion | flops 671580160 | bytes 5505024 | tf_op jit(solution)/shard_map/dot_general | solution.py:149
  (48 shorter events, 11.5 us)
Async XLA Ops:
  7.2 42.5 %all-gather.3.cloned.1.call-start = ((), (), s32[]{:S(2)}) async-start(), calls=%async_computation.1 | async-start | bytes 4718592 | tf_op jit(solution)/shard_map/all_gather | solution.py:141
  21.3 2.0 copy-start
  24.9 7.4 %collective-permute-start = (f32[512,1024]{1,0:T(8,128)}, f32[512,1024]{1,0:T(8,128)}, u32[]{:S(2)}, u32[]{:S(2)}) collective-permute-start(f32[512,1024]{1,0:T(8,128)} %constant_dynamic-slice_fusion.2), channel_id=1, source_target_pairs={{0,1},{1,0},{2,3},{3,2},{4,5},{5,4},{6,7},{7,6},{8,9},{9,8},{10,11... | collective-permute-start | bytes 6291464 | tf_op jit(solution)/shard_map/ppermute | solution.py:84
  36.4 46.6 %all-to-all-start = ((f32[16,32,1024]{2,1,0:T(8,128)}), f32[16,32,1024]{2,1,0:T(8,128)S(1)}, u32[]{:S(2)}, u32[]{:S(2)}) async-start(f32[16,32,1024]{2,1,0:T(8,128)} %bitcast.8), calls=%async_computation | async-start | bytes 4194304 | tf_op jit(solution)/shard_map/all_to_all | solution.py:107
  43.3 103.8 %all-gather.5.cloned.1.call-start = ((), (), s32[]{:S(2)}) async-start(), calls=%async_computation.2 | async-start | bytes 2228224 | tf_op jit(solution)/shard_map/all_gather | solution.py:112
  56.2 42.8 %copy-start.3 = (s32[4]{0:T(128)S(1)}, s32[4]{0:T(128)}, u32[]{:S(2)}) copy-start(s32[4]{0:T(128)} %param.10) | copy-start | bytes 52
  83.2 4.7 %collective-permute-start.1 = (f32[16,1024]{1,0:T(8,128)S(1)}, f32[16,1024]{1,0:T(8,128)S(1)}, u32[]{:S(2)}, u32[]{:S(2)}) collective-permute-start(f32[16,1024]{1,0:T(8,128)S(1)} %constant_dynamic-slice_fusion.1), channel_id=1, source_target_pairs={{0,4},{1,5},{2,6},{3,7},{4,0},{5,1},{6,2},{7,3},{8,12},{9,13},{10,... | collective-permute-start | bytes 196616 | tf_op jit(solution)/shard_map/ppermute | solution.py:84
  87.9 2.8 collective-permute-start.2
  90.8 2.8 collective-permute-start.3
  93.7 4.6 %collective-permute-start.4 = (f32[16,1024]{1,0:T(8,128)S(1)}, f32[16,1024]{1,0:T(8,128)S(1)}, u32[]{:S(2)}, u32[]{:S(2)}) collective-permute-start(f32[16,1024]{1,0:T(8,128)S(1)} %constant_dynamic-update-slice_fusion.4), channel_id=1, source_target_pairs={{0,4},{1,5},{2,6},{3,7},{4,0},{5,1},{6,2},{7,3},{8,12},{9,13},{10,... | collective-permute-start | bytes 196616 | tf_op jit(solution)/shard_map/ppermute | solution.py:84
  98.3 0.7 copy-start.2
  147.1 4.0 %copy-start.1 = (f32[512,1024]{1,0:T(8,128)S(1)}, f32[512,1024]{1,0:T(8,128)}, u32[]{:S(2)}) copy-start(f32[512,1024]{1,0:T(8,128)} %all-gather.5.cloned.1.call-done) | copy-start | bytes 6291460
  147.1 5.5 %collective-permute-start.5 = (f32[512,1024]{1,0:T(8,128)}, f32[512,1024]{1,0:T(8,128)S(1)}, u32[]{:S(2)}, u32[]{:S(2)}) collective-permute-start(f32[512,1024]{1,0:T(8,128)} %all-gather.5.cloned.1.call-done), channel_id=1, source_target_pairs={{0,1},{1,0},{2,3},{3,2},{4,5},{5,4},{6,7},{7,6},{8,9},{9,8},{10,11... | collective-permute-start | bytes 6291464 | tf_op jit(solution)/shard_map/ppermute | solution.py:84
Sparse Core Ops, SparseCore 0:
  13.7 35.9 all-gather.2
  99.1 47.9 all-gather.4

commit v8 on v7

--- a/solution.py
+++ b/solution.py
@@ -44,11 +44,18 @@
     return jnp.sum(diag, axis=1, keepdims=True), jnp.sum(diag, axis=0, keepdims=True)
 
 
-def _iterate_kernel(g_ref, s_ref, o_ref, a0_ref, e0_ref, a1_ref, e1_ref):
+def _iterate_kernel(low_ref, mine_ref, other_ref, s_ref, o_ref, a0_ref, e0_ref, a1_ref, e1_ref):
     o_ref[...] = s_ref[...]
+    width = mine_ref.shape[0]
+    low = low_ref[...] > 0.5
 
     def step(i, carry):
-        product = _mm(o_ref[...], g_ref[...])
+        subspace = o_ref[...]
+        first = subspace[:, 0:width]
+        second = subspace[:, width:]
+        product = _mm(jnp.where(low, first, second), mine_ref[...]) + _mm(
+            jnp.where(low, second, first), other_ref[...]
+        )
         moment = _mm_nt(product, product)
         a0_ref[...] = moment[0:HALF, 0:HALF]
         d0c, d0r = _eliminate(a0_ref, e0_ref)
@@ -65,7 +72,7 @@
     lax.fori_loop(0, ITERS, step, 0)
 
 
-def iterate(gram, start):
+def iterate(low, mine, other, start):
     rank = start.shape[0]
     rest = rank - HALF
     return pl.pallas_call(
@@ -77,7 +84,7 @@
             pltpu.VMEM((rest, rest), jnp.float32),
             pltpu.VMEM((rest, rest), jnp.float32),
         ],
-    )(gram, start)
+    )(low, mine, other, start)
 
 
 def _swap(x, flip, axis="seq"):
@@ -111,7 +118,8 @@
     s = _double(_double(s, z_low, 2), z_high, 4)
     s = lax.all_gather(s, "kv", axis=0, tiled=True)
     s, late = lax.optimization_barrier((s, late))
-    return _double(s, core, 1), early, late
+    low = jnp.where(core == 0, 1.0, 0.0).astype(jnp.float32).reshape(1, 1)
+    return (low, s, _swap(s, 1)), early, late
 
 
 def local(prefill_keys, queries, outlier_spans, start_basis):
@@ -144,7 +152,7 @@
         prefill_keys, prefill_keys, (((0,), (0,)), ((), ())), preferred_element_type=jnp.float32
     ) * inverse_tokens
     gram, landmark_scores, outlier_scores = sum_gram(local_gram, landmark_scores, outlier_scores)
-    subspace = iterate(gram, start_basis)
+    subspace = iterate(*gram, start_basis)
     rounded = subspace.astype(jnp.bfloat16)
     coefficients = lax.dot_general(
         rounded, prefill_keys, (((1,), (1,)), ((), ())), preferred_element_type=jnp.float32

time: 311 us -> 312 us (level)
  local copies, waits for them, and re-layouts: 25.2 us -> 21.1 us
  waiting for transfers between devices: 30 us -> 34 us
    ppermute x6, waiting for transfers between devices: 11.8 us -> 15.8 us  [_swap(): lax.ppermute(x, axis, [(i, i ^ flip) for i in range(lax.axis_size(axis))])]
  transfers between devices with their start and end apart: 9 -> 9, of which waited for: 7 -> 7; matrix products, arithmetic and copies ran while one was open for 24% -> 23% of each run, Pallas kernels for 0% -> 0%
where the time goes in v8:
time: 312 us; the launch traced here: 311 us
  Pallas kernels  146 us (47%)
  matrix products  42 us (13%)
  waiting for transfers between devices  34 us (11%)
  other arithmetic  23.1 us (7%)
  local copies, waits for them, and re-layouts  21.1 us (7%)
  blocking collectives  17.8 us (6%)
  between operations  14.2 us (5%)
  starting transfers between devices  13 us (4%)
    pallas_call x1, Pallas kernels, iterate(): pl.pallas_call(_iterate_kernel, out_shape=jax.ShapeDtypeStruct(start.shap...  146 us
    dot_general x16, matrix products, one_head(): jnp.einsum('qgd,cd->qgc', query_group, key_group, preferred_element_type=...  29.6 us
    all_gather x1, blocking collectives, local(): lax.all_gather(picked, 'seq', axis=0, tiled=True)  17.8 us
    ppermute x6, waiting for transfers between devices, _swap(): lax.ppermute(x, axis, [(i, i ^ flip) for i in range(lax.axis_size(axis))])  15.8 us
    dynamic_update_slice x16, other arithmetic, score_rows(): return lax.map(one_head, (query_heads, key_heads))  12.3 us
    all_gather x1, waiting for transfers between devices, sum_gram(): s = lax.all_gather(s, 'kv', axis=0, tiled=True)  11.8 us
    dot_general x1, matrix products, local(): lax.dot_general(prefill_keys, prefill_keys, (((0,), (0,)), ((), ())), pre...  7.7 us
    unnamed x9, local copies, waits for them, and re-layouts  7.21 us
  transfers between devices with their start and end apart: 9, of which 7 were waited for; matrix products, arithmetic and copies ran while one was open for 23% of the time, Pallas kernels for 0%

profile of v8, /device:TPU:1, one launch (start us, length us, event | category | flops | bytes accessed | tf_op | source)
XLA Modules:
  0.0 311.1 jit_solution(8464292428296950764)
XLA Ops:
  7.2 5.5 %convert_reduce_fusion = f32[256,1024]{1,0:T(8,128)S(1)} fusion(bf16[2048,1024]{1,0:T(8,128)(2,1)} %param.8), kind=kLoop, calls=%fused_computation.19 | loop fusion | flops 3932160 | bytes 5242880 | tf_op jit(solution)/shard_map/reduce_sum | solution.py:131
  13.6 7.7 %convolution_multiply_fusion = f32[1024,1024]{1,0:T(8,128)S(1)} fusion(bf16[2048,1024]{1,0:T(8,128)(2,1)} %param.8), kind=kOutput, calls=%fused_computation.21 | convolution fusion | flops 4296015872 | bytes 8388608 | tf_op jit(solution)/shard_map/dot_general | solution.py:151
  21.3 2.0 copy-done
  23.3 1.6 constant_dynamic-slice_fusion.2
  24.9 1.4 collective-permute-start
  26.3 3.3 %copy.19 = bf16[128,8192]{0,1:T(8,128)(2,1)S(1)} copy(bf16[128,8192]{1,0:T(8,128)(2,1)} %param.9) | data formatting | bytes 4194304 | tf_op args[1]
  29.6 2.7 copy.21
  32.2 4.2 %dynamic-slice_add_fusion = f32[512,1024]{1,0:T(8,128)} fusion(f32[512,1024]{1,0:T(8,128)} %collective-permute-done, f32[1024,1024]{1,0:T(8,128)} %copy-done, s32[]{:T(128)S(6)} %select_n.60), kind=kLoop, calls=%fused_computation.22 | loop fusion | flops 524288 | bytes 6291460 | tf_op jit(solution)/shard_map/add | solution.py:98
  36.4 6.8 %all-to-all-start = ((f32[16,32,1024]{2,1,0:T(8,128)}), f32[16,32,1024]{2,1,0:T(8,128)S(1)}, u32[]{:S(2)}, u32[]{:S(2)}) async-start(f32[16,32,1024]{2,1,0:T(8,128)} %bitcast.9), calls=%async_computation | async-start | bytes 4194304 | tf_op jit(solution)/shard_map/all_to_all | solution.py:114
  43.3 6.4 %all-gather.3.cloned.1.call-done = bf16[2048,1024]{1,0:T(8,128)(2,1)} async-done(((bf16[256,1024]{1,0:T(8,128)(2,1)}), bf16[2048,1024]{1,0:T(8,128)(2,1)}) %all-gather.3.cloned.1.call-update) | async-done | bytes 4194320 | tf_op jit(solution)/shard_map/all_gather | solution.py:149
  49.7 6.5 %copy.20 = bf16[2048,1024]{0,1:T(8,128)(2,1)} copy(bf16[2048,1024]{1,0:T(8,128)(2,1)} %all-gather.3.cloned.1.call-done) | data formatting | bytes 8388608 | tf_op jit(solution)/shard_map/all_gather | solution.py:149
  56.2 26.8 %while.20 = (s32[]{:T(128)}, bf16[8,128,2048]{2,1,0:T(8,128)(2,1)}, bf16[8,128,8,128]{3,1,2,0:T(8,128)(2,1)}, bf16[8,2048,128]{1,2,0:T(8,128)(2,1)}, s32[]{:T(128)}) while((s32[]{:T(128)}, bf16[8,128,2048]{2,1,0:T(8,128)(2,1)}, bf16[8,128,8,128]{3,1,2,0:T(8,128)(2,1)}, bf16[8,2048,128]{1,2,0:T(8,128)(2,1)}, s32[]{:T(128)}) %tuple.56), condition=%wide.region_3.4_spmd, body=%wide.region_1.0_spmd.sunk | while | flops 539230208 | bytes 3409469 | solution.py:147
  56.2 2.5 convolution_reduce_fusion.4
  58.7 0.9 fusion.26
  59.6 2.5 convolution_reduce_fusion.4
  62.0 0.9 fusion.26
  62.9 2.5 convolution_reduce_fusion.4
  65.4 0.9 fusion.26
  66.3 2.5 convolution_reduce_fusion.4
  68.7 0.9 fusion.26
  69.6 2.5 convolution_reduce_fusion.4
  72.1 0.9 fusion.26
  73.0 2.5 convolution_reduce_fusion.4
  76.4 2.5 convolution_reduce_fusion.4
  79.7 2.5 convolution_reduce_fusion.4
  83.2 1.5 collective-permute-start.1
  84.7 3.2 %collective-permute-done.1 = f32[16,1024]{1,0:T(8,128)S(1)} collective-permute-done((f32[16,1024]{1,0:T(8,128)S(1)}, f32[16,1024]{1,0:T(8,128)S(1)}, u32[]{:S(2)}, u32[]{:S(2)}) %collective-permute-start.1) | collective-permute-done | bytes 65568 | tf_op jit(solution)/shard_map/ppermute | solution.py:91
  88.1 2.7 collective-permute-done.2
  91.0 2.7 collective-permute-done.3
  93.7 1.4 collective-permute-start.4
  95.1 3.2 %collective-permute-done.4 = f32[16,1024]{1,0:T(8,128)S(1)} collective-permute-done((f32[16,1024]{1,0:T(8,128)S(1)}, f32[16,1024]{1,0:T(8,128)S(1)}, u32[]{:S(2)}, u32[]{:S(2)}) %collective-permute-start.4) | collective-permute-done | bytes 65568 | tf_op jit(solution)/shard_map/ppermute | solution.py:91
  99.2 2.7 gather_fusion
  102.0 17.8 %all_gather.11 = bf16[256,1024]{1,0:T(8,128)(2,1)S(1)} all-gather(bf16[32,1024]{1,0:T(8,128)(2,1)S(1)} %bitcast_select_fusion), channel_id=1, replica_groups=mesh['kv'=16,'seq'=8] {'seq'}, dimensions={0}, use_global_device_ids=true | all-gather | bytes 589824 | tf_op jit(solution)/shard_map/all_gather | solution.py:150
  120.1 15.2 %while.21 = (s32[]{:T(128)}, bf16[8,128,256]{2,1,0:T(8,128)(2,1)}, bf16[8,128,8,128]{3,1,2,0:T(8,128)(2,1)}, bf16[8,256,128]{1,2,0:T(8,128)(2,1)S(1)}, s32[]{:T(128)}) while((s32[]{:T(128)}, bf16[8,128,256]{2,1,0:T(8,128)(2,1)}, bf16[8,128,8,128]{3,1,2,0:T(8,128)(2,1)}, bf16[8,256,128]{1,2,0:T(8,128)(2,1)S(1)}, s32[]{:T(128)}) %tuple.58), condition=%wide.region_7.8_spmd, body=%wide.region_5.7_spmd.sunk | while | flops 67403776 | bytes 656957 | solution.py:147
  120.1 1.2 convolution_reduce_fusion.5
  122.0 1.2 convolution_reduce_fusion.5
  123.9 1.2 convolution_reduce_fusion.5
  125.8 1.2 convolution_reduce_fusion.5
  127.7 1.2 convolution_reduce_fusion.5
  129.6 1.2 convolution_reduce_fusion.5
  131.5 1.2 convolution_reduce_fusion.5
  133.4 1.2 convolution_reduce_fusion.5
  135.3 11.8 %all-gather.5.cloned.1.call-done.mine_ref = f32[512,1024]{1,0:T(8,128)} async-done(((f32[32,1024]{1,0:T(8,128)}), f32[512,1024]{1,0:T(8,128)}) %all-gather.5.cloned.1.call-update) | async-done | bytes 2097168 | tf_op jit(solution)/shard_map/all_gather | solution.py:119
  147.1 1.5 collective-permute-start.5
  148.6 4.0 %collective-permute-done.5.other_ref = f32[512,1024]{1,0:T(8,128)S(1)} collective-permute-done((f32[512,1024]{1,0:T(8,128)}, f32[512,1024]{1,0:T(8,128)S(1)}, u32[]{:S(2)}, u32[]{:S(2)}) %collective-permute-start.5) | collective-permute-done | bytes 2097184 | tf_op jit(solution)/shard_map/ppermute | solution.py:91
  152.6 1.3 copy-done.1
  153.9 145.6 %shard_map.75 = f32[160,1024]{1,0:T(8,128)} custom-call(f32[1,1]{1,0:T(1,128)} %bitcast.8.low_ref, f32[512,1024]{1,0:T(8,128)} %all-gather.5.cloned.1.call-done.mine_ref, f32[512,1024]{1,0:T(8,128)} %copy-done.1, f32[160,1024]{1,0:T(8,128)} %s_ref.1), custom_call_target="tpu_custom_call" | custom-call | tf_op jit(solution)/shard_map/pallas_call | solution.py:78
  299.5 4.8 %convolution_convert_fusion = bf16[160,2048]{1,0:T(8,128)(2,1)} fusion(bf16[2048,1024]{1,0:T(8,128)(2,1)} %param.8, f32[160,1024]{1,0:T(8,128)} %shard_map.75), kind=kOutput, calls=%fused_computation.20 | convolution fusion | flops 671580160 | bytes 5505024 | tf_op jit(solution)/shard_map/dot_general | solution.py:157
  (45 shorter events, 10.5 us)
Async XLA Ops:
  7.2 42.5 %all-gather.3.cloned.1.call-start = ((), (), s32[]{:S(2)}) async-start(), calls=%async_computation.1 | async-start | bytes 4718592 | tf_op jit(solution)/shard_map/all_gather | solution.py:149
  21.3 2.0 copy-start
  24.9 7.4 %collective-permute-start = (f32[512,1024]{1,0:T(8,128)}, f32[512,1024]{1,0:T(8,128)}, u32[]{:S(2)}, u32[]{:S(2)}) collective-permute-start(f32[512,1024]{1,0:T(8,128)} %constant_dynamic-slice_fusion.2), channel_id=1, source_target_pairs={{0,1},{1,0},{2,3},{3,2},{4,5},{5,4},{6,7},{7,6},{8,9},{9,8},{10,11... | collective-permute-start | bytes 6291464 | tf_op jit(solution)/shard_map/ppermute | solution.py:91
  36.4 46.6 %all-to-all-start = ((f32[16,32,1024]{2,1,0:T(8,128)}), f32[16,32,1024]{2,1,0:T(8,128)S(1)}, u32[]{:S(2)}, u32[]{:S(2)}) async-start(f32[16,32,1024]{2,1,0:T(8,128)} %bitcast.9), calls=%async_computation | async-start | bytes 4194304 | tf_op jit(solution)/shard_map/all_to_all | solution.py:114
  43.3 103.8 %all-gather.5.cloned.1.call-start = ((), (), s32[]{:S(2)}) async-start(), calls=%async_computation.2 | async-start | bytes 2228224 | tf_op jit(solution)/shard_map/all_gather | solution.py:119
  56.2 42.8 %copy-start.3 = (s32[4]{0:T(128)S(1)}, s32[4]{0:T(128)}, u32[]{:S(2)}) copy-start(s32[4]{0:T(128)} %param.10) | copy-start | bytes 52
  83.2 4.7 %collective-permute-start.1 = (f32[16,1024]{1,0:T(8,128)S(1)}, f32[16,1024]{1,0:T(8,128)S(1)}, u32[]{:S(2)}, u32[]{:S(2)}) collective-permute-start(f32[16,1024]{1,0:T(8,128)S(1)} %constant_dynamic-slice_fusion.1), channel_id=1, source_target_pairs={{0,4},{1,5},{2,6},{3,7},{4,0},{5,1},{6,2},{7,3},{8,12},{9,13},{10,... | collective-permute-start | bytes 196616 | tf_op jit(solution)/shard_map/ppermute | solution.py:91
  87.9 2.8 collective-permute-start.2
  90.8 2.8 collective-permute-start.3
  93.7 4.6 %collective-permute-start.4 = (f32[16,1024]{1,0:T(8,128)S(1)}, f32[16,1024]{1,0:T(8,128)S(1)}, u32[]{:S(2)}, u32[]{:S(2)}) collective-permute-start(f32[16,1024]{1,0:T(8,128)S(1)} %constant_dynamic-update-slice_fusion.2), channel_id=1, source_target_pairs={{0,4},{1,5},{2,6},{3,7},{4,0},{5,1},{6,2},{7,3},{8,12},{9,13},{10,... | collective-permute-start | bytes 196616 | tf_op jit(solution)/shard_map/ppermute | solution.py:91
  98.3 0.7 copy-start.2
  147.1 5.5 %collective-permute-start.5 = (f32[512,1024]{1,0:T(8,128)}, f32[512,1024]{1,0:T(8,128)S(1)}, u32[]{:S(2)}, u32[]{:S(2)}) collective-permute-start(f32[512,1024]{1,0:T(8,128)} %all-gather.5.cloned.1.call-done.mine_ref), channel_id=1, source_target_pairs={{0,1},{1,0},{2,3},{3,2},{4,5},{5,4},{6,7},{7,6},{8,9},{9,8},{10,11... | collective-permute-start | bytes 6291464 | tf_op jit(solution)/shard_map/ppermute | solution.py:91
  152.6 1.3 copy-start.1
Sparse Core Ops, SparseCore 0:
  13.7 35.9 all-gather.2
  99.1 47.9 all-gather.4

commit v9 on v7

--- a/solution.py
+++ b/solution.py
@@ -143,7 +143,7 @@
     local_gram = lax.dot_general(
         prefill_keys, prefill_keys, (((0,), (0,)), ((), ())), preferred_element_type=jnp.float32
     ) * inverse_tokens
-    gram, landmark_scores, outlier_scores = sum_gram(local_gram, landmark_scores, outlier_scores)
+    gram, outlier_scores, landmark_scores = sum_gram(local_gram, outlier_scores, landmark_scores)
     subspace = iterate(gram, start_basis)
     rounded = subspace.astype(jnp.bfloat16)
     coefficients = lax.dot_general(

time: 311 us -> 309 us (level)
  waiting for transfers between devices: 30 us -> 26.6 us
    all_gather x1, waiting for transfers between devices: 6.36 us -> 0.02 us  [local(): lax.all_gather(landmarks, 'seq', axis=0, tiled=True)]
    all_gather x1, waiting for transfers between devices: 11.8 us -> 15.5 us  [sum_gram(): s = lax.all_gather(s, 'kv', axis=0, tiled=True)]
  transfers between devices with their start and end apart: 9 -> 9, of which waited for: 7 -> 7; matrix products, arithmetic and copies ran while one was open for 24% -> 25% of each run, Pallas kernels for 0% -> 0%
where the time goes in v9:
time: 309 us; the launch traced here: 308 us
  Pallas kernels  145 us (47%)
  matrix products  42 us (14%)
  local copies, waits for them, and re-layouts  27.7 us (9%)
  waiting for transfers between devices  26.6 us (9%)
  other arithmetic  22.2 us (7%)
  blocking collectives  15.7 us (5%)
  starting transfers between devices  15.1 us (5%)
  between operations  14.2 us (5%)
    pallas_call x1, Pallas kernels, iterate(): pl.pallas_call(_iterate_kernel, out_shape=jax.ShapeDtypeStruct(start.shap...  145 us
    dot_general x16, matrix products, one_head(): jnp.einsum('qgd,cd->qgc', query_group, key_group, preferred_element_type=...  29.6 us
    all_gather x1, blocking collectives, local(): lax.all_gather(picked, 'seq', axis=0, tiled=True)  15.7 us
    all_gather x1, waiting for transfers between devices, sum_gram(): s = lax.all_gather(s, 'kv', axis=0, tiled=True)  15.5 us
    dynamic_update_slice x16, other arithmetic, score_rows(): return lax.map(one_head, (query_heads, key_heads))  12.3 us
    ppermute x6, waiting for transfers between devices, _swap(): lax.ppermute(x, axis, [(i, i ^ flip) for i in range(lax.axis_size(axis))])  11.1 us
    ppermute x6, starting transfers between devices, _swap(): lax.ppermute(x, axis, [(i, i ^ flip) for i in range(lax.axis_size(axis))])  8.19 us
    dot_general x1, matrix products, local(): lax.dot_general(prefill_keys, prefill_keys, (((0,), (0,)), ((), ())), pre...  7.64 us
  transfers between devices with their start and end apart: 9, of which 7 were waited for; matrix products, arithmetic and copies ran while one was open for 25% of the time, Pallas kernels for 0%

profile of v9, /device:TPU:1, one launch (start us, length us, event | category | flops | bytes accessed | tf_op | source)
XLA Modules:
  0.0 308.5 jit_solution(4045458581028764923)
XLA Ops:
  7.2 5.5 %convert_reduce_fusion = f32[256,1024]{1,0:T(8,128)S(1)} fusion(bf16[2048,1024]{1,0:T(8,128)(2,1)} %param.8), kind=kLoop, calls=%fused_computation.19 | loop fusion | flops 3932160 | bytes 5242880 | tf_op jit(solution)/shard_map/reduce_sum | solution.py:123
  13.6 7.6 %convolution_multiply_fusion = f32[1024,1024]{1,0:T(8,128)S(1)} fusion(bf16[2048,1024]{1,0:T(8,128)(2,1)} %param.8), kind=kOutput, calls=%fused_computation.21 | convolution fusion | flops 4296015872 | bytes 8388608 | tf_op jit(solution)/shard_map/dot_general | solution.py:143
  21.3 2.0 copy-done
  23.3 1.6 constant_dynamic-slice_fusion.2
  24.9 1.4 collective-permute-start
  26.5 3.2 %gather_fusion = bf16[4,8,1024]{2,1,0:T(8,128)(2,1)S(1)} fusion(bf16[256,8,1024]{2,1,0:T(8,128)(2,1)} %bitcast.53, s32[1024]{0:T(1024)S(1)} %pad_clamp_fusion), kind=kCustom, calls=%fused_computation | custom fusion | bytes 131088 | tf_op jit(solution)/shard_map/jit(_take)/gather | solution.py:124
  30.3 3.3 %dynamic-slice_add_fusion = f32[512,1024]{1,0:T(8,128)} fusion(f32[512,1024]{1,0:T(8,128)S(1)} %collective-permute-done, f32[1024,1024]{1,0:T(8,128)} %copy-done, s32[]{:T(128)S(6)} %select_n.57), kind=kLoop, calls=%fused_computation.22 | loop fusion | flops 524288 | bytes 6291460 | tf_op jit(solution)/shard_map/add | solution.py:91
  33.6 6.8 %all-to-all-start = ((f32[16,32,1024]{2,1,0:T(8,128)}), f32[16,32,1024]{2,1,0:T(8,128)S(1)}, u32[]{:S(2)}, u32[]{:S(2)}) async-start(f32[16,32,1024]{2,1,0:T(8,128)} %bitcast.8), calls=%async_computation | async-start | bytes 4194304 | tf_op jit(solution)/shard_map/all_to_all | solution.py:107
  40.5 15.7 %all_gather.9 = bf16[256,1024]{1,0:T(8,128)(2,1)S(1)} all-gather(bf16[32,1024]{1,0:T(8,128)(2,1)S(1)} %bitcast_select_fusion), channel_id=1, replica_groups=mesh['kv'=16,'seq'=8] {'seq'}, dimensions={0}, use_global_device_ids=true | all-gather | bytes 589824 | tf_op jit(solution)/shard_map/all_gather | solution.py:142
  56.2 4.1 %copy.19 = bf16[128,8192]{0,1:T(8,128)(2,1)} copy(bf16[128,8192]{1,0:T(8,128)(2,1)} %param.9) | data formatting | bytes 4194304 | tf_op args[1]
  60.2 3.9 %copy.21 = bf16[8,128,8,128]{3,1,2,0:T(8,128)(2,1)} copy(bf16[8,128,8,128]{1,3,2,0:T(8,128)(2,1)} %bitcast.54) | data formatting | bytes 4194304 | tf_op jit(solution)/shard_map/while | solution.py:139
  64.4 15.2 %while.20 = (s32[]{:T(128)}, bf16[8,128,256]{2,1,0:T(8,128)(2,1)}, bf16[8,128,8,128]{3,1,2,0:T(8,128)(2,1)}, bf16[8,256,128]{1,2,0:T(8,128)(2,1)S(1)}, s32[]{:T(128)}) while((s32[]{:T(128)}, bf16[8,128,256]{2,1,0:T(8,128)(2,1)}, bf16[8,128,8,128]{3,1,2,0:T(8,128)(2,1)}, bf16[8,256,128]{1,2,0:T(8,128)(2,1)S(1)}, s32[]{:T(128)}) %tuple.58), condition=%wide.region_2.3_spmd, body=%wide.region_0.2_spmd.sunk | while | flops 67403776 | bytes 656957 | solution.py:139
  64.4 1.3 convolution_reduce_fusion.4
  66.3 1.2 convolution_reduce_fusion.4
  68.2 1.2 convolution_reduce_fusion.4
  70.1 1.2 convolution_reduce_fusion.4
  72.0 1.2 convolution_reduce_fusion.4
  73.9 1.2 convolution_reduce_fusion.4
  75.8 1.2 convolution_reduce_fusion.4
  77.7 1.2 convolution_reduce_fusion.4
  79.7 1.3 collective-permute-start.1
  81.0 3.9 %collective-permute-done.1 = f32[16,1024]{1,0:T(8,128)S(1)} collective-permute-done((f32[16,1024]{1,0:T(8,128)S(1)}, f32[16,1024]{1,0:T(8,128)S(1)}, u32[]{:S(2)}, u32[]{:S(2)}) %collective-permute-start.1) | collective-permute-done | bytes 65568 | tf_op jit(solution)/shard_map/ppermute | solution.py:84
  84.9 1.0 collective-permute-start.2
  85.9 1.8 collective-permute-done.2
  87.8 1.0 collective-permute-start.3
  88.8 1.8 collective-permute-done.3
  90.6 1.9 collective-permute-start.4
  92.6 3.0 collective-permute-done.4
  96.3 6.5 %copy.23 = bf16[2048,1024]{0,1:T(8,128)(2,1)} copy(bf16[2048,1024]{1,0:T(8,128)(2,1)} %all-gather.5.cloned.1.call-done) | data formatting | bytes 8388608 | tf_op jit(solution)/shard_map/all_gather | solution.py:141
  102.8 26.8 %while.21 = (s32[]{:T(128)}, bf16[8,128,2048]{2,1,0:T(8,128)(2,1)}, bf16[8,128,8,128]{3,1,2,0:T(8,128)(2,1)}, bf16[8,2048,128]{1,2,0:T(8,128)(2,1)}, s32[]{:T(128)}) while((s32[]{:T(128)}, bf16[8,128,2048]{2,1,0:T(8,128)(2,1)}, bf16[8,128,8,128]{3,1,2,0:T(8,128)(2,1)}, bf16[8,2048,128]{1,2,0:T(8,128)(2,1)}, s32[]{:T(128)}) %tuple.57), condition=%wide.region_7.8_spmd, body=%wide.region_5.7_spmd.sunk | while | flops 539230208 | bytes 3409469 | solution.py:139
  102.8 2.5 convolution_reduce_fusion.5
  105.2 0.9 fusion.29
  106.1 2.5 convolution_reduce_fusion.5
  108.6 0.9 fusion.29
  109.5 2.5 convolution_reduce_fusion.5
  112.0 0.9 fusion.29
  112.9 2.5 convolution_reduce_fusion.5
  116.2 2.5 convolution_reduce_fusion.5
  119.6 2.5 convolution_reduce_fusion.5
  122.9 2.5 convolution_reduce_fusion.5
  126.3 2.5 convolution_reduce_fusion.5
  129.6 15.5 %all-gather.3.cloned.1.call-done = f32[512,1024]{1,0:T(8,128)} async-done(((f32[32,1024]{1,0:T(8,128)}), f32[512,1024]{1,0:T(8,128)}) %all-gather.3.cloned.1.call-update) | async-done | bytes 2097168 | tf_op jit(solution)/shard_map/all_gather | solution.py:112
  145.1 1.5 collective-permute-start.5
  146.6 2.5 broadcast_in_dim.35
  149.1 1.5 constant_dynamic-update-slice_fusion.1
  150.6 1.5 constant_dynamic-update-slice_fusion.g_ref
  152.1 144.8 %shard_map.75 = f32[160,1024]{1,0:T(8,128)} custom-call(f32[1024,1024]{1,0:T(8,128)} %constant_dynamic-update-slice_fusion.g_ref, f32[160,1024]{1,0:T(8,128)} %s_ref.1), custom_call_target="tpu_custom_call" | custom-call | tf_op jit(solution)/shard_map/pallas_call | solution.py:71
  296.9 4.8 %convolution_convert_fusion = bf16[160,2048]{1,0:T(8,128)(2,1)} fusion(bf16[2048,1024]{1,0:T(8,128)(2,1)} %param.8, f32[160,1024]{1,0:T(8,128)} %shard_map.75), kind=kOutput, calls=%fused_computation.20 | convolution fusion | flops 671580160 | bytes 5505024 | tf_op jit(solution)/shard_map/dot_general | solution.py:149
  (48 shorter events, 12.6 us)
Async XLA Ops:
  7.2 89.1 %all-gather.5.cloned.1.call-start = ((), (), s32[]{:S(2)}) async-start(), calls=%async_computation.2 | async-start | bytes 4718592 | tf_op jit(solution)/shard_map/all_gather | solution.py:141
  21.2 2.0 copy-start
  23.3 3.0 copy-start.3
  24.9 5.4 %collective-permute-start = (f32[512,1024]{1,0:T(8,128)}, f32[512,1024]{1,0:T(8,128)S(1)}, u32[]{:S(2)}, u32[]{:S(2)}) collective-permute-start(f32[512,1024]{1,0:T(8,128)} %constant_dynamic-slice_fusion.2), channel_id=1, source_target_pairs={{0,1},{1,0},{2,3},{3,2},{4,5},{5,4},{6,7},{7,6},{8,9},{9,8},{10,11... | collective-permute-start | bytes 6291464 | tf_op jit(solution)/shard_map/ppermute | solution.py:84
  33.6 46.0 %all-to-all-start = ((f32[16,32,1024]{2,1,0:T(8,128)}), f32[16,32,1024]{2,1,0:T(8,128)S(1)}, u32[]{:S(2)}, u32[]{:S(2)}) async-start(f32[16,32,1024]{2,1,0:T(8,128)} %bitcast.8), calls=%async_computation | async-start | bytes 4194304 | tf_op jit(solution)/shard_map/all_to_all | solution.py:107
  40.5 104.6 %all-gather.3.cloned.1.call-start = ((), (), s32[]{:S(2)}) async-start(), calls=%async_computation.1 | async-start | bytes 2228224 | tf_op jit(solution)/shard_map/all_gather | solution.py:112
  79.7 5.1 %collective-permute-start.1 = (f32[16,1024]{1,0:T(8,128)S(1)}, f32[16,1024]{1,0:T(8,128)S(1)}, u32[]{:S(2)}, u32[]{:S(2)}) collective-permute-start(f32[16,1024]{1,0:T(8,128)S(1)} %constant_dynamic-slice_fusion.1), channel_id=1, source_target_pairs={{0,4},{1,5},{2,6},{3,7},{4,0},{5,1},{6,2},{7,3},{8,12},{9,13},{10,... | collective-permute-start | bytes 196616 | tf_op jit(solution)/shard_map/ppermute | solution.py:84
  84.9 2.8 collective-permute-start.2
  87.8 2.8 collective-permute-start.3
  90.6 5.0 %collective-permute-start.4 = (f32[16,1024]{1,0:T(8,128)S(1)}, f32[16,1024]{1,0:T(8,128)S(1)}, u32[]{:S(2)}, u32[]{:S(2)}) collective-permute-start(f32[16,1024]{1,0:T(8,128)S(1)} %constant_dynamic-update-slice_fusion.4), channel_id=1, source_target_pairs={{0,4},{1,5},{2,6},{3,7},{4,0},{5,1},{6,2},{7,3},{8,12},{9,13},{10,... | collective-permute-start | bytes 196616 | tf_op jit(solution)/shard_map/ppermute | solution.py:84
  95.6 0.7 copy-start.2
  145.1 4.0 %copy-start.1 = (f32[512,1024]{1,0:T(8,128)S(1)}, f32[512,1024]{1,0:T(8,128)}, u32[]{:S(2)}) copy-start(f32[512,1024]{1,0:T(8,128)} %all-gather.3.cloned.1.call-done) | copy-start | bytes 6291460
  145.1 5.5 %collective-permute-start.5 = (f32[512,1024]{1,0:T(8,128)}, f32[512,1024]{1,0:T(8,128)S(1)}, u32[]{:S(2)}, u32[]{:S(2)}) collective-permute-start(f32[512,1024]{1,0:T(8,128)} %all-gather.3.cloned.1.call-done), channel_id=1, source_target_pairs={{0,1},{1,0},{2,3},{3,2},{4,5},{5,4},{6,7},{7,6},{8,9},{9,8},{10,11... | collective-permute-start | bytes 6291464 | tf_op jit(solution)/shard_map/ppermute | solution.py:84
Sparse Core Ops, SparseCore 0:
  13.7 36.3 all-gather.4
  96.4 48.6 all-gather.2

commit v10 on v9

--- a/solution.py
+++ b/solution.py
@@ -138,8 +138,10 @@
 
         return lax.map(one_head, (query_heads, key_heads))
 
-    landmark_scores = score_rows(lax.all_gather(landmarks, "seq", axis=0, tiled=True))
-    outlier_scores = score_rows(lax.all_gather(picked, "seq", axis=0, tiled=True))
+    gathered = lax.all_gather(jnp.concatenate([landmarks, picked], axis=0), "seq", axis=0)
+    span_count = landmarks.shape[0]
+    landmark_scores = score_rows(gathered[:, :span_count].reshape(-1, width))
+    outlier_scores = score_rows(gathered[:, span_count:].reshape(-1, width))
     local_gram = lax.dot_general(
         prefill_keys, prefill_keys, (((0,), (0,)), ((), ())), preferred_element_type=jnp.float32
     ) * inverse_tokens

time: 309 us -> 311 us (level)
  blocking collectives: 15.7 us -> 0 us
  waiting for transfers between devices: 26.6 us -> 36.4 us
  starting transfers between devices: 15.1 us -> 20.6 us
    all_gather x1 -> x0, blocking collectives: 15.7 us -> none  [local(): lax.all_gather(picked, 'seq', axis=0, tiled=True)]
    all_gather x2 -> x0, local copies, waits for them, and re-layouts: 6.69 us -> none  [the longest x1 6.49 us: local(): lax.all_gather(landmarks, 'seq', axis=0, tiled=True)]
    ppermute x6, starting transfers between devices: 8.19 us -> 13.7 us  [_swap(): lax.ppermute(x, axis, [(i, i ^ flip) for i in range(lax.axis_size(axis))])]
    all_gather x1, waiting for transfers between devices: 15.5 us -> 20 us  [sum_gram(): s = lax.all_gather(s, 'kv', axis=0, tiled=True)]
    all_to_all x1, waiting for transfers between devices: 0.01 us -> 4.08 us  [sum_gram(): lax.all_to_all(s.reshape((kv_size, -1) + s.shape[1:]), 'kv', 0, 0, tiled=...]
    slice x0 -> x2, local copies, waits for them, and re-layouts: none -> 3.71 us  [the longest x1 2.63 us: local(): landmark_scores = score_rows(gathered[:, :span_count].reshape(-1, width))]
    all_gather x1, waiting for transfers between devices: 0.02 us -> 3.19 us  [local(): lax.all_gather(jnp.concatenate([landmarks, picked], axis=0), 'seq', axis=0)]
    while x1 -> x3, local copies, waits for them, and re-layouts: 3.91 us -> 6.61 us  [score_rows(): return lax.map(one_head, (query_heads, key_heads))]
  transfers between devices with their start and end apart: 9 -> 9, of which waited for: 7 -> 8; matrix products, arithmetic and copies ran while one was open for 25% -> 24% of each run, Pallas kernels for 0% -> 0%
where the time goes in v10:
time: 311 us; the launch traced here: 310 us
  Pallas kernels  145 us (47%)
  matrix products  42.2 us (14%)
  waiting for transfers between devices  36.4 us (12%)
  local copies, waits for them, and re-layouts  28.3 us (9%)
  other arithmetic  23.7 us (8%)
  starting transfers between devices  20.6 us (7%)
  between operations  14.2 us (5%)
    pallas_call x1, Pallas kernels, iterate(): pl.pallas_call(_iterate_kernel, out_shape=jax.ShapeDtypeStruct(start.shap...  145 us
    dot_general x16, matrix products, one_head(): jnp.einsum('qgd,cd->qgc', query_group, key_group, preferred_element_type=...  29.8 us
    all_gather x1, waiting for transfers between devices, sum_gram(): s = lax.all_gather(s, 'kv', axis=0, tiled=True)  20 us
    ppermute x6, starting transfers between devices, _swap(): lax.ppermute(x, axis, [(i, i ^ flip) for i in range(lax.axis_size(axis))])  13.7 us
    dynamic_update_slice x16, other arithmetic, score_rows(): return lax.map(one_head, (query_heads, key_heads))  12.3 us
    ppermute x6, waiting for transfers between devices, _swap(): lax.ppermute(x, axis, [(i, i ^ flip) for i in range(lax.axis_size(axis))])  9.06 us
    unnamed x9, local copies, waits for them, and re-layouts  8 us
    dot_general x1, matrix products, local(): lax.dot_general(prefill_keys, prefill_keys, (((0,), (0,)), ((), ())), pre...  7.64 us
  transfers between devices with their start and end apart: 9, of which 8 were waited for; matrix products, arithmetic and copies ran while one was open for 24% of the time, Pallas kernels for 0%

profile of v10, /device:TPU:1, one launch (start us, length us, event | category | flops | bytes accessed | tf_op | source)
XLA Modules:
  0.0 310.4 jit_solution(14836719493318062498)
XLA Ops:
  8.5 5.5 %convert_reduce_fusion = f32[256,1024]{1,0:T(8,128)S(1)} fusion(bf16[2048,1024]{1,0:T(8,128)(2,1)} %param.8), kind=kLoop, calls=%fused_computation.19 | loop fusion | flops 3932160 | bytes 5242880 | tf_op jit(solution)/shard_map/reduce_sum | solution.py:123
  14.3 2.7 gather_fusion
  18.0 7.6 %convolution_multiply_fusion = f32[1024,1024]{1,0:T(8,128)S(1)} fusion(bf16[2048,1024]{1,0:T(8,128)(2,1)} %param.8), kind=kOutput, calls=%fused_computation.21 | convolution fusion | flops 4296015872 | bytes 8388608 | tf_op jit(solution)/shard_map/dot_general | solution.py:145
  25.6 2.0 copy-done
  27.7 1.6 constant_dynamic-slice_fusion.2
  29.3 1.4 collective-permute-start
  30.7 4.0 %collective-permute-done = f32[512,1024]{1,0:T(8,128)S(1)} collective-permute-done((f32[512,1024]{1,0:T(8,128)}, f32[512,1024]{1,0:T(8,128)S(1)}, u32[]{:S(2)}, u32[]{:S(2)}) %collective-permute-start) | collective-permute-done | bytes 2097184 | tf_op jit(solution)/shard_map/ppermute | solution.py:84
  34.7 3.4 %dynamic-slice_add_fusion = f32[512,1024]{1,0:T(8,128)} fusion(f32[512,1024]{1,0:T(8,128)S(1)} %collective-permute-done, f32[1024,1024]{1,0:T(8,128)} %copy-done, s32[]{:T(128)S(6)} %select_n.57), kind=kLoop, calls=%fused_computation.22 | loop fusion | flops 524288 | bytes 6291460 | tf_op jit(solution)/shard_map/add | solution.py:91
  38.1 6.8 %all-to-all-start = ((f32[16,32,1024]{2,1,0:T(8,128)}), f32[16,32,1024]{2,1,0:T(8,128)S(1)}, u32[]{:S(2)}, u32[]{:S(2)}) async-start(f32[16,32,1024]{2,1,0:T(8,128)} %bitcast.8), calls=%async_computation | async-start | bytes 4194304 | tf_op jit(solution)/shard_map/all_to_all | solution.py:107
  45.0 4.1 %copy.8 = bf16[128,8192]{0,1:T(8,128)(2,1)} copy(bf16[128,8192]{1,0:T(8,128)(2,1)} %param.9) | data formatting | bytes 4194304 | tf_op args[1]
  49.2 3.9 %copy.9 = bf16[8,128,8,128]{3,1,2,0:T(8,128)(2,1)} copy(bf16[8,128,8,128]{1,3,2,0:T(8,128)(2,1)} %bitcast.59) | data formatting | bytes 4194304 | tf_op jit(solution)/shard_map/while | solution.py:139
  53.1 3.2 %all-gather.6.cloned.1.call-done = bf16[2304,1024]{1,0:T(8,128)(2,1)} async-done(((bf16[288,1024]{1,0:T(8,128)(2,1)}), bf16[2304,1024]{1,0:T(8,128)(2,1)}) %all-gather.6.cloned.1.call-update) | async-done | bytes 4718608 | tf_op jit(solution)/shard_map/all_gather | solution.py:141
  57.6 15.3 %while.20 = (s32[]{:T(128)}, bf16[8,128,256]{2,1,0:T(8,128)(2,1)}, bf16[8,128,8,128]{3,1,2,0:T(8,128)(2,1)}, bf16[8,256,128]{2,1,0:T(8,128)(2,1)S(1)}, s32[]{:T(128)}) while((s32[]{:T(128)}, bf16[8,128,256]{2,1,0:T(8,128)(2,1)}, bf16[8,128,8,128]{3,1,2,0:T(8,128)(2,1)}, bf16[8,256,128]{2,1,0:T(8,128)(2,1)S(1)}, s32[]{:T(128)}) %tuple.42), condition=%wide.region_3.4_spmd, body=%wide.region_1.0_spmd.sunk | while | flops 67403776 | bytes 656957 | solution.py:139
  57.6 1.3 convolution_reduce_fusion.4
  59.5 1.3 convolution_reduce_fusion.4
  61.4 1.3 convolution_reduce_fusion.4
  63.3 1.3 convolution_reduce_fusion.4
  65.2 1.3 convolution_reduce_fusion.4
  67.2 1.3 convolution_reduce_fusion.4
  69.1 1.3 convolution_reduce_fusion.4
  71.0 1.3 convolution_reduce_fusion.4
  72.9 4.1 %all-to-all-done = f32[16,32,1024]{2,1,0:T(8,128)S(1)} async-done(((f32[16,32,1024]{2,1,0:T(8,128)}), f32[16,32,1024]{2,1,0:T(8,128)S(1)}, u32[]{:S(2)}, u32[]{:S(2)}) %all-to-all-start) | async-done | bytes 2097184 | tf_op jit(solution)/shard_map/all_to_all | solution.py:107
  77.1 4.3 %collective-permute-start.1 = (f32[16,1024]{1,0:T(8,128)S(1)}, f32[16,1024]{1,0:T(8,128)S(1)}, u32[]{:S(2)}, u32[]{:S(2)}) collective-permute-start(f32[16,1024]{1,0:T(8,128)S(1)} %constant_dynamic-slice_fusion.1), channel_id=1, source_target_pairs={{0,4},{1,5},{2,6},{3,7},{4,0},{5,1},{6,2},{7,3},{8,12},{9,13},{10,... | collective-permute-start | bytes 196616 | tf_op jit(solution)/shard_map/ppermute | solution.py:84
  81.4 1.7 collective-permute-done.1
  83.1 1.5 collective-permute-start.2
  84.6 1.7 collective-permute-done.2
  86.3 1.2 collective-permute-start.3
  87.5 2.6 slice.11
  90.1 1.1 copy.14
  91.2 2.6 copy.12
  93.8 3.8 %collective-permute-start.4 = (f32[16,1024]{1,0:T(8,128)S(1)}, f32[16,1024]{1,0:T(8,128)S(1)}, u32[]{:S(2)}, u32[]{:S(2)}) collective-permute-start(f32[16,1024]{1,0:T(8,128)S(1)} %constant_dynamic-update-slice_fusion.4), channel_id=1, source_target_pairs={{0,4},{1,5},{2,6},{3,7},{4,0},{5,1},{6,2},{7,3},{8,12},{9,13},{10,... | collective-permute-start | bytes 196616 | tf_op jit(solution)/shard_map/ppermute | solution.py:84
  97.7 1.6 collective-permute-done.4
  100.0 27.0 %while.21 = (s32[]{:T(128)}, bf16[8,128,2048]{2,1,0:T(8,128)(2,1)}, bf16[8,128,8,128]{3,1,2,0:T(8,128)(2,1)}, bf16[8,2048,128]{2,1,0:T(8,128)(2,1)}, s32[]{:T(128)}) while((s32[]{:T(128)}, bf16[8,128,2048]{2,1,0:T(8,128)(2,1)}, bf16[8,128,8,128]{3,1,2,0:T(8,128)(2,1)}, bf16[8,2048,128]{2,1,0:T(8,128)(2,1)}, s32[]{:T(128)}) %tuple.52), condition=%wide.region_7.8_spmd, body=%wide.region_5.7_spmd.sunk | while | flops 539230208 | bytes 3409469 | solution.py:139
  100.0 2.5 convolution_reduce_fusion.5
  103.4 2.5 convolution_reduce_fusion.5
  106.8 2.5 convolution_reduce_fusion.5
  110.1 2.5 convolution_reduce_fusion.5
  113.5 2.5 convolution_reduce_fusion.5
  116.9 2.5 convolution_reduce_fusion.5
  120.3 2.5 convolution_reduce_fusion.5
  123.6 2.5 convolution_reduce_fusion.5
  127.0 20.0 %all-gather.4.cloned.1.call-done = f32[512,1024]{1,0:T(8,128)} async-done(((f32[32,1024]{1,0:T(8,128)}), f32[512,1024]{1,0:T(8,128)}) %all-gather.4.cloned.1.call-update) | async-done | bytes 2097168 | tf_op jit(solution)/shard_map/all_gather | solution.py:112
  147.0 1.5 collective-permute-start.5
  148.5 2.5 broadcast_in_dim.35
  151.0 1.4 constant_dynamic-update-slice_fusion.1
  152.5 1.5 constant_dynamic-update-slice_fusion.g_ref
  154.0 144.8 %shard_map.75 = f32[160,1024]{1,0:T(8,128)} custom-call(f32[1024,1024]{1,0:T(8,128)} %constant_dynamic-update-slice_fusion.g_ref, f32[160,1024]{1,0:T(8,128)} %s_ref.1), custom_call_target="tpu_custom_call" | custom-call | tf_op jit(solution)/shard_map/pallas_call | solution.py:71
  298.8 4.8 %convolution_convert_fusion = bf16[160,2048]{1,0:T(8,128)(2,1)} fusion(bf16[2048,1024]{1,0:T(8,128)(2,1)} %param.8, f32[160,1024]{1,0:T(8,128)} %shard_map.75), kind=kOutput, calls=%fused_computation.20 | convolution fusion | flops 671580160 | bytes 5505024 | tf_op jit(solution)/shard_map/dot_general | solution.py:151
  (50 shorter events, 17.1 us)
Async XLA Ops:
  7.2 49.1 %all-gather.6.cloned.1.call-start = ((), (), s32[]{:S(2)}) async-start(), calls=%async_computation.2 | async-start | bytes 5308416 | tf_op jit(solution)/shard_map/all_gather | solution.py:141
  25.6 2.0 copy-start
  29.3 5.4 %collective-permute-start = (f32[512,1024]{1,0:T(8,128)}, f32[512,1024]{1,0:T(8,128)S(1)}, u32[]{:S(2)}, u32[]{:S(2)}) collective-permute-start(f32[512,1024]{1,0:T(8,128)} %constant_dynamic-slice_fusion.2), channel_id=1, source_target_pairs={{0,1},{1,0},{2,3},{3,2},{4,5},{5,4},{6,7},{7,6},{8,9},{9,8},{10,11... | collective-permute-start | bytes 6291464 | tf_op jit(solution)/shard_map/ppermute | solution.py:84
  38.1 38.9 %all-to-all-start = ((f32[16,32,1024]{2,1,0:T(8,128)}), f32[16,32,1024]{2,1,0:T(8,128)S(1)}, u32[]{:S(2)}, u32[]{:S(2)}) async-start(f32[16,32,1024]{2,1,0:T(8,128)} %bitcast.8), calls=%async_computation | async-start | bytes 4194304 | tf_op jit(solution)/shard_map/all_to_all | solution.py:107
  44.9 102.1 %all-gather.4.cloned.1.call-start = ((), (), s32[]{:S(2)}) async-start(), calls=%async_computation.1 | async-start | bytes 2228224 | tf_op jit(solution)/shard_map/all_gather | solution.py:112
  77.1 6.0 %collective-permute-start.1 = (f32[16,1024]{1,0:T(8,128)S(1)}, f32[16,1024]{1,0:T(8,128)S(1)}, u32[]{:S(2)}, u32[]{:S(2)}) collective-permute-start(f32[16,1024]{1,0:T(8,128)S(1)} %constant_dynamic-slice_fusion.1), channel_id=1, source_target_pairs={{0,4},{1,5},{2,6},{3,7},{4,0},{5,1},{6,2},{7,3},{8,12},{9,13},{10,... | collective-permute-start | bytes 196616 | tf_op jit(solution)/shard_map/ppermute | solution.py:84
  83.1 3.2 %collective-permute-start.2 = (f32[8,1024]{1,0:T(8,128)S(1)}, f32[8,1024]{1,0:T(8,128)S(1)}, u32[]{:S(2)}, u32[]{:S(2)}) collective-permute-start(f32[8,1024]{1,0:T(8,128)S(1)} %constant_dynamic-slice_fusion), channel_id=1, source_target_pairs={{0,2},{1,3},{2,0},{3,1},{4,6},{5,7},{6,4},{7,5},{8,10},{9,11},{10,... | collective-permute-start | bytes 98312 | tf_op jit(solution)/shard_map/ppermute | solution.py:84
  86.3 7.5 %collective-permute-start.3 = (f32[8,1024]{1,0:T(8,128)S(1)}, f32[8,1024]{1,0:T(8,128)S(1)}, u32[]{:S(2)}, u32[]{:S(2)}) collective-permute-start(f32[8,1024]{1,0:T(8,128)S(1)} %get-tuple-element.83), channel_id=1, source_target_pairs={{0,2},{1,3},{2,0},{3,1},{4,6},{5,7},{6,4},{7,5},{8,10},{9,11},{10,... | collective-permute-start | bytes 98312 | tf_op jit(solution)/shard_map/ppermute | solution.py:84
  93.8 5.5 %collective-permute-start.4 = (f32[16,1024]{1,0:T(8,128)S(1)}, f32[16,1024]{1,0:T(8,128)S(1)}, u32[]{:S(2)}, u32[]{:S(2)}) collective-permute-start(f32[16,1024]{1,0:T(8,128)S(1)} %constant_dynamic-update-slice_fusion.4), channel_id=1, source_target_pairs={{0,4},{1,5},{2,6},{3,7},{4,0},{5,1},{6,2},{7,3},{8,12},{9,13},{10,... | collective-permute-start | bytes 196616 | tf_op jit(solution)/shard_map/ppermute | solution.py:84
  99.3 0.7 copy-start.2
  147.0 4.0 %copy-start.1 = (f32[512,1024]{1,0:T(8,128)S(1)}, f32[512,1024]{1,0:T(8,128)}, u32[]{:S(2)}) copy-start(f32[512,1024]{1,0:T(8,128)} %all-gather.4.cloned.1.call-done) | copy-start | bytes 6291460
  147.0 5.5 %collective-permute-start.5 = (f32[512,1024]{1,0:T(8,128)}, f32[512,1024]{1,0:T(8,128)S(1)}, u32[]{:S(2)}, u32[]{:S(2)}) collective-permute-start(f32[512,1024]{1,0:T(8,128)} %all-gather.4.cloned.1.call-done), channel_id=1, source_target_pairs={{0,1},{1,0},{2,3},{3,2},{4,5},{5,4},{6,7},{7,6},{8,9},{9,8},{10,11... | collective-permute-start | bytes 6291464 | tf_op jit(solution)/shard_map/ppermute | solution.py:84
Sparse Core Ops, SparseCore 0:
  18.1 38.1 all-gather.5
  100.1 46.8 all-gather.3

commit v11 on v9

--- a/solution.py
+++ b/solution.py
@@ -44,7 +44,9 @@
     return jnp.sum(diag, axis=1, keepdims=True), jnp.sum(diag, axis=0, keepdims=True)
 
 
-def _iterate_kernel(g_ref, s_ref, o_ref, a0_ref, e0_ref, a1_ref, e1_ref):
+def _iterate_kernel(g_ref, s_ref, k_ref, o_ref, c_ref, a0_ref, e0_ref, a1_ref, e1_ref, kv_ref, sem):
+    keys_in = pltpu.make_async_copy(k_ref, kv_ref, sem)
+    keys_in.start()
     o_ref[...] = s_ref[...]
 
     def step(i, carry):
@@ -63,21 +65,36 @@
         return carry
 
     lax.fori_loop(0, ITERS, step, 0)
+    keys_in.wait()
+    c_ref[...] = lax.dot_general(
+        o_ref[...].astype(jnp.bfloat16),
+        kv_ref[...],
+        (((1,), (1,)), ((), ())),
+        preferred_element_type=jnp.float32,
+    ).astype(jnp.bfloat16)
 
 
-def iterate(gram, start):
+def iterate(gram, start, keys):
     rank = start.shape[0]
     rest = rank - HALF
+    whole = pl.BlockSpec(memory_space=pltpu.VMEM)
     return pl.pallas_call(
         _iterate_kernel,
-        out_shape=jax.ShapeDtypeStruct(start.shape, jnp.float32),
+        out_shape=(
+            jax.ShapeDtypeStruct(start.shape, jnp.float32),
+            jax.ShapeDtypeStruct((rank, keys.shape[0]), jnp.bfloat16),
+        ),
+        in_specs=[whole, whole, pl.BlockSpec(memory_space=pl.ANY)],
+        out_specs=(whole, whole),
         scratch_shapes=[
             pltpu.VMEM((HALF, HALF), jnp.float32),
             pltpu.VMEM((HALF, HALF), jnp.float32),
             pltpu.VMEM((rest, rest), jnp.float32),
             pltpu.VMEM((rest, rest), jnp.float32),
+            pltpu.VMEM(keys.shape, keys.dtype),
+            pltpu.SemaphoreType.DMA(()),
         ],
-    )(gram, start)
+    )(gram, start, keys)
 
 
 def _swap(x, flip, axis="seq"):
@@ -144,11 +161,7 @@
         prefill_keys, prefill_keys, (((0,), (0,)), ((), ())), preferred_element_type=jnp.float32
     ) * inverse_tokens
     gram, outlier_scores, landmark_scores = sum_gram(local_gram, outlier_scores, landmark_scores)
-    subspace = iterate(gram, start_basis)
-    rounded = subspace.astype(jnp.bfloat16)
-    coefficients = lax.dot_general(
-        rounded, prefill_keys, (((1,), (1,)), ((), ())), preferred_element_type=jnp.float32
-    ).astype(jnp.bfloat16)
+    subspace, coefficients = iterate(gram, start_basis, prefill_keys)
     return (subspace, coefficients, landmark_scores, outlier_scores)
 
 

time: 309 us -> 306 us (level)
  matrix products: 42 us -> 37.2 us
    dot_general x1 -> x0, matrix products: 4.77 us -> none  [local(): lax.dot_general(rounded, prefill_keys, (((1,), (1,)), ((), ())), preferre...]
where the time goes in v11:
time: 306 us; the launch traced here: 305 us
  Pallas kernels  146 us (48%)
  matrix products  37.2 us (12%)
  local copies, waits for them, and re-layouts  27.8 us (9%)
  waiting for transfers between devices  26.6 us (9%)
  other arithmetic  22.2 us (7%)
  blocking collectives  15.7 us (5%)
  starting transfers between devices  15.1 us (5%)
  between operations  14.2 us (5%)
    pallas_call x1, Pallas kernels, iterate(): pl.pallas_call(_iterate_kernel, out_shape=(jax.ShapeDtypeStruct(start.sha...  146 us
    dot_general x16, matrix products, one_head(): jnp.einsum('qgd,cd->qgc', query_group, key_group, preferred_element_type=...  29.6 us
    all_gather x1, blocking collectives, local(): lax.all_gather(picked, 'seq', axis=0, tiled=True)  15.7 us
    all_gather x1, waiting for transfers between devices, sum_gram(): s = lax.all_gather(s, 'kv', axis=0, tiled=True)  15.4 us
    dynamic_update_slice x16, other arithmetic, score_rows(): return lax.map(one_head, (query_heads, key_heads))  12.3 us
    ppermute x6, waiting for transfers between devices, _swap(): lax.ppermute(x, axis, [(i, i ^ flip) for i in range(lax.axis_size(axis))])  11.1 us
    ppermute x6, starting transfers between devices, _swap(): lax.ppermute(x, axis, [(i, i ^ flip) for i in range(lax.axis_size(axis))])  8.23 us
    dot_general x1, matrix products, local(): lax.dot_general(prefill_keys, prefill_keys, (((0,), (0,)), ((), ())), pre...  7.64 us
  transfers between devices with their start and end apart: 9, of which 7 were waited for; matrix products, arithmetic and copies ran while one was open for 25% of the time, Pallas kernels for 0%

profile of v11, /device:TPU:1, one launch (start us, length us, event | category | flops | bytes accessed | tf_op | source)
XLA Modules:
  0.0 305.3 jit_solution(11126468949323790486)
XLA Ops:
  7.2 5.5 %convert_reduce_fusion = f32[256,1024]{1,0:T(8,128)S(1)} fusion(bf16[2048,1024]{1,0:T(8,128)(2,1)} %k_ref.1), kind=kLoop, calls=%fused_computation.19 | loop fusion | flops 3932160 | bytes 5242880 | tf_op jit(solution)/shard_map/reduce_sum | solution.py:140
  13.6 7.6 %convolution_multiply_fusion = f32[1024,1024]{1,0:T(8,128)S(1)} fusion(bf16[2048,1024]{1,0:T(8,128)(2,1)} %k_ref.1), kind=kOutput, calls=%fused_computation.20 | convolution fusion | flops 4296015872 | bytes 8388608 | tf_op jit(solution)/shard_map/dot_general | solution.py:160
  21.3 2.0 copy-done
  23.3 1.6 constant_dynamic-slice_fusion.2
  24.9 1.4 collective-permute-start
  26.5 3.2 %gather_fusion = bf16[4,8,1024]{2,1,0:T(8,128)(2,1)S(1)} fusion(bf16[256,8,1024]{2,1,0:T(8,128)(2,1)} %bitcast.52, s32[1024]{0:T(1024)S(1)} %pad_clamp_fusion), kind=kCustom, calls=%fused_computation | custom fusion | bytes 131088 | tf_op jit(solution)/shard_map/jit(_take)/gather | solution.py:141
  30.3 3.3 %dynamic-slice_add_fusion = f32[512,1024]{1,0:T(8,128)} fusion(f32[512,1024]{1,0:T(8,128)S(1)} %collective-permute-done, f32[1024,1024]{1,0:T(8,128)} %copy-done, s32[]{:T(128)S(6)} %select_n.57), kind=kLoop, calls=%fused_computation.21 | loop fusion | flops 524288 | bytes 6291460 | tf_op jit(solution)/shard_map/add | solution.py:108
  33.6 6.8 %all-to-all-start = ((f32[16,32,1024]{2,1,0:T(8,128)}), f32[16,32,1024]{2,1,0:T(8,128)S(1)}, u32[]{:S(2)}, u32[]{:S(2)}) async-start(f32[16,32,1024]{2,1,0:T(8,128)} %bitcast.8), calls=%async_computation | async-start | bytes 4194304 | tf_op jit(solution)/shard_map/all_to_all | solution.py:124
  40.5 15.7 %all_gather.9 = bf16[256,1024]{1,0:T(8,128)(2,1)S(1)} all-gather(bf16[32,1024]{1,0:T(8,128)(2,1)S(1)} %bitcast_select_fusion), channel_id=1, replica_groups=mesh['kv'=16,'seq'=8] {'seq'}, dimensions={0}, use_global_device_ids=true | all-gather | bytes 589824 | tf_op jit(solution)/shard_map/all_gather | solution.py:159
  56.2 4.1 %copy.19 = bf16[128,8192]{0,1:T(8,128)(2,1)} copy(bf16[128,8192]{1,0:T(8,128)(2,1)} %param.9) | data formatting | bytes 4194304 | tf_op args[1]
  60.2 3.9 %copy.21 = bf16[8,128,8,128]{3,1,2,0:T(8,128)(2,1)} copy(bf16[8,128,8,128]{1,3,2,0:T(8,128)(2,1)} %bitcast.53) | data formatting | bytes 4194304 | tf_op jit(solution)/shard_map/while | solution.py:156
  64.4 15.2 %while.20 = (s32[]{:T(128)}, bf16[8,128,256]{2,1,0:T(8,128)(2,1)}, bf16[8,128,8,128]{3,1,2,0:T(8,128)(2,1)}, bf16[8,256,128]{1,2,0:T(8,128)(2,1)S(1)}, s32[]{:T(128)}) while((s32[]{:T(128)}, bf16[8,128,256]{2,1,0:T(8,128)(2,1)}, bf16[8,128,8,128]{3,1,2,0:T(8,128)(2,1)}, bf16[8,256,128]{1,2,0:T(8,128)(2,1)S(1)}, s32[]{:T(128)}) %tuple.58), condition=%wide.region_2.3_spmd, body=%wide.region_0.2_spmd.sunk | while | flops 67403776 | bytes 656957 | solution.py:156
  64.4 1.2 convolution_reduce_fusion.4
  66.3 1.2 convolution_reduce_fusion.4
  68.2 1.2 convolution_reduce_fusion.4
  70.1 1.2 convolution_reduce_fusion.4
  72.0 1.2 convolution_reduce_fusion.4
  73.9 1.2 convolution_reduce_fusion.4
  75.8 1.2 convolution_reduce_fusion.4
  77.7 1.2 convolution_reduce_fusion.4
  79.7 1.3 collective-permute-start.1
  81.0 3.9 %collective-permute-done.1 = f32[16,1024]{1,0:T(8,128)S(1)} collective-permute-done((f32[16,1024]{1,0:T(8,128)S(1)}, f32[16,1024]{1,0:T(8,128)S(1)}, u32[]{:S(2)}, u32[]{:S(2)}) %collective-permute-start.1) | collective-permute-done | bytes 65568 | tf_op jit(solution)/shard_map/ppermute | solution.py:101
  84.9 1.1 collective-permute-start.2
  86.0 1.8 collective-permute-done.2
  87.8 1.1 collective-permute-start.3
  88.8 1.8 collective-permute-done.3
  90.6 1.9 collective-permute-start.4
  92.5 3.0 collective-permute-done.4
  96.3 6.5 %copy.23 = bf16[2048,1024]{0,1:T(8,128)(2,1)} copy(bf16[2048,1024]{1,0:T(8,128)(2,1)} %all-gather.5.cloned.1.call-done) | data formatting | bytes 8388608 | tf_op jit(solution)/shard_map/all_gather | solution.py:158
  102.8 26.8 %while.21 = (s32[]{:T(128)}, bf16[8,128,2048]{2,1,0:T(8,128)(2,1)}, bf16[8,128,8,128]{3,1,2,0:T(8,128)(2,1)}, bf16[8,2048,128]{1,2,0:T(8,128)(2,1)}, s32[]{:T(128)}) while((s32[]{:T(128)}, bf16[8,128,2048]{2,1,0:T(8,128)(2,1)}, bf16[8,128,8,128]{3,1,2,0:T(8,128)(2,1)}, bf16[8,2048,128]{1,2,0:T(8,128)(2,1)}, s32[]{:T(128)}) %tuple.57), condition=%wide.region_7.8_spmd, body=%wide.region_5.7_spmd.sunk | while | flops 539230208 | bytes 3409469 | solution.py:156
  102.8 2.5 convolution_reduce_fusion.5
  105.3 0.9 fusion.27
  106.2 2.5 convolution_reduce_fusion.5
  109.6 2.5 convolution_reduce_fusion.5
  112.0 0.9 fusion.27
  112.9 2.5 convolution_reduce_fusion.5
  115.4 0.9 fusion.27
  116.3 2.5 convolution_reduce_fusion.5
  118.7 0.9 fusion.27
  119.6 2.5 convolution_reduce_fusion.5
  123.0 2.5 convolution_reduce_fusion.5
  126.3 2.5 convolution_reduce_fusion.5
  129.7 15.4 %all-gather.3.cloned.1.call-done = f32[512,1024]{1,0:T(8,128)} async-done(((f32[32,1024]{1,0:T(8,128)}), f32[512,1024]{1,0:T(8,128)}) %all-gather.3.cloned.1.call-update) | async-done | bytes 2097168 | tf_op jit(solution)/shard_map/all_gather | solution.py:129
  145.1 1.5 collective-permute-start.5
  146.6 2.5 broadcast_in_dim.35
  149.1 1.5 constant_dynamic-update-slice_fusion.1
  150.6 1.5 constant_dynamic-update-slice_fusion.g_ref
  152.1 146.3 %shard_map.75 = (f32[160,1024]{1,0:T(8,128)}, bf16[160,2048]{1,0:T(8,128)(2,1)}) custom-call(f32[1024,1024]{1,0:T(8,128)} %constant_dynamic-update-slice_fusion.g_ref, f32[160,1024]{1,0:T(8,128)} %s_ref.1, bf16[2048,1024]{1,0:T(8,128)(2,1)} %k_ref.1), custom_call_target="tpu_custom_call" | custom-call | tf_op jit(solution)/shard_map/pallas_call | solution.py:81
  (47 shorter events, 11.7 us)
Async XLA Ops:
  7.2 89.1 %all-gather.5.cloned.1.call-start = ((), (), s32[]{:S(2)}) async-start(), calls=%async_computation.2 | async-start | bytes 4718592 | tf_op jit(solution)/shard_map/all_gather | solution.py:158
  21.2 2.0 copy-start
  23.3 3.0 copy-start.3
  24.9 5.4 %collective-permute-start = (f32[512,1024]{1,0:T(8,128)}, f32[512,1024]{1,0:T(8,128)S(1)}, u32[]{:S(2)}, u32[]{:S(2)}) collective-permute-start(f32[512,1024]{1,0:T(8,128)} %constant_dynamic-slice_fusion.2), channel_id=1, source_target_pairs={{0,1},{1,0},{2,3},{3,2},{4,5},{5,4},{6,7},{7,6},{8,9},{9,8},{10,11... | collective-permute-start | bytes 6291464 | tf_op jit(solution)/shard_map/ppermute | solution.py:101
  33.6 46.0 %all-to-all-start = ((f32[16,32,1024]{2,1,0:T(8,128)}), f32[16,32,1024]{2,1,0:T(8,128)S(1)}, u32[]{:S(2)}, u32[]{:S(2)}) async-start(f32[16,32,1024]{2,1,0:T(8,128)} %bitcast.8), calls=%async_computation | async-start | bytes 4194304 | tf_op jit(solution)/shard_map/all_to_all | solution.py:124
  40.5 104.7 %all-gather.3.cloned.1.call-start = ((), (), s32[]{:S(2)}) async-start(), calls=%async_computation.1 | async-start | bytes 2228224 | tf_op jit(solution)/shard_map/all_gather | solution.py:129
  79.7 5.1 %collective-permute-start.1 = (f32[16,1024]{1,0:T(8,128)S(1)}, f32[16,1024]{1,0:T(8,128)S(1)}, u32[]{:S(2)}, u32[]{:S(2)}) collective-permute-start(f32[16,1024]{1,0:T(8,128)S(1)} %constant_dynamic-slice_fusion.1), channel_id=1, source_target_pairs={{0,4},{1,5},{2,6},{3,7},{4,0},{5,1},{6,2},{7,3},{8,12},{9,13},{10,... | collective-permute-start | bytes 196616 | tf_op jit(solution)/shard_map/ppermute | solution.py:101
  84.9 2.8 collective-permute-start.2
  87.8 2.8 collective-permute-start.3
  90.6 5.0 %collective-permute-start.4 = (f32[16,1024]{1,0:T(8,128)S(1)}, f32[16,1024]{1,0:T(8,128)S(1)}, u32[]{:S(2)}, u32[]{:S(2)}) collective-permute-start(f32[16,1024]{1,0:T(8,128)S(1)} %constant_dynamic-update-slice_fusion.4), channel_id=1, source_target_pairs={{0,4},{1,5},{2,6},{3,7},{4,0},{5,1},{6,2},{7,3},{8,12},{9,13},{10,... | collective-permute-start | bytes 196616 | tf_op jit(solution)/shard_map/ppermute | solution.py:101
  95.6 0.7 copy-start.2
  145.1 4.0 %copy-start.1 = (f32[512,1024]{1,0:T(8,128)S(1)}, f32[512,1024]{1,0:T(8,128)}, u32[]{:S(2)}) copy-start(f32[512,1024]{1,0:T(8,128)} %all-gather.3.cloned.1.call-done) | copy-start | bytes 6291460
  145.1 5.5 %collective-permute-start.5 = (f32[512,1024]{1,0:T(8,128)}, f32[512,1024]{1,0:T(8,128)S(1)}, u32[]{:S(2)}, u32[]{:S(2)}) collective-permute-start(f32[512,1024]{1,0:T(8,128)} %all-gather.3.cloned.1.call-done), channel_id=1, source_target_pairs={{0,1},{1,0},{2,3},{3,2},{4,5},{5,4},{6,7},{7,6},{8,9},{9,8},{10,11... | collective-permute-start | bytes 6291464 | tf_op jit(solution)/shard_map/ppermute | solution.py:101
Sparse Core Ops, SparseCore 0:
  13.7 36.3 all-gather.4
  96.4 48.6 all-gather.2

commit v12 on v11

--- a/solution.py
+++ b/solution.py
@@ -120,7 +120,8 @@
     seq = lax.axis_index("seq")
     kv_size = lax.axis_size("kv")
     core, z_low, z_high = seq % 2, (seq // 2) % 2, (seq // 4) % 2
-    s = _halve(local_gram, core, 1)
+    keep, send = local_gram
+    s = keep + _swap(send, 1)
     s = lax.all_to_all(s.reshape((kv_size, -1) + s.shape[1:]), "kv", 0, 0, tiled=True)
     s, early = lax.optimization_barrier((s, early))
     s = jnp.sum(s, axis=0)
@@ -157,9 +158,16 @@
 
     landmark_scores = score_rows(lax.all_gather(landmarks, "seq", axis=0, tiled=True))
     outlier_scores = score_rows(lax.all_gather(picked, "seq", axis=0, tiled=True))
-    local_gram = lax.dot_general(
-        prefill_keys, prefill_keys, (((0,), (0,)), ((), ())), preferred_element_type=jnp.float32
-    ) * inverse_tokens
+    half = width // 2
+    core = lax.axis_index("seq") % 2
+
+    def gram_rows(start):
+        cols = lax.dynamic_slice_in_dim(prefill_keys, start, half, axis=1)
+        return lax.dot_general(
+            cols, prefill_keys, (((0,), (0,)), ((), ())), preferred_element_type=jnp.float32
+        ) * inverse_tokens
+
+    local_gram = (gram_rows(core * half), gram_rows((1 - core) * half))
     gram, outlier_scores, landmark_scores = sum_gram(local_gram, outlier_scores, landmark_scores)
     subspace, coefficients = iterate(gram, start_basis, prefill_keys)
     return (subspace, coefficients, landmark_scores, outlier_scores)

time: 306 us -> 304 us (level)
  matrix products: 37.2 us -> 43.2 us
  local copies, waits for them, and re-layouts: 27.8 us -> 23.7 us
  other arithmetic: 22.2 us -> 18.9 us
    dot_general x1 -> x2, matrix products: 7.64 us -> 13.7 us  [gram_rows(): lax.dot_general(cols, prefill_keys, (((0,), (0,)), ((), ())), preferred_e...]
    add x2 -> x1, other arithmetic: 3.35 us -> 0.01 us  [_halve(): return keep + _swap(send, flip)]
    unnamed x9 -> x7, local copies, waits for them, and re-layouts: 6.73 us -> 4.72 us
  transfers between devices with their start and end apart: 9 -> 9, of which waited for: 7 -> 7; matrix products, arithmetic and copies ran while one was open for 25% -> 26% of each run, Pallas kernels for 0% -> 0%
where the time goes in v12:
time: 304 us; the launch traced here: 303 us
  Pallas kernels  146 us (48%)
  matrix products  43.2 us (14%)
  waiting for transfers between devices  27.7 us (9%)
  local copies, waits for them, and re-layouts  23.7 us (8%)
  other arithmetic  18.9 us (6%)
  blocking collectives  15.5 us (5%)
  between operations  14.2 us (5%)
  starting transfers between devices  13.6 us (4%)
    pallas_call x1, Pallas kernels, iterate(): pl.pallas_call(_iterate_kernel, out_shape=(jax.ShapeDtypeStruct(start.sha...  146 us
    dot_general x16, matrix products, one_head(): jnp.einsum('qgd,cd->qgc', query_group, key_group, preferred_element_type=...  29.6 us
    all_gather x1, blocking collectives, local(): lax.all_gather(picked, 'seq', axis=0, tiled=True)  15.5 us
    all_gather x1, waiting for transfers between devices, sum_gram(): s = lax.all_gather(s, 'kv', axis=0, tiled=True)  15 us
    dot_general x2, matrix products, gram_rows(): lax.dot_general(cols, prefill_keys, (((0,), (0,)), ((), ())), preferred_e...  13.7 us
    ppermute x6, waiting for transfers between devices, _swap(): lax.ppermute(x, axis, [(i, i ^ flip) for i in range(lax.axis_size(axis))])  12.7 us
    dynamic_update_slice x16, other arithmetic, score_rows(): return lax.map(one_head, (query_heads, key_heads))  12.3 us
    all_to_all x1, starting transfers between devices, sum_gram(): lax.all_to_all(s.reshape((kv_size, -1) + s.shape[1:]), 'kv', 0, 0, tiled=...  6.83 us
  transfers between devices with their start and end apart: 9, of which 7 were waited for; matrix products, arithmetic and copies ran while one was open for 26% of the time, Pallas kernels for 0%

profile of v12, /device:TPU:1, one launch (start us, length us, event | category | flops | bytes accessed | tf_op | source)
XLA Modules:
  0.0 303.2 jit_solution(3841089212595835042)
XLA Ops:
  7.2 5.5 %convert_reduce_fusion = f32[256,1024]{1,0:T(8,128)S(1)} fusion(bf16[2048,1024]{1,0:T(8,128)(2,1)} %k_ref.1), kind=kLoop, calls=%fused_computation.19 | loop fusion | flops 3932160 | bytes 5242880 | tf_op jit(solution)/shard_map/reduce_sum | solution.py:141
  13.6 6.6 %fusion.18 = f32[512,1024]{1,0:T(8,128)} fusion(bf16[2048,1024]{1,0:T(8,128)(2,1)} %k_ref.1, s32[]{:T(128)S(6)} %select_n.60), kind=kOutput, calls=%fused_computation.25 | convolution fusion | flops 2148007936 | bytes 8388612 | tf_op jit(solution)/shard_map/dot_general | solution.py:166
  20.2 1.3 collective-permute-start
  21.7 2.7 gather_fusion
  24.6 1.0 collective-permute-done
  25.5 7.1 %multiply_add_fusion = f32[512,1024]{1,0:T(8,128)} fusion(f32[512,1024]{1,0:T(8,128)S(1)} %collective-permute-done, bf16[2048,1024]{1,0:T(8,128)(2,1)} %k_ref.1, s32[]{:T(128)S(6)} %select_n.59), kind=kOutput, calls=%fused_computation.22 | convolution fusion | flops 2148532224 | bytes 10485764 | tf_op jit(solution)/shard_map/dot_general | solution.py:166
  32.6 6.8 %all-to-all-start = ((f32[16,32,1024]{2,1,0:T(8,128)}), f32[16,32,1024]{2,1,0:T(8,128)S(1)}, u32[]{:S(2)}, u32[]{:S(2)}) async-start(f32[16,32,1024]{2,1,0:T(8,128)} %bitcast.55), calls=%async_computation | async-start | bytes 4194304 | tf_op jit(solution)/shard_map/all_to_all | solution.py:125
  39.5 15.5 %all_gather.9 = bf16[256,1024]{1,0:T(8,128)(2,1)S(1)} all-gather(bf16[32,1024]{1,0:T(8,128)(2,1)S(1)} %bitcast_select_fusion), channel_id=1, replica_groups=mesh['kv'=16,'seq'=8] {'seq'}, dimensions={0}, use_global_device_ids=true | all-gather | bytes 589824 | tf_op jit(solution)/shard_map/all_gather | solution.py:160
  54.9 4.1 %copy.19 = bf16[128,8192]{0,1:T(8,128)(2,1)} copy(bf16[128,8192]{1,0:T(8,128)(2,1)} %param.9) | data formatting | bytes 4194304 | tf_op args[1]
  59.0 3.9 %copy.21 = bf16[8,128,8,128]{3,1,2,0:T(8,128)(2,1)} copy(bf16[8,128,8,128]{1,3,2,0:T(8,128)(2,1)} %bitcast.53) | data formatting | bytes 4194304 | tf_op jit(solution)/shard_map/while | solution.py:157
  63.1 15.2 %while.20 = (s32[]{:T(128)}, bf16[8,128,256]{2,1,0:T(8,128)(2,1)}, bf16[8,128,8,128]{3,1,2,0:T(8,128)(2,1)}, bf16[8,256,128]{1,2,0:T(8,128)(2,1)S(1)}, s32[]{:T(128)}) while((s32[]{:T(128)}, bf16[8,128,256]{2,1,0:T(8,128)(2,1)}, bf16[8,128,8,128]{3,1,2,0:T(8,128)(2,1)}, bf16[8,256,128]{1,2,0:T(8,128)(2,1)S(1)}, s32[]{:T(128)}) %tuple.58), condition=%wide.region_2.3_spmd, body=%wide.region_0.2_spmd.sunk | while | flops 67403776 | bytes 656957 | solution.py:157
  63.2 1.2 convolution_reduce_fusion.4
  65.1 1.2 convolution_reduce_fusion.4
  67.0 1.2 convolution_reduce_fusion.4
  68.9 1.2 convolution_reduce_fusion.4
  70.8 1.2 convolution_reduce_fusion.4
  72.6 1.2 convolution_reduce_fusion.4
  74.5 1.2 convolution_reduce_fusion.4
  76.4 1.2 convolution_reduce_fusion.4
  78.5 1.3 collective-permute-start.1
  79.8 3.8 %collective-permute-done.1 = f32[16,1024]{1,0:T(8,128)S(1)} collective-permute-done((f32[16,1024]{1,0:T(8,128)S(1)}, f32[16,1024]{1,0:T(8,128)S(1)}, u32[]{:S(2)}, u32[]{:S(2)}) %collective-permute-start.1) | collective-permute-done | bytes 65568 | tf_op jit(solution)/shard_map/ppermute | solution.py:101
  84.2 2.3 collective-permute-done.2
  87.1 2.3 collective-permute-done.3
  89.4 1.4 collective-permute-start.4
  90.8 3.2 %collective-permute-done.4 = f32[16,1024]{1,0:T(8,128)S(1)} collective-permute-done((f32[16,1024]{1,0:T(8,128)S(1)}, f32[16,1024]{1,0:T(8,128)S(1)}, u32[]{:S(2)}, u32[]{:S(2)}) %collective-permute-start.4) | collective-permute-done | bytes 65568 | tf_op jit(solution)/shard_map/ppermute | solution.py:101
  94.8 6.5 %copy.23 = bf16[2048,1024]{0,1:T(8,128)(2,1)} copy(bf16[2048,1024]{1,0:T(8,128)(2,1)} %all-gather.5.cloned.1.call-done) | data formatting | bytes 8388608 | tf_op jit(solution)/shard_map/all_gather | solution.py:159
  101.3 26.8 %while.21 = (s32[]{:T(128)}, bf16[8,128,2048]{2,1,0:T(8,128)(2,1)}, bf16[8,128,8,128]{3,1,2,0:T(8,128)(2,1)}, bf16[8,2048,128]{1,2,0:T(8,128)(2,1)}, s32[]{:T(128)}) while((s32[]{:T(128)}, bf16[8,128,2048]{2,1,0:T(8,128)(2,1)}, bf16[8,128,8,128]{3,1,2,0:T(8,128)(2,1)}, bf16[8,2048,128]{1,2,0:T(8,128)(2,1)}, s32[]{:T(128)}) %tuple.57), condition=%wide.region_7.8_spmd, body=%wide.region_5.7_spmd.sunk | while | flops 539230208 | bytes 3409469 | solution.py:157
  101.3 2.5 convolution_reduce_fusion.5
  103.7 0.9 fusion.38
  104.6 2.5 convolution_reduce_fusion.5
  107.1 0.9 fusion.38
  108.0 2.5 convolution_reduce_fusion.5
  110.4 0.9 fusion.38
  111.3 2.5 convolution_reduce_fusion.5
  113.8 0.9 fusion.38
  114.7 2.5 convolution_reduce_fusion.5
  117.2 0.9 fusion.38
  118.0 2.5 convolution_reduce_fusion.5
  121.4 2.5 convolution_reduce_fusion.5
  123.9 0.9 fusion.38
  124.8 2.5 convolution_reduce_fusion.5
  127.2 0.9 fusion.38
  128.1 15.0 %all-gather.3.cloned.1.call-done = f32[512,1024]{1,0:T(8,128)} async-done(((f32[32,1024]{1,0:T(8,128)}), f32[512,1024]{1,0:T(8,128)}) %all-gather.3.cloned.1.call-update) | async-done | bytes 2097168 | tf_op jit(solution)/shard_map/all_gather | solution.py:130
  143.1 1.5 collective-permute-start.5
  144.6 2.5 broadcast_in_dim.35
  147.1 1.5 constant_dynamic-update-slice_fusion.1
  148.6 1.5 constant_dynamic-update-slice_fusion.g_ref
  150.1 146.3 %shard_map.75 = (f32[160,1024]{1,0:T(8,128)}, bf16[160,2048]{1,0:T(8,128)(2,1)}) custom-call(f32[1024,1024]{1,0:T(8,128)} %constant_dynamic-update-slice_fusion.g_ref, f32[160,1024]{1,0:T(8,128)} %s_ref.1, bf16[2048,1024]{1,0:T(8,128)(2,1)} %k_ref.1), custom_call_target="tpu_custom_call" | custom-call | tf_op jit(solution)/shard_map/pallas_call | solution.py:81
  (44 shorter events, 9.6 us)
Async XLA Ops:
  7.2 87.6 %all-gather.5.cloned.1.call-start = ((), (), s32[]{:S(2)}) async-start(), calls=%async_computation.2 | async-start | bytes 4718592 | tf_op jit(solution)/shard_map/all_gather | solution.py:159
  13.6 7.9 %copy-start.2 = (s32[4]{0:T(128)S(1)}, s32[4]{0:T(128)}, u32[]{:S(2)}) copy-start(s32[4]{0:T(128)} %param.10) | copy-start | bytes 52
  20.2 5.3 %collective-permute-start = (f32[512,1024]{1,0:T(8,128)}, f32[512,1024]{1,0:T(8,128)S(1)}, u32[]{:S(2)}, u32[]{:S(2)}) collective-permute-start(f32[512,1024]{1,0:T(8,128)} %fusion.18), channel_id=1, source_target_pairs={{0,1},{1,0},{2,3},{3,2},{4,5},{5,4},{6,7},{7,6},{8,9},{9,8},{10,11... | collective-permute-start | bytes 6291464 | tf_op jit(solution)/shard_map/ppermute | solution.py:101
  32.6 45.8 %all-to-all-start = ((f32[16,32,1024]{2,1,0:T(8,128)}), f32[16,32,1024]{2,1,0:T(8,128)S(1)}, u32[]{:S(2)}, u32[]{:S(2)}) async-start(f32[16,32,1024]{2,1,0:T(8,128)} %bitcast.55), calls=%async_computation | async-start | bytes 4194304 | tf_op jit(solution)/shard_map/all_to_all | solution.py:125
  39.4 103.6 %all-gather.3.cloned.1.call-start = ((), (), s32[]{:S(2)}) async-start(), calls=%async_computation.1 | async-start | bytes 2228224 | tf_op jit(solution)/shard_map/all_gather | solution.py:130
  78.5 5.1 %collective-permute-start.1 = (f32[16,1024]{1,0:T(8,128)S(1)}, f32[16,1024]{1,0:T(8,128)S(1)}, u32[]{:S(2)}, u32[]{:S(2)}) collective-permute-start(f32[16,1024]{1,0:T(8,128)S(1)} %constant_dynamic-slice_fusion.1), channel_id=1, source_target_pairs={{0,4},{1,5},{2,6},{3,7},{4,0},{5,1},{6,2},{7,3},{8,12},{9,13},{10,... | collective-permute-start | bytes 196616 | tf_op jit(solution)/shard_map/ppermute | solution.py:101
  83.6 2.8 collective-permute-start.2
  86.5 2.8 collective-permute-start.3
  89.4 4.7 %collective-permute-start.4 = (f32[16,1024]{1,0:T(8,128)S(1)}, f32[16,1024]{1,0:T(8,128)S(1)}, u32[]{:S(2)}, u32[]{:S(2)}) collective-permute-start(f32[16,1024]{1,0:T(8,128)S(1)} %constant_dynamic-update-slice_fusion.4), channel_id=1, source_target_pairs={{0,4},{1,5},{2,6},{3,7},{4,0},{5,1},{6,2},{7,3},{8,12},{9,13},{10,... | collective-permute-start | bytes 196616 | tf_op jit(solution)/shard_map/ppermute | solution.py:101
  94.1 0.7 copy-start.1
  143.1 4.0 %copy-start = (f32[512,1024]{1,0:T(8,128)S(1)}, f32[512,1024]{1,0:T(8,128)}, u32[]{:S(2)}) copy-start(f32[512,1024]{1,0:T(8,128)} %all-gather.3.cloned.1.call-done) | copy-start | bytes 6291460
  143.1 5.5 %collective-permute-start.5 = (f32[512,1024]{1,0:T(8,128)}, f32[512,1024]{1,0:T(8,128)S(1)}, u32[]{:S(2)}, u32[]{:S(2)}) collective-permute-start(f32[512,1024]{1,0:T(8,128)} %all-gather.3.cloned.1.call-done), channel_id=1, source_target_pairs={{0,1},{1,0},{2,3},{3,2},{4,5},{5,4},{6,7},{7,6},{8,9},{9,8},{10,11... | collective-permute-start | bytes 6291464 | tf_op jit(solution)/shard_map/ppermute | solution.py:101
Sparse Core Ops, SparseCore 0:
  13.7 36.6 all-gather.4
  94.9 48.1 all-gather.2

commit v13 on v12

--- a/solution.py
+++ b/solution.py
@@ -138,7 +138,12 @@
     inverse_tokens = 1.0 / (rows_dev * lax.axis_size("kv") * lax.axis_size("seq"))
     scale_factor = 1.0 / math.sqrt(HEAD)
     spanned = prefill_keys.reshape(rows_dev // SPAN, SPAN, width)
-    landmarks = jnp.mean(spanned, axis=1, dtype=jnp.float32).astype(jnp.bfloat16)
+    span_of_row = lax.broadcasted_iota(jnp.int32, (rows_dev // SPAN, rows_dev), 1) // SPAN
+    span_index = lax.broadcasted_iota(jnp.int32, (rows_dev // SPAN, rows_dev), 0)
+    averaging = jnp.where(span_of_row == span_index, 1.0 / SPAN, 0.0).astype(jnp.bfloat16)
+    landmarks = jnp.dot(averaging, prefill_keys, preferred_element_type=jnp.float32).astype(
+        jnp.bfloat16
+    )
     picked = jnp.take(spanned, outlier_spans, axis=0).reshape(-1, width)
     query_count = queries.shape[0]
     query_heads = jnp.transpose(queries.reshape(query_count, KVH, GROUP, HEAD), (1, 0, 2, 3))

time: 304 us -> 302 us (level)
  other arithmetic: 18.9 us -> 12.6 us
  matrix products: 43.2 us -> 47.5 us
    all_gather x1 -> x0, local copies, waits for them, and re-layouts: 6.49 us -> none  [local(): lax.all_gather(landmarks, 'seq', axis=0, tiled=True)]
    reduce_sum x1 -> x0, other arithmetic: 5.47 us -> none  [local(): jnp.mean(spanned, axis=1, dtype=jnp.float32).astype(jnp.bfloat16)]
    transpose x0 -> x1, local copies, waits for them, and re-layouts: none -> 4.9 us  [score_rows(): key_heads = jnp.swapaxes(shard_rows.reshape(count_rows, KVH, HEAD), 0, 1)]
    dot_general x0 -> x1, matrix products: none -> 4.24 us  [local(): jnp.dot(averaging, prefill_keys, preferred_element_type=jnp.float32)]
  transfers between devices with their start and end apart: 9 -> 9, of which waited for: 7 -> 7; matrix products, arithmetic and copies ran while one was open for 26% -> 25% of each run, Pallas kernels for 0% -> 0%
where the time goes in v13:
time: 302 us; the launch traced here: 301 us
  Pallas kernels  146 us (48%)
  matrix products  47.5 us (16%)
  waiting for transfers between devices  29.2 us (10%)
  local copies, waits for them, and re-layouts  22.1 us (7%)
  blocking collectives  15.5 us (5%)
  between operations  14.2 us (5%)
  starting transfers between devices  13.6 us (5%)
  other arithmetic  12.6 us (4%)
    pallas_call x1, Pallas kernels, iterate(): pl.pallas_call(_iterate_kernel, out_shape=(jax.ShapeDtypeStruct(start.sha...  146 us
    dot_general x16, matrix products, one_head(): jnp.einsum('qgd,cd->qgc', query_group, key_group, preferred_element_type=...  29.7 us
    all_gather x1, waiting for transfers between devices, sum_gram(): s = lax.all_gather(s, 'kv', axis=0, tiled=True)  16.5 us
    all_gather x1, blocking collectives, local(): lax.all_gather(picked, 'seq', axis=0, tiled=True)  15.5 us
    dot_general x2, matrix products, gram_rows(): lax.dot_general(cols, prefill_keys, (((0,), (0,)), ((), ())), preferred_e...  13.6 us
    ppermute x6, waiting for transfers between devices, _swap(): lax.ppermute(x, axis, [(i, i ^ flip) for i in range(lax.axis_size(axis))])  12.7 us
    dynamic_update_slice x16, other arithmetic, score_rows(): return lax.map(one_head, (query_heads, key_heads))  12.3 us
    all_to_all x1, starting transfers between devices, sum_gram(): lax.all_to_all(s.reshape((kv_size, -1) + s.shape[1:]), 'kv', 0, 0, tiled=...  6.83 us
  transfers between devices with their start and end apart: 9, of which 7 were waited for; matrix products, arithmetic and copies ran while one was open for 25% of the time, Pallas kernels for 0%

profile of v13, /device:TPU:1, one launch (start us, length us, event | category | flops | bytes accessed | tf_op | source)
XLA Modules:
  0.0 301.2 jit_solution(10196315018236379532)
XLA Ops:
  7.2 4.2 %convolution_convert_fusion = bf16[256,1024]{1,0:T(8,128)(2,1)} fusion(bf16[2048,1024]{1,0:T(8,128)(2,1)} %k_ref.1, s32[2048]{0:T(1024)S(1)} %get-tuple-element.96, s32[2048]{0:T(1024)S(1)} %get-tuple-element.97, pred[2048]{0:T(1024)(128)(4,1)S(1)} %fusion.30), kind=kOutput, calls=%fused_computation.28 | convolution fusion | flops 1076101120 | bytes 4737024 | tf_op jit(solution)/shard_map/dot_general | solution.py:144
  11.5 6.5 %fusion.18 = f32[512,1024]{1,0:T(8,128)} fusion(bf16[2048,1024]{1,0:T(8,128)(2,1)} %k_ref.1, s32[]{:T(128)S(6)} %select_n.69), kind=kOutput, calls=%fused_computation.27 | convolution fusion | flops 2148007936 | bytes 8388612 | tf_op jit(solution)/shard_map/dot_general | solution.py:171
  18.1 1.4 collective-permute-start
  19.6 2.7 gather_fusion
  22.5 1.0 collective-permute-done
  23.4 7.1 %multiply_add_fusion = f32[512,1024]{1,0:T(8,128)} fusion(f32[512,1024]{1,0:T(8,128)S(1)} %collective-permute-done, bf16[2048,1024]{1,0:T(8,128)(2,1)} %k_ref.1, s32[]{:T(128)S(6)} %select_n.68), kind=kOutput, calls=%fused_computation.24 | convolution fusion | flops 2148532224 | bytes 10485764 | tf_op jit(solution)/shard_map/dot_general | solution.py:171
  30.5 6.8 %all-to-all-start = ((f32[16,32,1024]{2,1,0:T(8,128)}), f32[16,32,1024]{2,1,0:T(8,128)S(1)}, u32[]{:S(2)}, u32[]{:S(2)}) async-start(f32[16,32,1024]{2,1,0:T(8,128)} %bitcast.57), calls=%async_computation | async-start | bytes 4194304 | tf_op jit(solution)/shard_map/all_to_all | solution.py:125
  37.4 15.5 %all_gather.9 = bf16[256,1024]{1,0:T(8,128)(2,1)S(1)} all-gather(bf16[32,1024]{1,0:T(8,128)(2,1)S(1)} %bitcast_select_fusion), channel_id=1, replica_groups=mesh['kv'=16,'seq'=8] {'seq'}, dimensions={0}, use_global_device_ids=true | all-gather | bytes 589824 | tf_op jit(solution)/shard_map/all_gather | solution.py:165
  52.9 4.1 %copy.14 = bf16[128,8192]{0,1:T(8,128)(2,1)} copy(bf16[128,8192]{1,0:T(8,128)(2,1)} %param.9) | data formatting | bytes 4194304 | tf_op args[1]
  56.9 3.9 %copy.16 = bf16[8,128,8,128]{3,1,2,0:T(8,128)(2,1)} copy(bf16[8,128,8,128]{1,3,2,0:T(8,128)(2,1)} %bitcast.55) | data formatting | bytes 4194304 | tf_op jit(solution)/shard_map/while | solution.py:162
  61.1 15.2 %while.20 = (s32[]{:T(128)}, bf16[8,128,256]{2,1,0:T(8,128)(2,1)}, bf16[8,128,8,128]{3,1,2,0:T(8,128)(2,1)}, bf16[8,256,128]{1,2,0:T(8,128)(2,1)S(1)}, s32[]{:T(128)}) while((s32[]{:T(128)}, bf16[8,128,256]{2,1,0:T(8,128)(2,1)}, bf16[8,128,8,128]{3,1,2,0:T(8,128)(2,1)}, bf16[8,256,128]{1,2,0:T(8,128)(2,1)S(1)}, s32[]{:T(128)}) %tuple.56), condition=%wide.region_2.3_spmd, body=%wide.region_0.2_spmd.sunk | while | flops 67403776 | bytes 656957 | solution.py:162
  61.1 1.2 convolution_reduce_fusion.4
  63.0 1.2 convolution_reduce_fusion.4
  64.9 1.2 convolution_reduce_fusion.4
  66.8 1.2 convolution_reduce_fusion.4
  68.7 1.2 convolution_reduce_fusion.4
  70.6 1.2 convolution_reduce_fusion.4
  72.5 1.2 convolution_reduce_fusion.4
  74.4 1.2 convolution_reduce_fusion.4
  76.4 1.3 collective-permute-start.1
  77.7 3.8 %collective-permute-done.1 = f32[16,1024]{1,0:T(8,128)S(1)} collective-permute-done((f32[16,1024]{1,0:T(8,128)S(1)}, f32[16,1024]{1,0:T(8,128)S(1)}, u32[]{:S(2)}, u32[]{:S(2)}) %collective-permute-start.1) | collective-permute-done | bytes 65568 | tf_op jit(solution)/shard_map/ppermute | solution.py:101
  82.1 2.3 collective-permute-done.2
  85.0 2.3 collective-permute-done.3
  87.3 1.4 collective-permute-start.4
  88.7 3.2 %collective-permute-done.4 = f32[16,1024]{1,0:T(8,128)S(1)} collective-permute-done((f32[16,1024]{1,0:T(8,128)S(1)}, f32[16,1024]{1,0:T(8,128)S(1)}, u32[]{:S(2)}, u32[]{:S(2)}) %collective-permute-start.4) | collective-permute-done | bytes 65568 | tf_op jit(solution)/shard_map/ppermute | solution.py:101
  92.7 4.9 %bitcast_bitcast_fusion = bf16[8,2048,128]{2,1,0:T(8,128)(2,1)} fusion(bf16[2048,1024]{1,0:T(8,128)(2,1)} %all-gather.5.cloned.1.call-done), kind=kLoop, calls=%fused_computation.19 | loop fusion | bytes 8388608 | tf_op jit(solution)/shard_map/transpose | solution.py:153
  97.6 27.0 %while.21 = (s32[]{:T(128)}, bf16[8,128,2048]{2,1,0:T(8,128)(2,1)}, bf16[8,128,8,128]{3,1,2,0:T(8,128)(2,1)}, bf16[8,2048,128]{2,1,0:T(8,128)(2,1)}, s32[]{:T(128)}) while((s32[]{:T(128)}, bf16[8,128,2048]{2,1,0:T(8,128)(2,1)}, bf16[8,128,8,128]{3,1,2,0:T(8,128)(2,1)}, bf16[8,2048,128]{2,1,0:T(8,128)(2,1)}, s32[]{:T(128)}) %tuple.55), condition=%wide.region_6.7_spmd, body=%wide.region_4.6_spmd.sunk | while | flops 539230208 | bytes 3409469 | solution.py:162
  97.6 2.5 convolution_reduce_fusion.5
  100.1 0.9 fusion.50
  101.0 2.5 convolution_reduce_fusion.5
  103.4 0.9 fusion.50
  104.3 2.5 convolution_reduce_fusion.5
  106.8 0.9 fusion.50
  107.7 2.5 convolution_reduce_fusion.5
  110.2 0.9 fusion.50
  111.1 2.5 convolution_reduce_fusion.5
  113.6 0.9 fusion.50
  114.4 2.5 convolution_reduce_fusion.5
  116.9 0.9 fusion.50
  117.8 2.5 convolution_reduce_fusion.5
  121.2 2.5 convolution_reduce_fusion.5
  123.7 0.9 fusion.50
  124.6 16.5 %all-gather.3.cloned.1.call-done = f32[512,1024]{1,0:T(8,128)} async-done(((f32[32,1024]{1,0:T(8,128)}), f32[512,1024]{1,0:T(8,128)}) %all-gather.3.cloned.1.call-update) | async-done | bytes 2097168 | tf_op jit(solution)/shard_map/all_gather | solution.py:130
  141.0 1.5 collective-permute-start.5
  142.5 2.5 broadcast_in_dim.43
  145.0 1.4 constant_dynamic-update-slice_fusion.1
  146.5 1.5 constant_dynamic-update-slice_fusion.g_ref
  148.0 146.3 %shard_map.75 = (f32[160,1024]{1,0:T(8,128)}, bf16[160,2048]{1,0:T(8,128)(2,1)}) custom-call(f32[1024,1024]{1,0:T(8,128)} %constant_dynamic-update-slice_fusion.g_ref, f32[160,1024]{1,0:T(8,128)} %s_ref.1, bf16[2048,1024]{1,0:T(8,128)(2,1)} %k_ref.1), custom_call_target="tpu_custom_call" | custom-call | tf_op jit(solution)/shard_map/pallas_call | solution.py:81
  (45 shorter events, 8.8 us)
Async XLA Ops:
  7.2 85.5 %all-gather.5.cloned.1.call-start = ((), (), s32[]{:S(2)}) async-start(), calls=%async_computation.2 | async-start | bytes 4718592 | tf_op jit(solution)/shard_map/all_gather | solution.py:164
  11.5 7.9 %copy-start.2 = (s32[4]{0:T(128)S(1)}, s32[4]{0:T(128)}, u32[]{:S(2)}) copy-start(s32[4]{0:T(128)} %param.10) | copy-start | bytes 52
  18.1 5.4 %collective-permute-start = (f32[512,1024]{1,0:T(8,128)}, f32[512,1024]{1,0:T(8,128)S(1)}, u32[]{:S(2)}, u32[]{:S(2)}) collective-permute-start(f32[512,1024]{1,0:T(8,128)} %fusion.18), channel_id=1, source_target_pairs={{0,1},{1,0},{2,3},{3,2},{4,5},{5,4},{6,7},{7,6},{8,9},{9,8},{10,11... | collective-permute-start | bytes 6291464 | tf_op jit(solution)/shard_map/ppermute | solution.py:101
  30.5 45.8 %all-to-all-start = ((f32[16,32,1024]{2,1,0:T(8,128)}), f32[16,32,1024]{2,1,0:T(8,128)S(1)}, u32[]{:S(2)}, u32[]{:S(2)}) async-start(f32[16,32,1024]{2,1,0:T(8,128)} %bitcast.57), calls=%async_computation | async-start | bytes 4194304 | tf_op jit(solution)/shard_map/all_to_all | solution.py:125
  37.3 103.7 %all-gather.3.cloned.1.call-start = ((), (), s32[]{:S(2)}) async-start(), calls=%async_computation.1 | async-start | bytes 2228224 | tf_op jit(solution)/shard_map/all_gather | solution.py:130
  76.4 5.1 %collective-permute-start.1 = (f32[16,1024]{1,0:T(8,128)S(1)}, f32[16,1024]{1,0:T(8,128)S(1)}, u32[]{:S(2)}, u32[]{:S(2)}) collective-permute-start(f32[16,1024]{1,0:T(8,128)S(1)} %constant_dynamic-slice_fusion.1), channel_id=1, source_target_pairs={{0,4},{1,5},{2,6},{3,7},{4,0},{5,1},{6,2},{7,3},{8,12},{9,13},{10,... | collective-permute-start | bytes 196616 | tf_op jit(solution)/shard_map/ppermute | solution.py:101
  81.6 2.8 collective-permute-start.2
  84.4 2.8 collective-permute-start.3
  87.3 4.7 %collective-permute-start.4 = (f32[16,1024]{1,0:T(8,128)S(1)}, f32[16,1024]{1,0:T(8,128)S(1)}, u32[]{:S(2)}, u32[]{:S(2)}) collective-permute-start(f32[16,1024]{1,0:T(8,128)S(1)} %constant_dynamic-update-slice_fusion.4), channel_id=1, source_target_pairs={{0,4},{1,5},{2,6},{3,7},{4,0},{5,1},{6,2},{7,3},{8,12},{9,13},{10,... | collective-permute-start | bytes 196616 | tf_op jit(solution)/shard_map/ppermute | solution.py:101
  92.0 0.7 copy-start.1
  141.0 4.0 %copy-start = (f32[512,1024]{1,0:T(8,128)S(1)}, f32[512,1024]{1,0:T(8,128)}, u32[]{:S(2)}) copy-start(f32[512,1024]{1,0:T(8,128)} %all-gather.3.cloned.1.call-done) | copy-start | bytes 6291460
  141.0 5.5 %collective-permute-start.5 = (f32[512,1024]{1,0:T(8,128)}, f32[512,1024]{1,0:T(8,128)S(1)}, u32[]{:S(2)}, u32[]{:S(2)}) collective-permute-start(f32[512,1024]{1,0:T(8,128)} %all-gather.3.cloned.1.call-done), channel_id=1, source_target_pairs={{0,1},{1,0},{2,3},{3,2},{4,5},{5,4},{6,7},{7,6},{8,9},{9,8},{10,11... | collective-permute-start | bytes 6291464 | tf_op jit(solution)/shard_map/ppermute | solution.py:101
Sparse Core Ops, SparseCore 0:
  11.6 36.6 all-gather.4
  92.8 48.1 all-gather.2

commit v14 on v13

--- a/solution.py
+++ b/solution.py
@@ -144,7 +144,13 @@
     landmarks = jnp.dot(averaging, prefill_keys, preferred_element_type=jnp.float32).astype(
         jnp.bfloat16
     )
-    picked = jnp.take(spanned, outlier_spans, axis=0).reshape(-1, width)
+    picked = jnp.concatenate(
+        [
+            lax.dynamic_slice_in_dim(prefill_keys, outlier_spans[entry] * SPAN, SPAN)
+            for entry in range(outlier_spans.shape[0])
+        ],
+        axis=0,
+    )
     query_count = queries.shape[0]
     query_heads = jnp.transpose(queries.reshape(query_count, KVH, GROUP, HEAD), (1, 0, 2, 3))
 

time: 302 us -> 302 us (level)
  no operation moved by 1% of the time
where the time goes in v14:
time: 302 us; the launch traced here: 301 us
  Pallas kernels  146 us (48%)
  matrix products  47.6 us (16%)
  waiting for transfers between devices  28.3 us (9%)
  local copies, waits for them, and re-layouts  20.6 us (7%)
  between operations  16.7 us (6%)
  blocking collectives  15.5 us (5%)
  starting transfers between devices  13.6 us (5%)
  other arithmetic  12.5 us (4%)
    pallas_call x1, Pallas kernels, iterate(): pl.pallas_call(_iterate_kernel, out_shape=(jax.ShapeDtypeStruct(start.sha...  146 us
    dot_general x16, matrix products, one_head(): jnp.einsum('qgd,cd->qgc', query_group, key_group, preferred_element_type=...  29.7 us
    all_gather x1, waiting for transfers between devices, sum_gram(): s = lax.all_gather(s, 'kv', axis=0, tiled=True)  16.4 us
    all_gather x1, blocking collectives, local(): lax.all_gather(picked, 'seq', axis=0, tiled=True)  15.5 us
    dot_general x2, matrix products, gram_rows(): lax.dot_general(cols, prefill_keys, (((0,), (0,)), ((), ())), preferred_e...  13.6 us
    dynamic_update_slice x16, other arithmetic, score_rows(): return lax.map(one_head, (query_heads, key_heads))  12.3 us
    ppermute x6, waiting for transfers between devices, _swap(): lax.ppermute(x, axis, [(i, i ^ flip) for i in range(lax.axis_size(axis))])  11.8 us
    all_to_all x1, starting transfers between devices, sum_gram(): lax.all_to_all(s.reshape((kv_size, -1) + s.shape[1:]), 'kv', 0, 0, tiled=...  6.83 us
  transfers between devices with their start and end apart: 9, of which 7 were waited for; matrix products, arithmetic and copies ran while one was open for 25% of the time, Pallas kernels for 0%

profile of v14, /device:TPU:1, one launch (start us, length us, event | category | flops | bytes accessed | tf_op | source)
XLA Modules:
  0.0 301.1 jit_solution(1673426055245544262)
XLA Ops:
  7.2 4.2 %convolution_convert_fusion = bf16[256,1024]{1,0:T(8,128)(2,1)} fusion(bf16[2048,1024]{1,0:T(8,128)(2,1)} %k_ref.1, s32[2048]{0:T(1024)S(1)} %get-tuple-element.104, s32[2048]{0:T(1024)S(1)} %get-tuple-element.105, pred[2048]{0:T(1024)(128)(4,1)S(1)} %fusion.30), kind=kOutput, calls=%fused_computation.27 | convolution fusion | flops 1076101120 | bytes 4737024 | tf_op jit(solution)/shard_map/dot_general | solution.py:144
  11.5 6.5 %fusion.18 = f32[512,1024]{1,0:T(8,128)} fusion(bf16[2048,1024]{1,0:T(8,128)(2,1)} %k_ref.1, s32[]{:T(128)S(6)} %select_n.71), kind=kOutput, calls=%fused_computation.26 | convolution fusion | flops 2148007936 | bytes 8388612 | tf_op jit(solution)/shard_map/dot_general | solution.py:177
  18.1 1.4 collective-permute-start
  22.6 0.8 constant_dynamic-slice_fusion.5
  23.4 7.1 %multiply_add_fusion = f32[512,1024]{1,0:T(8,128)} fusion(f32[512,1024]{1,0:T(8,128)S(1)} %collective-permute-done, bf16[2048,1024]{1,0:T(8,128)(2,1)} %k_ref.1, s32[]{:T(128)S(6)} %select_n.70), kind=kOutput, calls=%fused_computation.23 | convolution fusion | flops 2148532224 | bytes 10485764 | tf_op jit(solution)/shard_map/dot_general | solution.py:177
  30.5 6.8 %all-to-all-start = ((f32[16,32,1024]{2,1,0:T(8,128)}), f32[16,32,1024]{2,1,0:T(8,128)S(1)}, u32[]{:S(2)}, u32[]{:S(2)}) async-start(f32[16,32,1024]{2,1,0:T(8,128)} %bitcast.57), calls=%async_computation | async-start | bytes 4194304 | tf_op jit(solution)/shard_map/all_to_all | solution.py:125
  37.4 15.5 %all_gather.9 = bf16[256,1024]{1,0:T(8,128)(2,1)S(1)} all-gather(bf16[32,1024]{1,0:T(8,128)(2,1)S(1)} %pad_maximum_fusion), channel_id=1, replica_groups=mesh['kv'=16,'seq'=8] {'seq'}, dimensions={0}, use_global_device_ids=true | all-gather | bytes 589824 | tf_op jit(solution)/shard_map/all_gather | solution.py:171
  53.1 4.1 %copy.18 = bf16[128,8192]{0,1:T(8,128)(2,1)} copy(bf16[128,8192]{1,0:T(8,128)(2,1)} %param.9) | data formatting | bytes 4194304 | tf_op args[1]
  57.1 3.9 %copy.20 = bf16[8,128,8,128]{3,1,2,0:T(8,128)(2,1)} copy(bf16[8,128,8,128]{1,3,2,0:T(8,128)(2,1)} %bitcast.56) | data formatting | bytes 4194304 | tf_op jit(solution)/shard_map/while | solution.py:168
  61.1 15.2 %while.20 = (s32[]{:T(128)}, bf16[8,128,256]{2,1,0:T(8,128)(2,1)}, bf16[8,128,8,128]{3,1,2,0:T(8,128)(2,1)}, bf16[8,256,128]{1,2,0:T(8,128)(2,1)S(1)}, s32[]{:T(128)}) while((s32[]{:T(128)}, bf16[8,128,256]{2,1,0:T(8,128)(2,1)}, bf16[8,128,8,128]{3,1,2,0:T(8,128)(2,1)}, bf16[8,256,128]{1,2,0:T(8,128)(2,1)S(1)}, s32[]{:T(128)}) %tuple.62), condition=%wide.region_2.3_spmd, body=%wide.region_0.2_spmd.sunk | while | flops 67403776 | bytes 656957 | solution.py:168
  61.1 1.3 convolution_reduce_fusion.4
  63.0 1.2 convolution_reduce_fusion.4
  64.9 1.2 convolution_reduce_fusion.4
  66.8 1.2 convolution_reduce_fusion.4
  68.7 1.2 convolution_reduce_fusion.4
  70.6 1.2 convolution_reduce_fusion.4
  72.5 1.2 convolution_reduce_fusion.4
  74.4 1.2 convolution_reduce_fusion.4
  76.4 1.3 collective-permute-start.1
  77.7 3.9 %collective-permute-done.1 = f32[16,1024]{1,0:T(8,128)S(1)} collective-permute-done((f32[16,1024]{1,0:T(8,128)S(1)}, f32[16,1024]{1,0:T(8,128)S(1)}, u32[]{:S(2)}, u32[]{:S(2)}) %collective-permute-start.1) | collective-permute-done | bytes 65568 | tf_op jit(solution)/shard_map/ppermute | solution.py:101
  82.1 2.3 collective-permute-done.2
  85.0 2.3 collective-permute-done.3
  87.3 1.4 collective-permute-start.4
  88.7 3.2 %collective-permute-done.4 = f32[16,1024]{1,0:T(8,128)S(1)} collective-permute-done((f32[16,1024]{1,0:T(8,128)S(1)}, f32[16,1024]{1,0:T(8,128)S(1)}, u32[]{:S(2)}, u32[]{:S(2)}) %collective-permute-start.4) | collective-permute-done | bytes 65568 | tf_op jit(solution)/shard_map/ppermute | solution.py:101
  92.7 4.9 %bitcast_bitcast_fusion = bf16[8,2048,128]{2,1,0:T(8,128)(2,1)} fusion(bf16[2048,1024]{1,0:T(8,128)(2,1)} %all-gather.5.cloned.1.call-done), kind=kLoop, calls=%fused_computation.18 | loop fusion | bytes 8388608 | tf_op jit(solution)/shard_map/transpose | solution.py:159
  97.6 27.0 %while.21 = (s32[]{:T(128)}, bf16[8,128,2048]{2,1,0:T(8,128)(2,1)}, bf16[8,128,8,128]{3,1,2,0:T(8,128)(2,1)}, bf16[8,2048,128]{2,1,0:T(8,128)(2,1)}, s32[]{:T(128)}) while((s32[]{:T(128)}, bf16[8,128,2048]{2,1,0:T(8,128)(2,1)}, bf16[8,128,8,128]{3,1,2,0:T(8,128)(2,1)}, bf16[8,2048,128]{2,1,0:T(8,128)(2,1)}, s32[]{:T(128)}) %tuple.61), condition=%wide.region_6.7_spmd, body=%wide.region_4.6_spmd.sunk | while | flops 539230208 | bytes 3409469 | solution.py:168
  97.6 2.5 convolution_reduce_fusion.5
  100.1 0.9 fusion.51
  101.0 2.5 convolution_reduce_fusion.5
  103.4 0.9 fusion.51
  104.3 2.5 convolution_reduce_fusion.5
  106.8 0.9 fusion.51
  107.7 2.5 convolution_reduce_fusion.5
  110.2 0.9 fusion.51
  111.1 2.5 convolution_reduce_fusion.5
  113.6 0.9 fusion.51
  114.5 2.5 convolution_reduce_fusion.5
  116.9 0.9 fusion.51
  117.8 2.5 convolution_reduce_fusion.5
  120.3 0.9 fusion.51
  121.2 2.5 convolution_reduce_fusion.5
  123.7 0.9 fusion.51
  124.6 16.4 %all-gather.3.cloned.1.call-done = f32[512,1024]{1,0:T(8,128)} async-done(((f32[32,1024]{1,0:T(8,128)}), f32[512,1024]{1,0:T(8,128)}) %all-gather.3.cloned.1.call-update) | async-done | bytes 2097168 | tf_op jit(solution)/shard_map/all_gather | solution.py:130
  141.0 1.5 collective-permute-start.5
  142.5 2.5 broadcast_in_dim.27
  145.0 1.5 constant_dynamic-update-slice_fusion.1
  146.5 1.5 constant_dynamic-update-slice_fusion.g_ref
  148.0 146.3 %shard_map.75 = (f32[160,1024]{1,0:T(8,128)}, bf16[160,2048]{1,0:T(8,128)(2,1)}) custom-call(f32[1024,1024]{1,0:T(8,128)} %constant_dynamic-update-slice_fusion.g_ref, f32[160,1024]{1,0:T(8,128)} %s_ref.1, bf16[2048,1024]{1,0:T(8,128)(2,1)} %k_ref.1), custom_call_target="tpu_custom_call" | custom-call | tf_op jit(solution)/shard_map/pallas_call | solution.py:81
  (41 shorter events, 8.2 us)
Async XLA Ops:
  7.2 85.5 %all-gather.5.cloned.1.call-start = ((), (), s32[]{:S(2)}) async-start(), calls=%async_computation.2 | async-start | bytes 4718592 | tf_op jit(solution)/shard_map/all_gather | solution.py:170
  11.5 7.9 %copy-start.2 = (s32[4]{0:T(128)S(1)}, s32[4]{0:T(128)}, u32[]{:S(2)}) copy-start(s32[4]{0:T(128)} %param.10) | copy-start | bytes 52
  18.1 5.4 %collective-permute-start = (f32[512,1024]{1,0:T(8,128)}, f32[512,1024]{1,0:T(8,128)S(1)}, u32[]{:S(2)}, u32[]{:S(2)}) collective-permute-start(f32[512,1024]{1,0:T(8,128)} %fusion.18), channel_id=1, source_target_pairs={{0,1},{1,0},{2,3},{3,2},{4,5},{5,4},{6,7},{7,6},{8,9},{9,8},{10,11... | collective-permute-start | bytes 6291464 | tf_op jit(solution)/shard_map/ppermute | solution.py:101
  30.5 45.7 %all-to-all-start = ((f32[16,32,1024]{2,1,0:T(8,128)}), f32[16,32,1024]{2,1,0:T(8,128)S(1)}, u32[]{:S(2)}, u32[]{:S(2)}) async-start(f32[16,32,1024]{2,1,0:T(8,128)} %bitcast.57), calls=%async_computation | async-start | bytes 4194304 | tf_op jit(solution)/shard_map/all_to_all | solution.py:125
  37.3 103.6 %all-gather.3.cloned.1.call-start = ((), (), s32[]{:S(2)}) async-start(), calls=%async_computation.1 | async-start | bytes 2228224 | tf_op jit(solution)/shard_map/all_gather | solution.py:130
  76.4 5.1 %collective-permute-start.1 = (f32[16,1024]{1,0:T(8,128)S(1)}, f32[16,1024]{1,0:T(8,128)S(1)}, u32[]{:S(2)}, u32[]{:S(2)}) collective-permute-start(f32[16,1024]{1,0:T(8,128)S(1)} %constant_dynamic-slice_fusion.1), channel_id=1, source_target_pairs={{0,4},{1,5},{2,6},{3,7},{4,0},{5,1},{6,2},{7,3},{8,12},{9,13},{10,... | collective-permute-start | bytes 196616 | tf_op jit(solution)/shard_map/ppermute | solution.py:101
  81.6 2.8 collective-permute-start.2
  84.4 2.8 collective-permute-start.3
  87.3 4.7 %collective-permute-start.4 = (f32[16,1024]{1,0:T(8,128)S(1)}, f32[16,1024]{1,0:T(8,128)S(1)}, u32[]{:S(2)}, u32[]{:S(2)}) collective-permute-start(f32[16,1024]{1,0:T(8,128)S(1)} %constant_dynamic-update-slice_fusion.4), channel_id=1, source_target_pairs={{0,4},{1,5},{2,6},{3,7},{4,0},{5,1},{6,2},{7,3},{8,12},{9,13},{10,... | collective-permute-start | bytes 196616 | tf_op jit(solution)/shard_map/ppermute | solution.py:101
  92.0 0.7 copy-start.1
  141.0 4.0 %copy-start = (f32[512,1024]{1,0:T(8,128)S(1)}, f32[512,1024]{1,0:T(8,128)}, u32[]{:S(2)}) copy-start(f32[512,1024]{1,0:T(8,128)} %all-gather.3.cloned.1.call-done) | copy-start | bytes 6291460
  141.0 5.5 %collective-permute-start.5 = (f32[512,1024]{1,0:T(8,128)}, f32[512,1024]{1,0:T(8,128)S(1)}, u32[]{:S(2)}, u32[]{:S(2)}) collective-permute-start(f32[512,1024]{1,0:T(8,128)} %all-gather.3.cloned.1.call-done), channel_id=1, source_target_pairs={{0,1},{1,0},{2,3},{3,2},{4,5},{5,4},{6,7},{7,6},{8,9},{9,8},{10,11... | collective-permute-start | bytes 6291464 | tf_op jit(solution)/shard_map/ppermute | solution.py:101
Sparse Core Ops, SparseCore 0:
  11.6 36.6 all-gather.4
  92.8 48.1 all-gather.2
